TPU v7x, 768 devices: a whole 4x8x12 slice. The times are simulated.
768 devices in a mesh: seq: 96 (over z, y), head: 8 (over x, core).
Axes of the slice: x: 4, y: 8, z: 12, core: 2. Of those that a mesh axis runs over, the one named last changes fastest.
Arguments:
- query_vectors: bfloat16 [46080, 6144], P('seq', 'head'), may hold values from -250 to 250
- key_vectors: bfloat16 [46080, 6144], P('seq', 'head'), may hold values from -6 to 6
- value_vectors: bfloat16 [46080, 6144], P('seq', 'head'), may hold values from -2.5 to 2.5
- doc_ids: int32 [46080], P('seq'), may hold values from 0 to 191, never falling along the last dimension, each value on 1 to 960 neighbouring positions
- gradients: bfloat16 [192, 128, 7168], P('seq', 'head'), may hold values from -600 to 600
- weights: bfloat16 [192, 128, 7168], P('seq', None, 'head'), may hold values from -2.5 to 2.5
Outputs:
- attention_out: bfloat16 [46080, 6144], P('seq', 'head')
- update: bfloat16 [192, 128, 7168], P('seq', None, 'head')
- new_weights: bfloat16 [192, 128, 7168], P('seq', None, 'head')
Inputs may be any that keep to these rules, and one draw needn't show every extreme that they name: `doc_ids`: document ids never fall along the sequence; every document has 1 to 960 tokens and one has exactly 960.
All inputs are finite; a program needn't handle non-finite values.
Results may differ from a plain program's by a relative error of at most 0.0034.
Values may be sent and summed in bfloat16 or wider, within the bound.
No kernel may reach another device: no remote copies, remote signals or barrier semaphores. Data moves between devices by JAX's collectives and lax.ppermute only.
A program may use at most 32 MiB of HBM per device.

v0:
```python
import math

import jax
import jax.numpy as jnp
from jax import lax
from jax.sharding import PartitionSpec as P

D = 7168
HD = 128
REACH = 2
NS_ITERS = 5


first_coef = 3.4445
second_coef = -4.775
third_coef = 2.0315
clip_tau = 100.0
learn_rate = 0.1
decay_rate = 0.1
norm_eps = 1e-07
update_gain = 0.2
masked_fill = -1e30


def shifted(shard, axis, by):
    size = lax.axis_size(axis)
    pairs = [(i, i + by) for i in range(size) if 0 <= i + by < size]
    return lax.ppermute(shard, axis, pairs)


def polynomial_of(square, identity):
    highest = lax.Precision.HIGHEST
    return (
        first_coef * identity
        + second_coef * square
        + third_coef * jnp.matmul(square, square, precision=highest)
    )


def shards(query_vectors, key_vectors, value_vectors, doc_ids, gradients, weights):
    highest = lax.Precision.HIGHEST
    tokens_here = query_vectors.shape[0]
    heads_here = query_vectors.shape[1] // HD
    seq_index = lax.axis_index("seq")
    head_count = lax.axis_size("head")
    local_block = (key_vectors, value_vectors, doc_ids)
    earlier = []
    passed = local_block
    for distance in range(REACH):
        passed = shifted((passed[0], passed[1], passed[2]), "seq", 1)
        earlier.append(passed)
    ordered = [earlier[REACH - 1 - position] for position in range(REACH)] + [local_block]
    keys_all = jnp.concatenate([member[0] for member in ordered], axis=0)
    values_all = jnp.concatenate([member[1] for member in ordered], axis=0)
    docs_all = jnp.concatenate([member[2] for member in ordered], axis=0)
    key_place = (seq_index - REACH) * tokens_here + jnp.arange(
        (REACH + 1) * tokens_here, dtype=jnp.int32
    )
    query_place = seq_index * tokens_here + jnp.arange(tokens_here, dtype=jnp.int32)
    same_doc = (
        (doc_ids[:, None] == docs_all[None, :])
        & (key_place[None, :] <= query_place[:, None])
        & (key_place[None, :] >= 0)
    )

    def one_head(head_index):
        col_start = head_index * HD
        query_cols = lax.dynamic_slice_in_dim(query_vectors, col_start, HD, 1)
        key_cols = lax.dynamic_slice_in_dim(keys_all, col_start, HD, 1)
        value_cols = lax.dynamic_slice_in_dim(values_all, col_start, HD, 1)
        scores = jnp.einsum(
            "qd,kd->qk", query_cols, key_cols, preferred_element_type=jnp.float32
        ) / math.sqrt(HD)
        masked = jnp.where(same_doc, scores, masked_fill)
        row_max = jnp.max(masked, axis=1)
        exp_scores = jnp.exp(masked - row_max[:, None])
        row_total = jnp.sum(exp_scores, axis=1)
        mixed_rows = (
            jnp.dot(exp_scores.astype(jnp.bfloat16), value_cols, preferred_element_type=jnp.float32)
            / row_total[:, None]
        )
        return (mixed_rows.astype(jnp.bfloat16), jnp.max(row_max))

    mixed_heads, head_max = lax.map(one_head, jnp.arange(heads_here, dtype=jnp.int32))
    attention_out = jnp.transpose(mixed_heads, (1, 0, 2)).reshape(tokens_here, heads_here * HD)
    heads_all = heads_here * head_count
    head_slots = jnp.arange(heads_all, dtype=jnp.int32)
    spread_max = jnp.where(
        head_slots // heads_here == lax.axis_index("head"),
        jnp.tile(head_max, head_count),
        masked_fill,
    )
    max_logit = lax.pmax(spread_max, ("seq", "head"))
    root_gamma = jnp.sqrt(clip_tau / jnp.maximum(max_logit, clip_tau))
    owned = lax.all_to_all(gradients, "head", split_axis=2, concat_axis=1, tiled=True)
    identity = jnp.eye(HD, dtype=jnp.float32)
    gram_local = jnp.einsum("mid,mjd->mij", owned, owned, preferred_element_type=jnp.float32)
    gram_whole = lax.psum(gram_local, "head")
    norm_value = jnp.sqrt(jnp.trace(gram_whole, axis1=1, axis2=2)) + norm_eps
    square = gram_whole / (norm_value * norm_value)[:, None, None]
    current = owned.astype(jnp.float32) / norm_value[:, None, None]
    for iteration in range(NS_ITERS):
        if iteration > 0:
            square = lax.psum(
                jnp.einsum("mid,mjd->mij", current, current, precision=highest), "head"
            )
        current = jnp.matmul(polynomial_of(square, identity), current, precision=highest)
    update = (current * (update_gain * math.sqrt(D))).astype(jnp.bfloat16)
    mats_here = owned.shape[0]
    matrix_index = seq_index * mats_here + jnp.arange(mats_here, dtype=jnp.int32)
    one_hot = (matrix_index[:, None] % heads_all == head_slots[None, :]).astype(jnp.float32)
    picked = jnp.sum(one_hot * root_gamma[None, :], axis=1)
    factor = jnp.where(matrix_index < 2 * heads_all, picked, 1.0)
    kept = (1.0 - learn_rate * decay_rate) * weights.astype(jnp.float32)
    new_weights = (factor[:, None, None] * (kept - learn_rate * update.astype(jnp.float32))).astype(
        jnp.bfloat16
    )
    return (attention_out, update, new_weights)


def solution(mesh):
    return jax.shard_map(
        shards,
        mesh=mesh,
        in_specs=(
            P("seq", "head"),
            P("seq", "head"),
            P("seq", "head"),
            P("seq"),
            P("seq", "head", None),
            P("seq", None, "head"),
        ),
        out_specs=(P("seq", "head"), P("seq", None, "head"), P("seq", None, "head")),
        check_vma=False,
    )
```

profile of v0, /device:TPU:1, one launch (start us, length us, event | category | flops | bytes accessed | tf_op | source)
XLA Modules:
  0.0 625.4 jit_solution(9086265491055637012)
XLA Ops:
  7.2 7.8 %copy.19 = bf16[2,16,7168]{1,0,2:T(2,128)(2,1)} copy(bf16[2,16,7168]{2,1,0:T(8,128)(2,1)} %param.12) | data formatting | bytes 917504 | tf_op args[4]
  15.0 6.1 reshape.69
  21.1 13.9 %all-to-all-start = ((bf16[8,2,14336]{2,1,0:T(2,128)(2,1)}), bf16[8,2,14336]{2,1,0:T(2,128)(2,1)S(1)}, u32[]{:S(2)}, u32[]{:S(2)}) async-start(bf16[8,2,14336]{2,1,0:T(2,128)(2,1)} %reshape.69), calls=%async_computation | async-start | bytes 917504 | tf_op jit(solution)/shard_map/all_to_all | solution.py:95
  35.0 2.2 collective-permute-start
  37.2 2.2 collective-permute-start.4
  40.6 3.1 all-to-all-done
  43.8 3.9 reshape.70
  47.6 7.9 %copy.20 = bf16[2,16,8,896]{3,1,2,0:T(8,128)(2,1)S(1)} copy(bf16[2,16,8,896]{1,0,3,2:T(2,128)(2,1)} %bitcast.47) | data formatting | bytes 917504 | tf_op jit(solution)/shard_map/all_to_all | solution.py:95
  56.6 72.4 %all-reduce.6.cloned.1.call-done = f32[2,128,128]{2,1,0:T(8,128)} async-done(((f32[2,128,128]{2,1,0:T(8,128)}), f32[2,128,128]{2,1,0:T(8,128)}) %all-reduce.6.cloned.1.call-update) | async-done | bytes 131088 | tf_op jit(solution)/shard_map/psum | solution.py:98
  132.4 1.7 fusion.42
  134.2 74.7 %all-reduce.8.cloned.1.call-done = f32[2,128,128]{2,1,0:T(8,128)} async-done(((f32[2,128,128]{2,1,0:T(8,128)}), f32[2,128,128]{2,1,0:T(8,128)}) %all-reduce.8.cloned.1.call-update) | async-done | bytes 131088 | tf_op jit(solution)/shard_map/psum | solution.py:104
  213.0 74.7 %all-reduce.10.cloned.1.call-done = f32[2,128,128]{2,1,0:T(8,128)} async-done(((f32[2,128,128]{2,1,0:T(8,128)}), f32[2,128,128]{2,1,0:T(8,128)}) %all-reduce.10.cloned.1.call-update) | async-done | bytes 131088 | tf_op jit(solution)/shard_map/psum | solution.py:104
  293.3 73.0 %all-reduce.12.cloned.1.call-done = f32[2,128,128]{2,1,0:T(8,128)} async-done(((f32[2,128,128]{2,1,0:T(8,128)}), f32[2,128,128]{2,1,0:T(8,128)}) %all-reduce.12.cloned.1.call-update) | async-done | bytes 131088 | tf_op jit(solution)/shard_map/psum | solution.py:104
  367.7 2.5 collective-permute-start.1
  371.1 3.1 collective-permute-start.5
  376.1 74.5 %all-reduce.14.cloned.1.call-done = f32[2,128,128]{2,1,0:T(8,128)} async-done(((f32[2,128,128]{2,1,0:T(8,128)}), f32[2,128,128]{2,1,0:T(8,128)}) %all-reduce.14.cloned.1.call-update) | async-done | bytes 131088 | tf_op jit(solution)/shard_map/psum | solution.py:104
  453.7 3.1 pad_maximum_fusion.1
  456.8 46.0 %while.13 = (s32[]{:T(128)}, bf16[6,480,128]{2,1,0:T(8,128)(2,1)}, f32[6]{0:T(128)S(1)}, s32[6]{0:T(128)S(1)}, bf16[480,768]{1,0:T(8,128)(2,1)}, /*index=5*/bf16...) while((s32[]{:T(128)}, bf16[6,480,128]{2,1,0:T(8,128)(2,1)}, ...), condition=%wide.region_4.5_spmd.clone, body=%wide.region_0.4_spmd.clone.sunk | while | flops 362310720 | bytes 9310831 | solution.py:84
  458.1 2.0 fusion.83
  461.5 2.2 fusion.85
  465.7 2.0 fusion.83
  469.2 2.2 fusion.85
  473.4 2.0 fusion.83
  476.8 2.2 fusion.85
  481.1 2.0 fusion.83
  484.5 2.2 fusion.85
  488.7 2.0 fusion.83
  492.2 2.2 fusion.85
  496.4 2.0 fusion.83
  499.8 2.2 fusion.85
  505.5 111.2 %pmax.7 = f32[48]{0:T(128)S(1)} all-reduce(f32[48]{0:T(128)S(1)} %compare_select_fusion), channel_id=1, replica_groups=mesh['seq'=96,'head'=8] {'seq','head'}, use_global_device_ids=true, to_apply=%region_11.12 | all-reduce | flops 48 | bytes 384 | tf_op jit(solution)/shard_map/pmax | solution.py:93
  617.0 1.9 multiply_convert_fusion
  (78 shorter events, 41.9 us)
Async XLA Ops:
  15.0 20.0 %copy-start = (bf16[480,768]{1,0:T(8,128)(2,1)S(1)}, bf16[480,768]{1,0:T(8,128)(2,1)}, u32[]{:S(2)}) copy-start(bf16[480,768]{1,0:T(8,128)(2,1)} %param.9) | copy-start | bytes 2211844
  15.0 22.2 %copy-start.1 = (bf16[480,768]{1,0:T(8,128)(2,1)S(1)}, bf16[480,768]{1,0:T(8,128)(2,1)}, u32[]{:S(2)}) copy-start(bf16[480,768]{1,0:T(8,128)(2,1)} %param.10) | copy-start | bytes 2211844
  15.0 24.3 %copy-start.3 = (s32[480]{0:T(512)S(1)}, s32[480]{0:T(512)}, u32[]{:S(2)}) copy-start(s32[480]{0:T(512)} %param.11) | copy-start | bytes 5764
  21.1 22.7 %all-to-all-start = ((bf16[8,2,14336]{2,1,0:T(2,128)(2,1)}), bf16[8,2,14336]{2,1,0:T(2,128)(2,1)S(1)}, u32[]{:S(2)}, u32[]{:S(2)}) async-start(bf16[8,2,14336]{2,1,0:T(2,128)(2,1)} %reshape.69), calls=%async_computation | async-start | bytes 917504 | tf_op jit(solution)/shard_map/all_to_all | solution.py:95
  35.0 94.0 %all-reduce.6.cloned.1.call-start = ((), (), s32[]{:S(2)}) async-start(), calls=%async_computation.1 | async-start | bytes 262144 | tf_op jit(solution)/shard_map/psum | solution.py:98
  35.0 332.7 %collective-permute-start = (bf16[480,768]{1,0:T(8,128)(2,1)S(1)}, bf16[480,768]{1,0:T(8,128)(2,1)}, u32[]{:S(2)}, u32[]{:S(2)}) collective-permute-start(bf16[480,768]{1,0:T(8,128)(2,1)S(1)} %copy-done), channel_id=1, source_target_pairs={{0,8},{8,16},{16,24},{24,32},{32,40},{40,48},{48,56},{56,64},{64,7... | collective-permute-start | bytes 2211848 | tf_op jit(solution)/shard_map/ppermute | solution.py:28
  37.2 333.9 %collective-permute-start.4 = (bf16[480,768]{1,0:T(8,128)(2,1)S(1)}, bf16[480,768]{1,0:T(8,128)(2,1)}, u32[]{:S(2)}, u32[]{:S(2)}) collective-permute-start(bf16[480,768]{1,0:T(8,128)(2,1)S(1)} %copy-done.1), channel_id=1, source_target_pairs={{0,8},{8,16},{16,24},{24,32},{32,40},{40,48},{48,56},{56,64},{64,7... | collective-permute-start | bytes 2211848 | tf_op jit(solution)/shard_map/ppermute | solution.py:28
  39.3 252.3 %collective-permute-start.2 = (s32[480]{0:T(512)S(1)}, s32[480]{0:T(512)S(1)}, u32[]{:S(2)}, u32[]{:S(2)}) collective-permute-start(s32[480]{0:T(512)S(1)} %copy-done.3), channel_id=1, source_target_pairs={{0,8},{8,16},{16,24},{24,32},{32,40},{40,48},{48,56},{56,64},{64,7... | collective-permute-start | bytes 5768 | tf_op jit(solution)/shard_map/ppermute | solution.py:28
  56.5 152.4 %all-reduce.8.cloned.1.call-start = ((), (), s32[]{:S(2)}) async-start(), calls=%async_computation.2 | async-start | bytes 262144 | tf_op jit(solution)/shard_map/psum | solution.py:104
  134.2 153.4 %all-reduce.10.cloned.1.call-start = ((), (), s32[]{:S(2)}) async-start(), calls=%async_computation.3 | async-start | bytes 262144 | tf_op jit(solution)/shard_map/psum | solution.py:104
  212.9 153.4 %all-reduce.12.cloned.1.call-start = ((), (), s32[]{:S(2)}) async-start(), calls=%async_computation.4 | async-start | bytes 262144 | tf_op jit(solution)/shard_map/psum | solution.py:104
  291.6 159.1 %all-reduce.14.cloned.1.call-start = ((), (), s32[]{:S(2)}) async-start(), calls=%async_computation.5 | async-start | bytes 262144 | tf_op jit(solution)/shard_map/psum | solution.py:104
  291.7 84.4 %collective-permute-start.3 = (s32[480]{0:T(512)S(1)}, s32[480]{0:T(512)S(1)}, u32[]{:S(2)}, u32[]{:S(2)}) collective-permute-start(s32[480]{0:T(512)S(1)} %collective-permute-done.2), channel_id=1, source_target_pairs={{0,8},{8,16},{16,24},{24,32},{32,40},{40,48},{48,56},{56,64},{64,7... | collective-permute-start | bytes 5768 | tf_op jit(solution)/shard_map/ppermute | solution.py:28
  367.7 84.4 %collective-permute-start.1 = (bf16[480,768]{1,0:T(8,128)(2,1)}, bf16[480,768]{1,0:T(8,128)(2,1)}, u32[]{:S(2)}, u32[]{:S(2)}) collective-permute-start(bf16[480,768]{1,0:T(8,128)(2,1)} %collective-permute-done), channel_id=1, source_target_pairs={{0,8},{8,16},{16,24},{24,32},{32,40},{40,48},{48,56},{56,64},{64,7... | collective-permute-start | bytes 2211848 | tf_op jit(solution)/shard_map/ppermute | solution.py:28
  371.1 82.6 %collective-permute-start.5 = (bf16[480,768]{1,0:T(8,128)(2,1)}, bf16[480,768]{1,0:T(8,128)(2,1)}, u32[]{:S(2)}, u32[]{:S(2)}) collective-permute-start(bf16[480,768]{1,0:T(8,128)(2,1)} %collective-permute-done.4), channel_id=1, source_target_pairs={{0,8},{8,16},{16,24},{24,32},{32,40},{40,48},{48,56},{56,64},{64,7... | collective-permute-start | bytes 2211848 | tf_op jit(solution)/shard_map/ppermute | solution.py:28
  502.8 114.1 %copy-start.2 = (bf16[2,128,896]{2,1,0:T(8,128)(2,1)S(1)}, bf16[2,128,896]{2,1,0:T(8,128)(2,1)}, u32[]{:S(2)}) copy-start(bf16[2,128,896]{2,1,0:T(8,128)(2,1)} %param.13) | copy-start | bytes 1376260
Sparse Core Ops, SparseCore 0:
  56.6 72.3 all-reduce.5
  134.3 74.5 all-reduce.7
  213.0 74.5 all-reduce.9
  291.7 74.5 all-reduce.11
  376.1 74.4 all-reduce.13
where the time goes:
time: 627 us; the launch traced here: 625 us
  waiting for transfers between devices  372 us (59%)
  blocking collectives  111 us (18%)
  matrix products  45.8 us (7%)
  local copies, waits for them, and re-layouts  36.4 us (6%)
  starting transfers between devices  27 us (4%)
  other arithmetic  14.5 us (2%)
  between operations  14 us (2%)
    psum x4, waiting for transfers between devices, shards(): lax.psum(jnp.einsum('mid,mjd->mij', current, current, precision=highest),...  297 us
    pmax x1, blocking collectives, shards(): max_logit = lax.pmax(spread_max, ('seq', 'head'))  111 us
    psum x1, waiting for transfers between devices, shards(): gram_whole = lax.psum(gram_local, 'head')  72.4 us
    unnamed x12, local copies, waits for them, and re-layouts  18.9 us
    all_to_all x1, starting transfers between devices, shards(): lax.all_to_all(gradients, 'head', split_axis=2, concat_axis=1, tiled=True)  13.9 us
    dot_general x6, matrix products, one_head(): jnp.dot(exp_scores.astype(jnp.bfloat16), value_cols, preferred_element_ty...  13.5 us
    ppermute x6, starting transfers between devices, shifted(): return lax.ppermute(shard, axis, pairs)  12.9 us
  transfers between devices with their start and end apart: 12, of which 6 were waited for; matrix products, arithmetic and copies ran while one was open for 5% of the time, Pallas kernels for 0%

commit v1 on v0

--- a/solution.py
+++ b/solution.py
@@ -37,18 +37,21 @@
     )
 
 
+def gathered(values, axis):
+    size = lax.axis_size(axis)
+    spread = jnp.broadcast_to(values[None], (size,) + values.shape)
+    return lax.all_to_all(spread, axis, 0, 0, tiled=True)
+
+
 def shards(query_vectors, key_vectors, value_vectors, doc_ids, gradients, weights):
     highest = lax.Precision.HIGHEST
     tokens_here = query_vectors.shape[0]
     heads_here = query_vectors.shape[1] // HD
     seq_index = lax.axis_index("seq")
+    head_index = lax.axis_index("head")
     head_count = lax.axis_size("head")
     local_block = (key_vectors, value_vectors, doc_ids)
-    earlier = []
-    passed = local_block
-    for distance in range(REACH):
-        passed = shifted((passed[0], passed[1], passed[2]), "seq", 1)
-        earlier.append(passed)
+    earlier = [shifted(local_block, "seq", distance) for distance in range(1, REACH + 1)]
     ordered = [earlier[REACH - 1 - position] for position in range(REACH)] + [local_block]
     keys_all = jnp.concatenate([member[0] for member in ordered], axis=0)
     values_all = jnp.concatenate([member[1] for member in ordered], axis=0)
@@ -63,8 +66,8 @@
         & (key_place[None, :] >= 0)
     )
 
-    def one_head(head_index):
-        col_start = head_index * HD
+    def one_head(head_slot):
+        col_start = head_slot * HD
         query_cols = lax.dynamic_slice_in_dim(query_vectors, col_start, HD, 1)
         key_cols = lax.dynamic_slice_in_dim(keys_all, col_start, HD, 1)
         value_cols = lax.dynamic_slice_in_dim(values_all, col_start, HD, 1)
@@ -85,28 +88,36 @@
     attention_out = jnp.transpose(mixed_heads, (1, 0, 2)).reshape(tokens_here, heads_here * HD)
     heads_all = heads_here * head_count
     head_slots = jnp.arange(heads_all, dtype=jnp.int32)
-    spread_max = jnp.where(
-        head_slots // heads_here == lax.axis_index("head"),
-        jnp.tile(head_max, head_count),
-        masked_fill,
+    seq_max = jnp.max(gathered(head_max, "seq"), axis=0)
+    max_logit = gathered(seq_max, "head").reshape(heads_all)
+    root_gamma = jnp.sqrt(clip_tau / jnp.maximum(max_logit, clip_tau))
+
+    pieces = gathered(gradients, "head")
+    mats_here, rows_here = gradients.shape[0], gradients.shape[1]
+    cols_here = weights.shape[2]
+    gram = jnp.einsum(
+        "jmrd,kmsd->mjrks", pieces, pieces, preferred_element_type=jnp.float32
+    ).reshape(mats_here, HD, HD)
+    norm_value = jnp.sqrt(jnp.trace(gram, axis1=1, axis2=2)) + norm_eps
+    square = gram / (norm_value * norm_value)[:, None, None]
+    identity = jnp.eye(HD, dtype=jnp.float32)
+    total = None
+    for iteration in range(NS_ITERS):
+        poly = polynomial_of(square, identity)
+        total = poly if total is None else jnp.matmul(poly, total, precision=highest)
+        if iteration + 1 < NS_ITERS:
+            square = jnp.matmul(
+                poly, jnp.matmul(square, poly, precision=highest), precision=highest
+            )
+    own_cols = lax.dynamic_slice_in_dim(pieces, head_index * cols_here, cols_here, 3)
+    start = own_cols.astype(jnp.float32) / norm_value[None, :, None, None]
+    current = jnp.einsum(
+        "mijr,jmrd->mid",
+        total.reshape(mats_here, HD, head_count, rows_here),
+        start,
+        precision=highest,
     )
-    max_logit = lax.pmax(spread_max, ("seq", "head"))
-    root_gamma = jnp.sqrt(clip_tau / jnp.maximum(max_logit, clip_tau))
-    owned = lax.all_to_all(gradients, "head", split_axis=2, concat_axis=1, tiled=True)
-    identity = jnp.eye(HD, dtype=jnp.float32)
-    gram_local = jnp.einsum("mid,mjd->mij", owned, owned, preferred_element_type=jnp.float32)
-    gram_whole = lax.psum(gram_local, "head")
-    norm_value = jnp.sqrt(jnp.trace(gram_whole, axis1=1, axis2=2)) + norm_eps
-    square = gram_whole / (norm_value * norm_value)[:, None, None]
-    current = owned.astype(jnp.float32) / norm_value[:, None, None]
-    for iteration in range(NS_ITERS):
-        if iteration > 0:
-            square = lax.psum(
-                jnp.einsum("mid,mjd->mij", current, current, precision=highest), "head"
-            )
-        current = jnp.matmul(polynomial_of(square, identity), current, precision=highest)
     update = (current * (update_gain * math.sqrt(D))).astype(jnp.bfloat16)
-    mats_here = owned.shape[0]
     matrix_index = seq_index * mats_here + jnp.arange(mats_here, dtype=jnp.int32)
     one_hot = (matrix_index[:, None] % heads_all == head_slots[None, :]).astype(jnp.float32)
     picked = jnp.sum(one_hot * root_gamma[None, :], axis=1)

time: 627 us -> 282 us (0.45)
  waiting for transfers between devices: 372 us -> 83.8 us
  blocking collectives: 111 us -> 58.8 us
  starting transfers between devices: 27 us -> 65.5 us
  local copies, waits for them, and re-layouts: 36.4 us -> 14.1 us
  between operations: 14 us -> 0.98 us
    psum x5 -> x0, waiting for transfers between devices: 369 us -> none  [the longest x4 297 us: shards(): lax.psum(jnp.einsum('mid,mjd->mij', current, current, precision=highest),...]
    pmax x1 -> x0, blocking collectives: 111 us -> none  [shards(): max_logit = lax.pmax(spread_max, ('seq', 'head'))]
    all_to_all x0 -> x2, blocking collectives: none -> 58.8 us  [gathered(): return lax.all_to_all(spread, axis, 0, 0, tiled=True)]
    ppermute x6, starting transfers between devices: 12.9 us -> 60.3 us  [shifted(): return lax.ppermute(shard, axis, pairs)]
    ppermute x6, waiting for transfers between devices: 0.02 us -> 42.4 us  [shifted(): return lax.ppermute(shard, axis, pairs)]
    all_to_all x1, waiting for transfers between devices: 3.14 us -> 41.4 us  [gathered(): return lax.all_to_all(spread, axis, 0, 0, tiled=True)]
    unnamed x12 -> x13, local copies, waits for them, and re-layouts: 18.9 us -> 2.03 us
    all_to_all x1, starting transfers between devices: 13.9 us -> 5.2 us  [gathered(): return lax.all_to_all(spread, axis, 0, 0, tiled=True)]
  transfers between devices with their start and end apart: 12 -> 7, of which waited for: 6 -> 3; matrix products, arithmetic and copies ran while one was open for 5% -> 2% of each run, Pallas kernels for 0% -> 0%
where the time goes in v1:
time: 282 us; the launch traced here: 281 us
  waiting for transfers between devices  83.8 us (30%)
  starting transfers between devices  65.5 us (23%)
  blocking collectives  58.8 us (21%)
  matrix products  40.6 us (14%)
  local copies, waits for them, and re-layouts  14.1 us (5%)
  other arithmetic  13.5 us (5%)
  loops' own time  3.96 us (1%)
    ppermute x6, starting transfers between devices, shifted(): return lax.ppermute(shard, axis, pairs)  60.3 us
    all_to_all x2, blocking collectives, gathered(): return lax.all_to_all(spread, axis, 0, 0, tiled=True)  58.8 us
    ppermute x6, waiting for transfers between devices, shifted(): return lax.ppermute(shard, axis, pairs)  42.4 us
    all_to_all x1, waiting for transfers between devices, gathered(): return lax.all_to_all(spread, axis, 0, 0, tiled=True)  41.4 us
    dot_general x6, matrix products, one_head(): jnp.dot(exp_scores.astype(jnp.bfloat16), value_cols, preferred_element_ty...  13.5 us
    dot_general x6, matrix products, one_head(): jnp.einsum('qd,kd->qk', query_cols, key_cols, preferred_element_type=jnp....  12.2 us
    reduce_max x6, other arithmetic, one_head(): return (mixed_rows.astype(jnp.bfloat16), jnp.max(row_max))  8.4 us
    dot_general x1, matrix products, shards(): jnp.einsum('jmrd,kmsd->mjrks', pieces, pieces, preferred_element_type=jnp...  6.89 us
  transfers between devices with their start and end apart: 7, of which 3 were waited for; matrix products, arithmetic and copies ran while one was open for 2% of the time, Pallas kernels for 0%

profile of v1, /device:TPU:1, one launch (start us, length us, event | category | flops | bytes accessed | tf_op | source)
XLA Modules:
  0.0 281.2 jit_solution(1808738556791895505)
XLA Ops:
  0.6 4.2 %collective-permute-start.1 = (bf16[480,768]{1,0:T(8,128)(2,1)}, bf16[480,768]{1,0:T(8,128)(2,1)S(1)}, u32[]{:S(2)}, u32[]{:S(2)}) collective-permute-start(bf16[480,768]{1,0:T(8,128)(2,1)} %param.9), channel_id=1, source_target_pairs={{0,8},{8,16},{16,24},{24,32},{32,40},{40,48},{48,56},{56,64},{64,7... | collective-permute-start | bytes 2211848 | tf_op jit(solution)/shard_map/ppermute | solution.py:28
  4.9 5.1 %collective-permute-start = (bf16[480,768]{1,0:T(8,128)(2,1)}, bf16[480,768]{1,0:T(8,128)(2,1)}, u32[]{:S(2)}, u32[]{:S(2)}) collective-permute-start(bf16[480,768]{1,0:T(8,128)(2,1)} %param.9), channel_id=1, source_target_pairs={{0,16},{8,24},{16,32},{24,40},{32,48},{40,56},{48,64},{56,72},{64,... | collective-permute-start | bytes 2211848 | tf_op jit(solution)/shard_map/ppermute | solution.py:28
  9.9 5.3 %collective-permute-start.5 = (bf16[480,768]{1,0:T(8,128)(2,1)}, bf16[480,768]{1,0:T(8,128)(2,1)}, u32[]{:S(2)}, u32[]{:S(2)}) collective-permute-start(bf16[480,768]{1,0:T(8,128)(2,1)} %param.10), channel_id=1, source_target_pairs={{0,8},{8,16},{16,24},{24,32},{32,40},{40,48},{48,56},{56,64},{64,7... | collective-permute-start | bytes 2211848 | tf_op jit(solution)/shard_map/ppermute | solution.py:28
  15.2 2.2 collective-permute-start.4
  17.4 1.9 collective-permute-start.2
  19.3 41.5 %collective-permute-done.2 = s32[480]{0:T(512)S(1)} collective-permute-done((s32[480]{0:T(512)}, s32[480]{0:T(512)S(1)}, u32[]{:S(2)}, u32[]{:S(2)}) %collective-permute-start.2) | collective-permute-done | bytes 1952 | tf_op jit(solution)/shard_map/ppermute | solution.py:28
  60.8 41.8 %collective-permute-start.3 = (s32[480]{0:T(512)}, s32[480]{0:T(512)S(1)}, u32[]{:S(2)}, u32[]{:S(2)}) collective-permute-start(s32[480]{0:T(512)} %param.11), channel_id=1, source_target_pairs={{0,8},{8,16},{16,24},{24,32},{32,40},{40,48},{48,56},{56,64},{64,7... | collective-permute-start | bytes 5768 | tf_op jit(solution)/shard_map/ppermute | solution.py:28
  105.1 1.7 pad_maximum_fusion
  106.9 2.9 %pad_maximum_fusion.1 = bf16[1440,768]{1,0:T(8,128)(2,1)} fusion(bf16[480,768]{1,0:T(8,128)(2,1)S(1)} %copy-done, bf16[480,768]{1,0:T(8,128)(2,1)} %collective-permute-done.5, bf16[480,768]{1,0:T(8,128)(2,1)} %collective-permute-done.4), kind=kLoop, calls=%fused_computation.21 | loop fusion | flops 6635520 | bytes 4423680 | tf_op jit(solution)/shard_map/concatenate | solution.py:57
  109.8 46.0 %while.13 = (s32[]{:T(128)}, bf16[6,480,128]{2,1,0:T(8,128)(2,1)}, f32[6]{0:T(128)S(1)}, s32[6]{0:T(128)S(1)}, bf16[480,768]{1,0:T(8,128)(2,1)}, /*index=5*/bf16...) while((s32[]{:T(128)}, bf16[6,480,128]{2,1,0:T(8,128)(2,1)}, ...), condition=%wide.region_4.5_spmd.clone, body=%wide.region_0.4_spmd.clone.sunk | while | flops 362310720 | bytes 9310831 | solution.py:87
  111.0 2.0 fusion.94
  113.0 1.4 fusion.95
  114.4 2.2 fusion.96
  118.7 2.0 fusion.94
  120.7 1.4 fusion.95
  122.1 2.2 fusion.96
  126.3 2.0 fusion.94
  128.4 1.4 fusion.95
  129.8 2.2 fusion.96
  134.0 2.0 fusion.94
  137.4 2.3 fusion.96
  141.7 2.0 fusion.94
  145.1 2.2 fusion.96
  149.3 2.0 fusion.94
  152.8 2.2 fusion.96
  155.8 46.0 %all_to_all.17 = f32[96,1,6]{2,1,0:T(1,128)S(1)} all-to-all(f32[96,1,6]{2,1,0:T(1,128)S(1)} %broadcast_in_dim.38), channel_id=1, replica_groups=mesh['seq'=96,'head'=8] {'seq'}, dimensions={0} | all-to-all | bytes 4608 | tf_op jit(solution)/shard_map/all_to_all | solution.py:43
  202.0 12.7 %all_to_all.18 = f32[8,1,6]{2,1,0:T(1,128)S(1)} all-to-all(f32[8,1,6]{2,1,0:T(1,128)S(1)} %broadcast_in_dim.39), channel_id=1, replica_groups=mesh['seq'=96,'head'=8] {'head'}, dimensions={0} | all-to-all | bytes 384 | tf_op jit(solution)/shard_map/all_to_all | solution.py:43
  214.7 2.3 broadcast_in_dim.35
  217.0 5.2 %all-to-all-start = ((bf16[8,2,16,7168]{3,2,1,0:T(8,128)(2,1)}), bf16[8,2,16,7168]{3,2,1,0:T(8,128)(2,1)}, u32[]{:S(2)}, u32[]{:S(2)}) async-start(bf16[8,2,16,7168]{3,2,1,0:T(8,128)(2,1)} %broadcast_in_dim.35), calls=%async_computation | async-start | bytes 7340032 | tf_op jit(solution)/shard_map/all_to_all | solution.py:43
  224.1 41.4 %all-to-all-done = bf16[8,2,16,7168]{3,2,1,0:T(8,128)(2,1)} async-done(((bf16[8,2,16,7168]{3,2,1,0:T(8,128)(2,1)}), bf16[8,2,16,7168]{3,2,1,0:T(8,128)(2,1)}, u32[]{:S(2)}, u32[]{:S(2)}) %all-to-all-start) | async-done | bytes 3670048 | tf_op jit(solution)/shard_map/all_to_all | solution.py:43
  265.5 6.9 %select_reduce_fusion = (f32[2]{0:T(128)S(1)}, f32[2,8,16,8,16]{4,2,3,1,0:T(8,128)S(1)}) fusion(pred[8,16,8,16]{3,1,2,0:T(8,128)(4,1)S(1)} %broadcast_compare_fusion, bf16[8,2,16,7168]{3,2,1,0:T(8,128)(2,1)} %all-to-all-done), kind=kOutput, calls=%fused_computation.35 | convolution fusion | flops 469827584 | bytes 3817480 | tf_op jit(solution)/shard_map/jmrd,kmsd->mjrks/dot_general | solution.py:98
  278.1 3.1 %multiply_convert_fusion = (bf16[2,128,896]{2,1,0:T(8,128)(2,1)}, bf16[2,128,896]{2,1,0:T(8,128)(2,1)}) fusion(bf16[2,128,896]{2,1,0:T(8,128)(2,1)S(1)} %copy-done.5, f32[2]{0:T(128)S(1)} %compare_select_fusion.1, f32[2,128,8,16]{1,3,2,0:T(8,128)S(1)} %bitcast.65, f32[2]{0:T(128)S(1)} %get-tuple-element.122, bf16[8,2,16,7168]{3,2,1,0:T(8,128)(2,1)} %all-to-all-done, ...), kind=kOutput, calls=%fused_computation.37 | convolution fusion | flops 354844672 | bytes 1966100 | tf_op jit(solution)/shard_map/mijr,jmrd->mid/dot_general | solution.py:114
  (72 shorter events, 22.4 us)
Async XLA Ops:
  0.6 106.2 %copy-start = (bf16[480,768]{1,0:T(8,128)(2,1)S(1)}, bf16[480,768]{1,0:T(8,128)(2,1)}, u32[]{:S(2)}) copy-start(bf16[480,768]{1,0:T(8,128)(2,1)} %param.10) | copy-start | bytes 2211844
  0.6 103.6 %collective-permute-start.1 = (bf16[480,768]{1,0:T(8,128)(2,1)}, bf16[480,768]{1,0:T(8,128)(2,1)S(1)}, u32[]{:S(2)}, u32[]{:S(2)}) collective-permute-start(bf16[480,768]{1,0:T(8,128)(2,1)} %param.9), channel_id=1, source_target_pairs={{0,8},{8,16},{16,24},{24,32},{32,40},{40,48},{48,56},{56,64},{64,7... | collective-permute-start | bytes 2211848 | tf_op jit(solution)/shard_map/ppermute | solution.py:28
  4.9 100.3 %collective-permute-start = (bf16[480,768]{1,0:T(8,128)(2,1)}, bf16[480,768]{1,0:T(8,128)(2,1)}, u32[]{:S(2)}, u32[]{:S(2)}) collective-permute-start(bf16[480,768]{1,0:T(8,128)(2,1)} %param.9), channel_id=1, source_target_pairs={{0,16},{8,24},{16,32},{24,40},{32,48},{40,56},{48,64},{56,72},{64,... | collective-permute-start | bytes 2211848 | tf_op jit(solution)/shard_map/ppermute | solution.py:28
  9.9 96.9 %collective-permute-start.5 = (bf16[480,768]{1,0:T(8,128)(2,1)}, bf16[480,768]{1,0:T(8,128)(2,1)}, u32[]{:S(2)}, u32[]{:S(2)}) collective-permute-start(bf16[480,768]{1,0:T(8,128)(2,1)} %param.10), channel_id=1, source_target_pairs={{0,8},{8,16},{16,24},{24,32},{32,40},{40,48},{48,56},{56,64},{64,7... | collective-permute-start | bytes 2211848 | tf_op jit(solution)/shard_map/ppermute | solution.py:28
  15.2 91.6 %collective-permute-start.4 = (bf16[480,768]{1,0:T(8,128)(2,1)}, bf16[480,768]{1,0:T(8,128)(2,1)}, u32[]{:S(2)}, u32[]{:S(2)}) collective-permute-start(bf16[480,768]{1,0:T(8,128)(2,1)} %param.10), channel_id=1, source_target_pairs={{0,16},{8,24},{16,32},{24,40},{32,48},{40,56},{48,64},{56,72},{64,... | collective-permute-start | bytes 2211848 | tf_op jit(solution)/shard_map/ppermute | solution.py:28
  17.4 43.4 %collective-permute-start.2 = (s32[480]{0:T(512)}, s32[480]{0:T(512)S(1)}, u32[]{:S(2)}, u32[]{:S(2)}) collective-permute-start(s32[480]{0:T(512)} %param.11), channel_id=1, source_target_pairs={{0,16},{8,24},{16,32},{24,40},{32,48},{40,56},{48,64},{56,72},{64,... | collective-permute-start | bytes 5768 | tf_op jit(solution)/shard_map/ppermute | solution.py:28
  60.8 42.7 %collective-permute-start.3 = (s32[480]{0:T(512)}, s32[480]{0:T(512)S(1)}, u32[]{:S(2)}, u32[]{:S(2)}) collective-permute-start(s32[480]{0:T(512)} %param.11), channel_id=1, source_target_pairs={{0,8},{8,16},{16,24},{24,32},{32,40},{40,48},{48,56},{56,64},{64,7... | collective-permute-start | bytes 5768 | tf_op jit(solution)/shard_map/ppermute | solution.py:28
  104.2 0.9 copy-start.1
  106.8 2.9 %copy-start.4 = (s32[480]{0:T(512)S(1)}, s32[480]{0:T(512)}, u32[]{:S(2)}) copy-start(s32[480]{0:T(512)} %param.11) | copy-start | bytes 5764
  109.7 105.0 %copy-start.3 = (bf16[2,16,7168]{2,1,0:T(8,128)(2,1)S(1)}, bf16[2,16,7168]{2,1,0:T(8,128)(2,1)}, u32[]{:S(2)}) copy-start(bf16[2,16,7168]{2,1,0:T(8,128)(2,1)} %param.12) | copy-start | bytes 1376260
  217.0 5.4 %copy-start.2 = (bf16[6,480,128]{2,1,0:T(8,128)(2,1)S(1)}, bf16[6,480,128]{2,1,0:T(8,128)(2,1)}, u32[]{:S(2)}) copy-start(bf16[6,480,128]{2,1,0:T(8,128)(2,1)} %get-tuple-element.46) | copy-start | bytes 2211844
  217.0 48.5 %all-to-all-start = ((bf16[8,2,16,7168]{3,2,1,0:T(8,128)(2,1)}), bf16[8,2,16,7168]{3,2,1,0:T(8,128)(2,1)}, u32[]{:S(2)}, u32[]{:S(2)}) async-start(bf16[8,2,16,7168]{3,2,1,0:T(8,128)(2,1)} %broadcast_in_dim.35), calls=%async_computation | async-start | bytes 7340032 | tf_op jit(solution)/shard_map/all_to_all | solution.py:43
  274.0 4.1 %copy-start.5 = (bf16[2,128,896]{2,1,0:T(8,128)(2,1)S(1)}, bf16[2,128,896]{2,1,0:T(8,128)(2,1)}, u32[]{:S(2)}) copy-start(bf16[2,128,896]{2,1,0:T(8,128)(2,1)} %param.13) | copy-start | bytes 1376260

commit v2 on v1

--- a/solution.py
+++ b/solution.py
@@ -50,8 +50,39 @@
     seq_index = lax.axis_index("seq")
     head_index = lax.axis_index("head")
     head_count = lax.axis_size("head")
+    pieces = gathered(gradients, "head")
+    mats_here, rows_here = gradients.shape[0], gradients.shape[1]
+    cols_here = weights.shape[2]
+    gram = jnp.einsum(
+        "jmrd,kmsd->mjrks", pieces, pieces, preferred_element_type=jnp.float32
+    ).reshape(mats_here, HD, HD)
+    norm_value = jnp.sqrt(jnp.trace(gram, axis1=1, axis2=2)) + norm_eps
+    square = gram / (norm_value * norm_value)[:, None, None]
+    identity = jnp.eye(HD, dtype=jnp.float32)
+    total = None
+    for iteration in range(NS_ITERS):
+        poly = polynomial_of(square, identity)
+        total = poly if total is None else jnp.matmul(poly, total, precision=highest)
+        if iteration + 1 < NS_ITERS:
+            square = jnp.matmul(
+                poly, jnp.matmul(square, poly, precision=highest), precision=highest
+            )
+    own_cols = lax.dynamic_slice_in_dim(pieces, head_index * cols_here, cols_here, 3)
+    start = own_cols.astype(jnp.float32) / norm_value[None, :, None, None]
+    current = jnp.einsum(
+        "mijr,jmrd->mid",
+        total.reshape(mats_here, HD, head_count, rows_here),
+        start,
+        precision=highest,
+    )
+    update = (current * (update_gain * math.sqrt(D))).astype(jnp.bfloat16)
+    update, query_vectors = lax.optimization_barrier((update, query_vectors))
     local_block = (key_vectors, value_vectors, doc_ids)
-    earlier = [shifted(local_block, "seq", distance) for distance in range(1, REACH + 1)]
+    earlier = []
+    passed = local_block
+    for distance in range(REACH):
+        passed = shifted(passed, "seq", 1)
+        earlier.append(passed)
     ordered = [earlier[REACH - 1 - position] for position in range(REACH)] + [local_block]
     keys_all = jnp.concatenate([member[0] for member in ordered], axis=0)
     values_all = jnp.concatenate([member[1] for member in ordered], axis=0)
@@ -92,32 +123,6 @@
     max_logit = gathered(seq_max, "head").reshape(heads_all)
     root_gamma = jnp.sqrt(clip_tau / jnp.maximum(max_logit, clip_tau))
 
-    pieces = gathered(gradients, "head")
-    mats_here, rows_here = gradients.shape[0], gradients.shape[1]
-    cols_here = weights.shape[2]
-    gram = jnp.einsum(
-        "jmrd,kmsd->mjrks", pieces, pieces, preferred_element_type=jnp.float32
-    ).reshape(mats_here, HD, HD)
-    norm_value = jnp.sqrt(jnp.trace(gram, axis1=1, axis2=2)) + norm_eps
-    square = gram / (norm_value * norm_value)[:, None, None]
-    identity = jnp.eye(HD, dtype=jnp.float32)
-    total = None
-    for iteration in range(NS_ITERS):
-        poly = polynomial_of(square, identity)
-        total = poly if total is None else jnp.matmul(poly, total, precision=highest)
-        if iteration + 1 < NS_ITERS:
-            square = jnp.matmul(
-                poly, jnp.matmul(square, poly, precision=highest), precision=highest
-            )
-    own_cols = lax.dynamic_slice_in_dim(pieces, head_index * cols_here, cols_here, 3)
-    start = own_cols.astype(jnp.float32) / norm_value[None, :, None, None]
-    current = jnp.einsum(
-        "mijr,jmrd->mid",
-        total.reshape(mats_here, HD, head_count, rows_here),
-        start,
-        precision=highest,
-    )
-    update = (current * (update_gain * math.sqrt(D))).astype(jnp.bfloat16)
     matrix_index = seq_index * mats_here + jnp.arange(mats_here, dtype=jnp.int32)
     one_hot = (matrix_index[:, None] % heads_all == head_slots[None, :]).astype(jnp.float32)
     picked = jnp.sum(one_hot * root_gamma[None, :], axis=1)

time: 282 us -> 190 us (0.67)
  blocking collectives: 58.8 us -> 0 us
  waiting for transfers between devices: 83.8 us -> 63.4 us
  starting transfers between devices: 65.5 us -> 55.5 us
  matrix products: 40.6 us -> 35.9 us
    all_to_all x2 -> x0, blocking collectives: 58.8 us -> none  [gathered(): return lax.all_to_all(spread, axis, 0, 0, tiled=True)]
    ppermute x6, starting transfers between devices: 60.3 us -> 17.1 us  [shifted(): return lax.ppermute(shard, axis, pairs)]
    all_to_all x1 -> x3, starting transfers between devices: 5.2 us -> 38.4 us  [gathered(): return lax.all_to_all(spread, axis, 0, 0, tiled=True)]
    all_to_all x1 -> x3, waiting for transfers between devices: 41.4 us -> 16 us  [gathered(): return lax.all_to_all(spread, axis, 0, 0, tiled=True)]
    ppermute x6, waiting for transfers between devices: 42.4 us -> 47.4 us  [shifted(): return lax.ppermute(shard, axis, pairs)]
    dot_general x6, matrix products: 13.5 us -> 9.87 us  [one_head(): jnp.dot(exp_scores.astype(jnp.bfloat16), value_cols, preferred_element_ty...]
  transfers between devices with their start and end apart: 7 -> 9, of which waited for: 3 -> 5; matrix products, arithmetic and copies ran while one was open for 2% -> 3% of each run, Pallas kernels for 0% -> 0%
where the time goes in v2:
time: 190 us; the launch traced here: 189 us
  waiting for transfers between devices  63.4 us (33%)
  starting transfers between devices  55.5 us (29%)
  matrix products  35.9 us (19%)
  local copies, waits for them, and re-layouts  14.9 us (8%)
  other arithmetic  14.5 us (8%)
  loops' own time  3.98 us (2%)
    ppermute x6, waiting for transfers between devices, shifted(): return lax.ppermute(shard, axis, pairs)  47.4 us
    all_to_all x3, starting transfers between devices, gathered(): return lax.all_to_all(spread, axis, 0, 0, tiled=True)  38.4 us
    ppermute x6, starting transfers between devices, shifted(): return lax.ppermute(shard, axis, pairs)  17.1 us
    all_to_all x3, waiting for transfers between devices, gathered(): return lax.all_to_all(spread, axis, 0, 0, tiled=True)  16 us
    dot_general x6, matrix products, one_head(): jnp.einsum('qd,kd->qk', query_cols, key_cols, preferred_element_type=jnp....  12.2 us
    dot_general x6, matrix products, one_head(): jnp.dot(exp_scores.astype(jnp.bfloat16), value_cols, preferred_element_ty...  9.87 us
    reduce_max x6, other arithmetic, one_head(): return (mixed_rows.astype(jnp.bfloat16), jnp.max(row_max))  8.41 us
    dot_general x1, matrix products, shards(): jnp.einsum('jmrd,kmsd->mjrks', pieces, pieces, preferred_element_type=jnp...  6.9 us
  transfers between devices with their start and end apart: 9, of which 5 were waited for; matrix products, arithmetic and copies ran while one was open for 3% of the time, Pallas kernels for 0%

profile of v2, /device:TPU:1, one launch (start us, length us, event | category | flops | bytes accessed | tf_op | source)
XLA Modules:
  0.0 189.1 jit_solution(8381502276657580565)
XLA Ops:
  0.6 3.3 %broadcast_in_dim.35 = bf16[8,2,16,7168]{3,2,1,0:T(8,128)(2,1)} broadcast(bf16[2,16,7168]{2,1,0:T(8,128)(2,1)} %param.12), dimensions={1,2,3} | broadcast | bytes 4128768 | tf_op jit(solution)/shard_map/broadcast_in_dim | solution.py:42
  3.9 15.0 %all-to-all-start = ((bf16[8,2,16,7168]{3,2,1,0:T(8,128)(2,1)}), bf16[8,2,16,7168]{3,2,1,0:T(8,128)(2,1)}, u32[]{:S(2)}, u32[]{:S(2)}) async-start(bf16[8,2,16,7168]{3,2,1,0:T(8,128)(2,1)} %broadcast_in_dim.35), calls=%async_computation | async-start | bytes 7340032 | tf_op jit(solution)/shard_map/all_to_all | solution.py:43
  18.9 2.1 %collective-permute-start = (bf16[480,768]{1,0:T(8,128)(2,1)S(1)}, bf16[480,768]{1,0:T(8,128)(2,1)}, u32[]{:S(2)}, u32[]{:S(2)}) collective-permute-start(bf16[480,768]{1,0:T(8,128)(2,1)S(1)} %copy-done), channel_id=1, source_target_pairs={{0,8},{8,16},{16,24},{24,32},{32,40},{40,48},{48,56},{56,64},{64,7... | collective-permute-start | bytes 2211848 | tf_op jit(solution)/shard_map/ppermute | solution.py:28
  21.1 2.2 %collective-permute-start.4 = (bf16[480,768]{1,0:T(8,128)(2,1)S(1)}, bf16[480,768]{1,0:T(8,128)(2,1)}, u32[]{:S(2)}, u32[]{:S(2)}) collective-permute-start(bf16[480,768]{1,0:T(8,128)(2,1)S(1)} %copy-done.1), channel_id=1, source_target_pairs={{0,8},{8,16},{16,24},{24,32},{32,40},{40,48},{48,56},{56,64},{64,7... | collective-permute-start | bytes 2211848 | tf_op jit(solution)/shard_map/ppermute | solution.py:28
  24.5 11.6 %collective-permute-done = bf16[480,768]{1,0:T(8,128)(2,1)} collective-permute-done((bf16[480,768]{1,0:T(8,128)(2,1)S(1)}, bf16[480,768]{1,0:T(8,128)(2,1)}, u32[]{:S(2)}, u32[]{:S(2)}) %collective-permute-start) | collective-permute-done | bytes 737312 | tf_op jit(solution)/shard_map/ppermute | solution.py:28
  36.2 5.2 %collective-permute-start.1 = (bf16[480,768]{1,0:T(8,128)(2,1)}, bf16[480,768]{1,0:T(8,128)(2,1)}, u32[]{:S(2)}, u32[]{:S(2)}) collective-permute-start(bf16[480,768]{1,0:T(8,128)(2,1)} %collective-permute-done), channel_id=1, source_target_pairs={{0,8},{8,16},{16,24},{24,32},{32,40},{40,48},{48,56},{56,64},{64,7... | collective-permute-start | bytes 2211848 | tf_op jit(solution)/shard_map/ppermute | solution.py:28
  41.4 10.6 %collective-permute-done.4 = bf16[480,768]{1,0:T(8,128)(2,1)} collective-permute-done((bf16[480,768]{1,0:T(8,128)(2,1)S(1)}, bf16[480,768]{1,0:T(8,128)(2,1)}, u32[]{:S(2)}, u32[]{:S(2)}) %collective-permute-start.4) | collective-permute-done | bytes 737312 | tf_op jit(solution)/shard_map/ppermute | solution.py:28
  52.0 5.1 %collective-permute-start.5 = (bf16[480,768]{1,0:T(8,128)(2,1)}, bf16[480,768]{1,0:T(8,128)(2,1)}, u32[]{:S(2)}, u32[]{:S(2)}) collective-permute-start(bf16[480,768]{1,0:T(8,128)(2,1)} %collective-permute-done.4), channel_id=1, source_target_pairs={{0,8},{8,16},{16,24},{24,32},{32,40},{40,48},{48,56},{56,64},{64,7... | collective-permute-start | bytes 2211848 | tf_op jit(solution)/shard_map/ppermute | solution.py:28
  58.6 25.1 %collective-permute-done.3 = s32[480]{0:T(512)S(1)} collective-permute-done((s32[480]{0:T(512)S(1)}, s32[480]{0:T(512)S(1)}, u32[]{:S(2)}, u32[]{:S(2)}) %collective-permute-start.3) | collective-permute-done | bytes 1952 | tf_op jit(solution)/shard_map/ppermute | solution.py:28
  83.8 1.5 pad_maximum_fusion
  85.3 3.1 %pad_maximum_fusion.1 = bf16[1440,768]{1,0:T(8,128)(2,1)} fusion(bf16[480,768]{1,0:T(8,128)(2,1)} %param.10, bf16[480,768]{1,0:T(8,128)(2,1)} %collective-permute-done.4, bf16[480,768]{1,0:T(8,128)(2,1)} %collective-permute-done.5), kind=kLoop, calls=%fused_computation.21 | loop fusion | flops 6635520 | bytes 4423680 | tf_op jit(solution)/shard_map/concatenate | solution.py:88
  88.4 6.9 %select_reduce_fusion = (f32[2]{0:T(128)S(1)}, f32[2,8,16,8,16]{4,2,3,1,0:T(8,128)S(1)}) fusion(pred[8,16,8,16]{3,1,2,0:T(8,128)(4,1)S(1)} %broadcast_compare_fusion, bf16[8,2,16,7168]{3,2,1,0:T(8,128)(2,1)} %all-to-all-done), kind=kOutput, calls=%fused_computation.35 | convolution fusion | flops 469827584 | bytes 3817480 | tf_op jit(solution)/shard_map/jmrd,kmsd->mjrks/dot_general | solution.py:56
  101.1 2.0 %fusion.29 = bf16[2,128,896]{2,1,0:T(8,128)(2,1)S(1)} fusion(f32[2,128,8,16]{1,3,2,0:T(8,128)S(1)} %bitcast.65, f32[2]{0:T(128)S(1)} %get-tuple-element.126, bf16[8,2,16,7168]{3,2,1,0:T(8,128)(2,1)} %all-to-all-done, s32[]{:T(128)S(6)} %select_n.39), kind=kOutput, calls=%fused_computation.24 | convolution fusion | flops 353239040 | bytes 1048588 | tf_op jit(solution)/shard_map/mijr,jmrd->mid/dot_general | solution.py:72
  103.2 42.5 %while.13 = (s32[]{:T(128)}, bf16[6,480,128]{2,1,0:T(8,128)(2,1)S(1)}, f32[6]{0:T(128)S(1)}, s32[6]{0:T(128)S(1)}, bf16[480,768]{1,0:T(8,128)(2,1)}, /*index=5*/...) while((s32[]{:T(128)}, ...), condition=%wide.region_5.6_spmd.clone, body=%wide.region_1.5_spmd.clone.sunk | while | flops 362310720 | bytes 9495907 | solution.py:118
  104.4 2.0 %fusion.94 = (f32[480]{0:T(512)S(1)}, f32[480,1440]{1,0:T(8,128)S(1)}) fusion(bf16[1440,768]{1,0:T(8,128)(2,1)S(1)} %get-tuple-element.248, s32[]{:T(128)S(6)} %select_n.49, bf16[480,768]{1,0:T(8,128)(2,1)} %get-tuple-element.247, pred[1440]{0:T(1024)(128)(4,1)S(1)} %get-tuple-element.254, s32[480]{0:T(512)S(1)} %get-tuple-element.252, ...), kind=kOutput, calls=%fused_computation.57.clone.1 | convolution fusion | flops 181785120 | bytes 3281792 | tf_op jit(solution)/shard_map/while/body/eval_jaxpr/qd,kd->qk/dot_general | solution.py:105
  107.9 1.6 fusion.96
  111.5 2.0 %fusion.94 = (f32[480]{0:T(512)S(1)}, f32[480,1440]{1,0:T(8,128)S(1)}) fusion(bf16[1440,768]{1,0:T(8,128)(2,1)S(1)} %get-tuple-element.248, s32[]{:T(128)S(6)} %select_n.49, bf16[480,768]{1,0:T(8,128)(2,1)} %get-tuple-element.247, pred[1440]{0:T(1024)(128)(4,1)S(1)} %get-tuple-element.254, s32[480]{0:T(512)S(1)} %get-tuple-element.252, ...), kind=kOutput, calls=%fused_computation.57.clone.1 | convolution fusion | flops 181785120 | bytes 3281792 | tf_op jit(solution)/shard_map/while/body/eval_jaxpr/qd,kd->qk/dot_general | solution.py:105
  114.9 1.6 fusion.96
  118.6 2.0 %fusion.94 = (f32[480]{0:T(512)S(1)}, f32[480,1440]{1,0:T(8,128)S(1)}) fusion(bf16[1440,768]{1,0:T(8,128)(2,1)S(1)} %get-tuple-element.248, s32[]{:T(128)S(6)} %select_n.49, bf16[480,768]{1,0:T(8,128)(2,1)} %get-tuple-element.247, pred[1440]{0:T(1024)(128)(4,1)S(1)} %get-tuple-element.254, s32[480]{0:T(512)S(1)} %get-tuple-element.252, ...), kind=kOutput, calls=%fused_computation.57.clone.1 | convolution fusion | flops 181785120 | bytes 3281792 | tf_op jit(solution)/shard_map/while/body/eval_jaxpr/qd,kd->qk/dot_general | solution.py:105
  120.6 1.4 fusion.95
  122.0 1.6 fusion.96
  125.6 2.0 %fusion.94 = (f32[480]{0:T(512)S(1)}, f32[480,1440]{1,0:T(8,128)S(1)}) fusion(bf16[1440,768]{1,0:T(8,128)(2,1)S(1)} %get-tuple-element.248, s32[]{:T(128)S(6)} %select_n.49, bf16[480,768]{1,0:T(8,128)(2,1)} %get-tuple-element.247, pred[1440]{0:T(1024)(128)(4,1)S(1)} %get-tuple-element.254, s32[480]{0:T(512)S(1)} %get-tuple-element.252, ...), kind=kOutput, calls=%fused_computation.57.clone.1 | convolution fusion | flops 181785120 | bytes 3281792 | tf_op jit(solution)/shard_map/while/body/eval_jaxpr/qd,kd->qk/dot_general | solution.py:105
  127.7 1.4 fusion.95
  129.1 1.6 fusion.96
  132.7 2.0 %fusion.94 = (f32[480]{0:T(512)S(1)}, f32[480,1440]{1,0:T(8,128)S(1)}) fusion(bf16[1440,768]{1,0:T(8,128)(2,1)S(1)} %get-tuple-element.248, s32[]{:T(128)S(6)} %select_n.49, bf16[480,768]{1,0:T(8,128)(2,1)} %get-tuple-element.247, pred[1440]{0:T(1024)(128)(4,1)S(1)} %get-tuple-element.254, s32[480]{0:T(512)S(1)} %get-tuple-element.252, ...), kind=kOutput, calls=%fused_computation.57.clone.1 | convolution fusion | flops 181785120 | bytes 3281792 | tf_op jit(solution)/shard_map/while/body/eval_jaxpr/qd,kd->qk/dot_general | solution.py:105
  136.2 1.6 fusion.96
  139.8 2.0 %fusion.94 = (f32[480]{0:T(512)S(1)}, f32[480,1440]{1,0:T(8,128)S(1)}) fusion(bf16[1440,768]{1,0:T(8,128)(2,1)S(1)} %get-tuple-element.248, s32[]{:T(128)S(6)} %select_n.49, bf16[480,768]{1,0:T(8,128)(2,1)} %get-tuple-element.247, pred[1440]{0:T(1024)(128)(4,1)S(1)} %get-tuple-element.254, s32[480]{0:T(512)S(1)} %get-tuple-element.252, ...), kind=kOutput, calls=%fused_computation.57.clone.1 | convolution fusion | flops 181785120 | bytes 3281792 | tf_op jit(solution)/shard_map/while/body/eval_jaxpr/qd,kd->qk/dot_general | solution.py:105
  143.2 1.6 fusion.96
  146.3 16.5 %all-to-all-start.1 = ((f32[96,1,6]{2,1,0:T(1,128)}), f32[96,1,6]{2,1,0:T(1,128)S(1)}, u32[]{:S(2)}, u32[]{:S(2)}) async-start(f32[96,1,6]{2,1,0:T(1,128)} %broadcast_in_dim.38), calls=%async_computation.1 | async-start | bytes 98304 | tf_op jit(solution)/shard_map/all_to_all | solution.py:43
  162.9 12.9 %all-to-all-done.1 = f32[96,1,6]{2,1,0:T(1,128)S(1)} async-done(((f32[96,1,6]{2,1,0:T(1,128)}), f32[96,1,6]{2,1,0:T(1,128)S(1)}, u32[]{:S(2)}, u32[]{:S(2)}) %all-to-all-start.1) | async-done | bytes 2336 | tf_op jit(solution)/shard_map/all_to_all | solution.py:43
  176.5 6.8 %all-to-all-start.2 = ((f32[8,1,6]{2,1,0:T(1,128)}), f32[8,1,6]{2,1,0:T(1,128)S(1)}, u32[]{:S(2)}, u32[]{:S(2)}) async-start(f32[8,1,6]{2,1,0:T(1,128)} %broadcast_in_dim.39), calls=%async_computation.2 | async-start | bytes 8192 | tf_op jit(solution)/shard_map/all_to_all | solution.py:43
  184.7 3.1 %all-to-all-done.2 = f32[8,1,6]{2,1,0:T(1,128)S(1)} async-done(((f32[8,1,6]{2,1,0:T(1,128)}), f32[8,1,6]{2,1,0:T(1,128)S(1)}, u32[]{:S(2)}, u32[]{:S(2)}) %all-to-all-start.2) | async-done | bytes 224 | tf_op jit(solution)/shard_map/all_to_all | solution.py:43
  (75 shorter events, 26.2 us)
Async XLA Ops:
  3.9 15.0 %copy-start = (bf16[480,768]{1,0:T(8,128)(2,1)S(1)}, bf16[480,768]{1,0:T(8,128)(2,1)}, u32[]{:S(2)}) copy-start(bf16[480,768]{1,0:T(8,128)(2,1)} %param.9) | copy-start | bytes 2211844
  3.9 17.2 %copy-start.1 = (bf16[480,768]{1,0:T(8,128)(2,1)S(1)}, bf16[480,768]{1,0:T(8,128)(2,1)}, u32[]{:S(2)}) copy-start(bf16[480,768]{1,0:T(8,128)(2,1)} %param.10) | copy-start | bytes 2211844
  3.9 19.3 %copy-start.5 = (s32[480]{0:T(512)S(1)}, s32[480]{0:T(512)}, u32[]{:S(2)}) copy-start(s32[480]{0:T(512)} %param.11) | copy-start | bytes 5764
  3.9 84.5 %all-to-all-start = ((bf16[8,2,16,7168]{3,2,1,0:T(8,128)(2,1)}), bf16[8,2,16,7168]{3,2,1,0:T(8,128)(2,1)}, u32[]{:S(2)}, u32[]{:S(2)}) async-start(bf16[8,2,16,7168]{3,2,1,0:T(8,128)(2,1)} %broadcast_in_dim.35), calls=%async_computation | async-start | bytes 7340032 | tf_op jit(solution)/shard_map/all_to_all | solution.py:43
  18.9 17.2 %collective-permute-start = (bf16[480,768]{1,0:T(8,128)(2,1)S(1)}, bf16[480,768]{1,0:T(8,128)(2,1)}, u32[]{:S(2)}, u32[]{:S(2)}) collective-permute-start(bf16[480,768]{1,0:T(8,128)(2,1)S(1)} %copy-done), channel_id=1, source_target_pairs={{0,8},{8,16},{16,24},{24,32},{32,40},{40,48},{48,56},{56,64},{64,7... | collective-permute-start | bytes 2211848 | tf_op jit(solution)/shard_map/ppermute | solution.py:28
  21.1 30.9 %collective-permute-start.4 = (bf16[480,768]{1,0:T(8,128)(2,1)S(1)}, bf16[480,768]{1,0:T(8,128)(2,1)}, u32[]{:S(2)}, u32[]{:S(2)}) collective-permute-start(bf16[480,768]{1,0:T(8,128)(2,1)S(1)} %copy-done.1), channel_id=1, source_target_pairs={{0,8},{8,16},{16,24},{24,32},{32,40},{40,48},{48,56},{56,64},{64,7... | collective-permute-start | bytes 2211848 | tf_op jit(solution)/shard_map/ppermute | solution.py:28
  23.2 34.0 %collective-permute-start.2 = (s32[480]{0:T(512)S(1)}, s32[480]{0:T(512)S(1)}, u32[]{:S(2)}, u32[]{:S(2)}) collective-permute-start(s32[480]{0:T(512)S(1)} %copy-done.5), channel_id=1, source_target_pairs={{0,8},{8,16},{16,24},{24,32},{32,40},{40,48},{48,56},{56,64},{64,7... | collective-permute-start | bytes 5768 | tf_op jit(solution)/shard_map/ppermute | solution.py:28
  36.2 47.6 %collective-permute-start.1 = (bf16[480,768]{1,0:T(8,128)(2,1)}, bf16[480,768]{1,0:T(8,128)(2,1)}, u32[]{:S(2)}, u32[]{:S(2)}) collective-permute-start(bf16[480,768]{1,0:T(8,128)(2,1)} %collective-permute-done), channel_id=1, source_target_pairs={{0,8},{8,16},{16,24},{24,32},{32,40},{40,48},{48,56},{56,64},{64,7... | collective-permute-start | bytes 2211848 | tf_op jit(solution)/shard_map/ppermute | solution.py:28
  52.0 33.3 %collective-permute-start.5 = (bf16[480,768]{1,0:T(8,128)(2,1)}, bf16[480,768]{1,0:T(8,128)(2,1)}, u32[]{:S(2)}, u32[]{:S(2)}) collective-permute-start(bf16[480,768]{1,0:T(8,128)(2,1)} %collective-permute-done.4), channel_id=1, source_target_pairs={{0,8},{8,16},{16,24},{24,32},{32,40},{40,48},{48,56},{56,64},{64,7... | collective-permute-start | bytes 2211848 | tf_op jit(solution)/shard_map/ppermute | solution.py:28
  57.2 26.5 %collective-permute-start.3 = (s32[480]{0:T(512)S(1)}, s32[480]{0:T(512)S(1)}, u32[]{:S(2)}, u32[]{:S(2)}) collective-permute-start(s32[480]{0:T(512)S(1)} %collective-permute-done.2), channel_id=1, source_target_pairs={{0,8},{8,16},{16,24},{24,32},{32,40},{40,48},{48,56},{56,64},{64,7... | collective-permute-start | bytes 5768 | tf_op jit(solution)/shard_map/ppermute | solution.py:28
  99.5 3.7 %copy-start.2 = (bf16[6,480,128]{2,1,0:T(8,128)(2,1)S(1)}, bf16[6,480,128]{2,1,0:T(8,128)(2,1)}, u32[]{:S(2)}) copy-start(bf16[6,480,128]{2,1,0:T(8,128)(2,1)} %custom-call) | copy-start | bytes 2211844
  103.1 85.0 %copy-start.4 = (bf16[2,128,896]{2,1,0:T(8,128)(2,1)}, bf16[2,128,896]{2,1,0:T(8,128)(2,1)S(1)}, u32[]{:S(2)}) copy-start(bf16[2,128,896]{2,1,0:T(8,128)(2,1)S(1)} %fusion.29) | copy-start | bytes 1376260
  145.6 42.5 %copy-start.3 = (bf16[2,128,896]{2,1,0:T(8,128)(2,1)S(1)}, bf16[2,128,896]{2,1,0:T(8,128)(2,1)}, u32[]{:S(2)}) copy-start(bf16[2,128,896]{2,1,0:T(8,128)(2,1)} %param.13) | copy-start | bytes 1376260
  146.3 29.5 %all-to-all-start.1 = ((f32[96,1,6]{2,1,0:T(1,128)}), f32[96,1,6]{2,1,0:T(1,128)S(1)}, u32[]{:S(2)}, u32[]{:S(2)}) async-start(f32[96,1,6]{2,1,0:T(1,128)} %broadcast_in_dim.38), calls=%async_computation.1 | async-start | bytes 98304 | tf_op jit(solution)/shard_map/all_to_all | solution.py:43
  176.5 11.3 %all-to-all-start.2 = ((f32[8,1,6]{2,1,0:T(1,128)}), f32[8,1,6]{2,1,0:T(1,128)S(1)}, u32[]{:S(2)}, u32[]{:S(2)}) async-start(f32[8,1,6]{2,1,0:T(1,128)} %broadcast_in_dim.39), calls=%async_computation.2 | async-start | bytes 8192 | tf_op jit(solution)/shard_map/all_to_all | solution.py:43

commit v3 on v2

--- a/solution.py
+++ b/solution.py
@@ -76,13 +76,36 @@
         precision=highest,
     )
     update = (current * (update_gain * math.sqrt(D))).astype(jnp.bfloat16)
-    update, query_vectors = lax.optimization_barrier((update, query_vectors))
     local_block = (key_vectors, value_vectors, doc_ids)
-    earlier = []
-    passed = local_block
-    for distance in range(REACH):
-        passed = shifted(passed, "seq", 1)
-        earlier.append(passed)
+    query_place = seq_index * tokens_here + jnp.arange(tokens_here, dtype=jnp.int32)
+    def block_max(member, block):
+        keys_blk, docs_blk = member[0], member[2]
+        place_blk = (seq_index - REACH + block) * tokens_here + jnp.arange(
+            tokens_here, dtype=jnp.int32
+        )
+        allowed = (
+            (doc_ids[:, None] == docs_blk[None, :])
+            & (place_blk[None, :] <= query_place[:, None])
+            & (place_blk[None, :] >= 0)
+        )
+        found = []
+        for head_slot in range(heads_here):
+            cols = slice(head_slot * HD, (head_slot + 1) * HD)
+            scores = jnp.einsum(
+                "qd,kd->qk", query_vectors[:, cols], keys_blk[:, cols],
+                preferred_element_type=jnp.float32,
+            ) / math.sqrt(HD)
+            found.append(jnp.max(jnp.where(allowed, scores, masked_fill)))
+        return jnp.stack(found)
+
+    first = shifted(local_block, "seq", 1)
+    local_max = block_max(local_block, REACH)
+    first, local_max = lax.optimization_barrier((first, local_max))
+    second = shifted(first, "seq", 1)
+    first_max = block_max(first, REACH - 1)
+    second, first_max, update = lax.optimization_barrier((second, first_max, update))
+    head_max = jnp.maximum(jnp.maximum(local_max, first_max), block_max(second, REACH - 2))
+    earlier = [first, second]
     ordered = [earlier[REACH - 1 - position] for position in range(REACH)] + [local_block]
     keys_all = jnp.concatenate([member[0] for member in ordered], axis=0)
     values_all = jnp.concatenate([member[1] for member in ordered], axis=0)
@@ -90,7 +113,6 @@
     key_place = (seq_index - REACH) * tokens_here + jnp.arange(
         (REACH + 1) * tokens_here, dtype=jnp.int32
     )
-    query_place = seq_index * tokens_here + jnp.arange(tokens_here, dtype=jnp.int32)
     same_doc = (
         (doc_ids[:, None] == docs_all[None, :])
         & (key_place[None, :] <= query_place[:, None])
@@ -115,7 +137,7 @@
         )
         return (mixed_rows.astype(jnp.bfloat16), jnp.max(row_max))
 
-    mixed_heads, head_max = lax.map(one_head, jnp.arange(heads_here, dtype=jnp.int32))
+    mixed_heads, _ = lax.map(one_head, jnp.arange(heads_here, dtype=jnp.int32))
     attention_out = jnp.transpose(mixed_heads, (1, 0, 2)).reshape(tokens_here, heads_here * HD)
     heads_all = heads_here * head_count
     head_slots = jnp.arange(heads_all, dtype=jnp.int32)

time: 190 us -> 176 us (0.926)
  waiting for transfers between devices: 63.4 us -> 15 us
  matrix products: 35.9 us -> 72.2 us
  local copies, waits for them, and re-layouts: 14.9 us -> 23.4 us
  other arithmetic: 14.5 us -> 8.25 us
  starting transfers between devices: 55.5 us -> 50.6 us
    ppermute x6, waiting for transfers between devices: 47.4 us -> 13.1 us  [shifted(): return lax.ppermute(shard, axis, pairs)]
    dot_general x0 -> x18, matrix products: none -> 31.7 us  [block_max(): jnp.einsum('qd,kd->qk', query_vectors[:, cols], keys_blk[:, cols], prefer...]
    all_to_all x3, waiting for transfers between devices: 16 us -> 1.98 us  [gathered(): return lax.all_to_all(spread, axis, 0, 0, tiled=True)]
    another operation x0 -> x3, local copies, waits for them, and re-layouts: none -> 11.6 us  [block_max(): return jnp.stack(found)]
    reduce_max x6 -> x0, other arithmetic: 8.41 us -> none  [one_head(): return (mixed_rows.astype(jnp.bfloat16), jnp.max(row_max))]
    ppermute x6, starting transfers between devices: 17.1 us -> 12.6 us  [shifted(): return lax.ppermute(shard, axis, pairs)]
    dynamic_update_slice x6 -> x0, local copies, waits for them, and re-layouts: 4.55 us -> none  [shards(): lax.map(one_head, jnp.arange(heads_here, dtype=jnp.int32))]
    dot_general x6, matrix products: 9.87 us -> 13.5 us  [one_head(): jnp.dot(exp_scores.astype(jnp.bfloat16), value_cols, preferred_element_ty...]
  transfers between devices with their start and end apart: 9 -> 9, of which waited for: 5 -> 2; matrix products, arithmetic and copies ran while one was open for 3% -> 47% of each run, Pallas kernels for 0% -> 0%
where the time goes in v3:
time: 176 us; the launch traced here: 175 us
  matrix products  72.2 us (41%)
  starting transfers between devices  50.6 us (29%)
  local copies, waits for them, and re-layouts  23.4 us (13%)
  waiting for transfers between devices  15 us (9%)
  other arithmetic  8.25 us (5%)
  loops' own time  4.15 us (2%)
    all_to_all x3, starting transfers between devices, gathered(): return lax.all_to_all(spread, axis, 0, 0, tiled=True)  38 us
    dot_general x18, matrix products, block_max(): jnp.einsum('qd,kd->qk', query_vectors[:, cols], keys_blk[:, cols], prefer...  31.7 us
    dot_general x6, matrix products, one_head(): jnp.dot(exp_scores.astype(jnp.bfloat16), value_cols, preferred_element_ty...  13.5 us
    ppermute x6, waiting for transfers between devices, shifted(): return lax.ppermute(shard, axis, pairs)  13.1 us
    ppermute x6, starting transfers between devices, shifted(): return lax.ppermute(shard, axis, pairs)  12.6 us
    dot_general x6, matrix products, one_head(): jnp.einsum('qd,kd->qk', query_cols, key_cols, preferred_element_type=jnp....  12.1 us
    another operation x3, local copies, waits for them, and re-layouts, block_max(): return jnp.stack(found)  11.6 us
    dot_general x1, matrix products, shards(): jnp.einsum('jmrd,kmsd->mjrks', pieces, pieces, preferred_element_type=jnp...  7.08 us
  transfers between devices with their start and end apart: 9, of which 2 were waited for; matrix products, arithmetic and copies ran while one was open for 47% of the time, Pallas kernels for 0%

profile of v3, /device:TPU:1, one launch (start us, length us, event | category | flops | bytes accessed | tf_op | source)
XLA Modules:
  0.0 174.6 jit_solution(411281969245421776)
XLA Ops:
  0.6 3.3 %broadcast_in_dim.53 = bf16[8,2,16,7168]{3,2,1,0:T(8,128)(2,1)} broadcast(bf16[2,16,7168]{2,1,0:T(8,128)(2,1)} %param.12), dimensions={1,2,3} | broadcast | bytes 4128768 | tf_op jit(solution)/shard_map/broadcast_in_dim | solution.py:42
  3.9 15.0 %all-to-all-start = ((bf16[8,2,16,7168]{3,2,1,0:T(8,128)(2,1)}), bf16[8,2,16,7168]{3,2,1,0:T(8,128)(2,1)}, u32[]{:S(2)}, u32[]{:S(2)}) async-start(bf16[8,2,16,7168]{3,2,1,0:T(8,128)(2,1)} %broadcast_in_dim.53), calls=%async_computation | async-start | bytes 7340032 | tf_op jit(solution)/shard_map/all_to_all | solution.py:43
  26.9 2.0 %fusion.81 = f32[]{:T(128)} fusion(bf16[480,768]{1,0:T(8,128)(2,1)S(1)} %copy-done, bf16[480,768]{1,0:T(8,128)(2,1)} %param.8, pred[480]{0:T(512)(128)(4,1)S(1)} %broadcast_compare_fusion.4, s32[480]{0:T(512)S(1)} %iota_add_fusion.3, s32[480]{0:T(512)S(1)} %copy-done.6), kind=kOutput, calls=%fused_computation.105 | convolution fusion | flops 60595200 | bytes 254468 | tf_op jit(solution)/shard_map/qd,kd->qk/dot_general | solution.py:94
  32.9 2.0 %fusion.78 = f32[]{:T(128)} fusion(bf16[480,768]{1,0:T(8,128)(2,1)S(1)} %copy-done, bf16[480,768]{1,0:T(8,128)(2,1)} %param.8, pred[480]{0:T(512)(128)(4,1)S(1)} %broadcast_compare_fusion.4, s32[480]{0:T(512)S(1)} %iota_add_fusion.3, s32[480]{0:T(512)S(1)} %copy-done.6), kind=kOutput, calls=%fused_computation.102 | convolution fusion | flops 60595200 | bytes 254468 | tf_op jit(solution)/shard_map/qd,kd->qk/dot_general | solution.py:94
  35.1 3.9 %stack.69 = f32[6]{0:T(128)S(1)} concatenate(f32[1]{0:T(128)} %bitcast, f32[1]{0:T(128)} %bitcast.1, f32[1]{0:T(128)} %bitcast.2, f32[1]{0:T(128)} %bitcast.3, f32[1]{0:T(128)} %bitcast.4, f32[1]{0:T(128)} %bitcast.5), dimensions={0} | concatenate | bytes 48 | tf_op jit(solution)/shard_map/stack | solution.py:99
  39.0 13.0 %collective-permute-done.2 = s32[480]{0:T(512)S(1)} collective-permute-done((s32[480]{0:T(512)S(1)}, s32[480]{0:T(512)S(1)}, u32[]{:S(2)}, u32[]{:S(2)}) %collective-permute-start.2) | collective-permute-done | bytes 1952 | tf_op jit(solution)/shard_map/ppermute | solution.py:28
  52.0 5.2 %collective-permute-start.3 = (bf16[480,768]{1,0:T(8,128)(2,1)S(1)}, bf16[480,768]{1,0:T(8,128)(2,1)}, u32[]{:S(2)}, u32[]{:S(2)}) collective-permute-start(bf16[480,768]{1,0:T(8,128)(2,1)S(1)} %collective-permute-done), channel_id=1, source_target_pairs={{0,8},{8,16},{16,24},{24,32},{32,40},{40,48},{48,56},{56,64},{64,7... | collective-permute-start | bytes 2211848 | tf_op jit(solution)/shard_map/ppermute | solution.py:28
  57.2 2.2 %collective-permute-start.4 = (bf16[480,768]{1,0:T(8,128)(2,1)S(1)}, bf16[480,768]{1,0:T(8,128)(2,1)}, u32[]{:S(2)}, u32[]{:S(2)}) collective-permute-start(bf16[480,768]{1,0:T(8,128)(2,1)S(1)} %collective-permute-done.1), channel_id=1, source_target_pairs={{0,8},{8,16},{16,24},{24,32},{32,40},{40,48},{48,56},{56,64},{64,7... | collective-permute-start | bytes 2211848 | tf_op jit(solution)/shard_map/ppermute | solution.py:28
  68.7 3.9 %stack.76 = f32[6]{0:T(128)S(1)} concatenate(f32[1]{0:T(128)} %bitcast.7, f32[1]{0:T(128)} %bitcast.9, f32[1]{0:T(128)} %bitcast.11, f32[1]{0:T(128)} %bitcast.13, f32[1]{0:T(128)} %bitcast.15, f32[1]{0:T(128)} %bitcast.17), dimensions={0} | concatenate | bytes 48 | tf_op jit(solution)/shard_map/stack | solution.py:99
  72.6 7.1 %select_reduce_fusion = (f32[2]{0:T(128)S(1)}, f32[2,8,16,8,16]{4,2,3,1,0:T(8,128)S(1)}) fusion(pred[8,16,8,16]{3,1,2,0:T(8,128)(4,1)S(1)} %broadcast_compare_fusion, bf16[8,2,16,7168]{3,2,1,0:T(8,128)(2,1)} %all-to-all-done), kind=kOutput, calls=%fused_computation.83 | convolution fusion | flops 469827584 | bytes 3817480 | tf_op jit(solution)/shard_map/jmrd,kmsd->mjrks/dot_general | solution.py:56
  85.4 2.8 %fusion.59 = bf16[2,128,896]{2,1,0:T(8,128)(2,1)} fusion(f32[2,128,8,16]{1,3,2,0:T(8,128)S(1)} %bitcast.152, f32[2]{0:T(128)S(1)} %get-tuple-element.127, bf16[8,2,16,7168]{3,2,1,0:T(8,128)(2,1)} %all-to-all-done, s32[]{:T(128)S(6)} %select_n.106), kind=kOutput, calls=%fused_computation.72 | convolution fusion | flops 353239040 | bytes 1048588 | tf_op jit(solution)/shard_map/mijr,jmrd->mid/dot_general | solution.py:72
  88.2 2.0 %fusion.66 = f32[]{:T(128)} fusion(bf16[480,768]{1,0:T(8,128)(2,1)} %collective-permute-done.3, bf16[480,768]{1,0:T(8,128)(2,1)S(1)} %copy-done.8, pred[480]{0:T(512)(128)(4,1)S(1)} %broadcast_compare_fusion.2, s32[480]{0:T(512)S(1)} %iota_add_fusion.3, s32[480]{0:T(512)S(1)} %iota_add_fusion.1, s32[480]{0:T(512)S(1)} %collective-permute-done.5, ...), kind=kOutput, calls=%fused_computation.90 | convolution fusion | flops 60595200 | bytes 254468 | tf_op jit(solution)/shard_map/qd,kd->qk/dot_general | solution.py:94
  90.2 2.0 %fusion.67 = f32[]{:T(128)} fusion(bf16[480,768]{1,0:T(8,128)(2,1)} %collective-permute-done.3, bf16[480,768]{1,0:T(8,128)(2,1)S(1)} %copy-done.8, pred[480]{0:T(512)(128)(4,1)S(1)} %broadcast_compare_fusion.2, s32[480]{0:T(512)S(1)} %iota_add_fusion.3, s32[480]{0:T(512)S(1)} %iota_add_fusion.1, s32[480]{0:T(512)S(1)} %collective-permute-done.5, ...), kind=kOutput, calls=%fused_computation.91 | convolution fusion | flops 60595200 | bytes 254468 | tf_op jit(solution)/shard_map/qd,kd->qk/dot_general | solution.py:94
  96.1 2.0 %fusion.70 = f32[]{:T(128)} fusion(bf16[480,768]{1,0:T(8,128)(2,1)} %collective-permute-done.3, bf16[480,768]{1,0:T(8,128)(2,1)S(1)} %copy-done.8, pred[480]{0:T(512)(128)(4,1)S(1)} %broadcast_compare_fusion.2, s32[480]{0:T(512)S(1)} %iota_add_fusion.3, s32[480]{0:T(512)S(1)} %iota_add_fusion.1, s32[480]{0:T(512)S(1)} %collective-permute-done.5, ...), kind=kOutput, calls=%fused_computation.94 | convolution fusion | flops 60595200 | bytes 254468 | tf_op jit(solution)/shard_map/qd,kd->qk/dot_general | solution.py:94
  100.1 3.8 %stack.83 = f32[6]{0:T(128)S(1)} concatenate(f32[1]{0:T(128)} %bitcast.26, f32[1]{0:T(128)} %bitcast.28, f32[1]{0:T(128)} %bitcast.30, f32[1]{0:T(128)} %bitcast.32, f32[1]{0:T(128)} %bitcast.34, f32[1]{0:T(128)} %bitcast.36), dimensions={0} | concatenate | bytes 48 | tf_op jit(solution)/shard_map/stack | solution.py:99
  104.7 16.8 %all-to-all-start.1 = ((f32[96,1,6]{2,1,0:T(1,128)}), f32[96,1,6]{2,1,0:T(1,128)S(1)}, u32[]{:S(2)}, u32[]{:S(2)}) async-start(f32[96,1,6]{2,1,0:T(1,128)} %broadcast_in_dim.56), calls=%async_computation.1 | async-start | bytes 98304 | tf_op jit(solution)/shard_map/all_to_all | solution.py:43
  121.5 3.4 %pad_maximum_fusion = (bf16[1440,768]{1,0:T(8,128)(2,1)S(1)}, bf16[1440,768]{1,0:T(8,128)(2,1)}) fusion(bf16[480,768]{1,0:T(8,128)(2,1)S(1)} %copy-done, bf16[480,768]{1,0:T(8,128)(2,1)} %copy-done.2, bf16[480,768]{1,0:T(8,128)(2,1)} %collective-permute-done.3, bf16[480,768]{1,0:T(8,128)(2,1)} %param.10, bf16[480,768]{1,0:T(8,128)(2,1)} %copy-done.3, ...), kind=kLoop, calls=%fused_computation.20 | loop fusion | flops 13271040 | bytes 8847360 | tf_op jit(solution)/shard_map/concatenate | solution.py:110
  124.9 37.0 %while.11 = (s32[]{:T(128)}, bf16[6,480,128]{2,1,0:T(8,128)(2,1)}, s32[6]{0:T(128)S(1)}, bf16[480,768]{1,0:T(8,128)(2,1)}, bf16[1440,768]{1,0:T(8,128)(2,1)S(1)}...) while((s32[]{:T(128)}, bf16[6,480,128]{2,1,0:T(8,128)(2,1)}, ...), condition=%wide.region_16.17_spmd.clone, body=%wide.region_13.16_spmd.clone.sunk | while | flops 361619520 | bytes 9311307 | solution.py:140
  126.2 2.0 %fusion.177 = (f32[480]{0:T(512)S(1)}, f32[480,1440]{1,0:T(8,128)S(1)}) fusion(bf16[1440,768]{1,0:T(8,128)(2,1)S(1)} %get-tuple-element.238, s32[]{:T(128)S(6)} %select_n.176, bf16[480,768]{1,0:T(8,128)(2,1)} %get-tuple-element.237, pred[1440]{0:T(1024)(128)(4,1)S(1)} %get-tuple-element.244, s32[480]{0:T(512)S(1)} %get-tuple-element.242, ...), kind=kOutput, calls=%fused_computation.167.clone.1 | convolution fusion | flops 181785120 | bytes 3281792 | tf_op jit(solution)/shard_map/while/body/eval_jaxpr/qd,kd->qk/dot_general | solution.py:127
  128.8 2.2 %fusion.179 = bf16[6,480,128]{2,1,0:T(8,128)(2,1)} fusion(bf16[6,480,128]{2,1,0:T(8,128)(2,1)} %get-tuple-element.220, s32[]{:T(128)} %get-tuple-element.219, f32[480,1440]{1,0:T(8,128)S(1)} %get-tuple-element.202, f32[480]{0:T(512)S(1)} %get-tuple-element.203, bf16[1440,768]{1,0:T(8,128)(2,1)} %get-tuple-element.239, s32[]{:T(128)S(6)} %select_n.176, ...), kind=kOutput, calls=%fused_computation.11.clone.1 | convolution fusion | flops 178452480 | bytes 3260676 | tf_op jit(solution)/shard_map/while/body/eval_jaxpr/dot_general | solution.py:135
  132.4 2.0 %fusion.177 = (f32[480]{0:T(512)S(1)}, f32[480,1440]{1,0:T(8,128)S(1)}) fusion(bf16[1440,768]{1,0:T(8,128)(2,1)S(1)} %get-tuple-element.238, s32[]{:T(128)S(6)} %select_n.176, bf16[480,768]{1,0:T(8,128)(2,1)} %get-tuple-element.237, pred[1440]{0:T(1024)(128)(4,1)S(1)} %get-tuple-element.244, s32[480]{0:T(512)S(1)} %get-tuple-element.242, ...), kind=kOutput, calls=%fused_computation.167.clone.1 | convolution fusion | flops 181785120 | bytes 3281792 | tf_op jit(solution)/shard_map/while/body/eval_jaxpr/qd,kd->qk/dot_general | solution.py:127
  134.9 2.2 %fusion.179 = bf16[6,480,128]{2,1,0:T(8,128)(2,1)} fusion(bf16[6,480,128]{2,1,0:T(8,128)(2,1)} %get-tuple-element.220, s32[]{:T(128)} %get-tuple-element.219, f32[480,1440]{1,0:T(8,128)S(1)} %get-tuple-element.202, f32[480]{0:T(512)S(1)} %get-tuple-element.203, bf16[1440,768]{1,0:T(8,128)(2,1)} %get-tuple-element.239, s32[]{:T(128)S(6)} %select_n.176, ...), kind=kOutput, calls=%fused_computation.11.clone.1 | convolution fusion | flops 178452480 | bytes 3260676 | tf_op jit(solution)/shard_map/while/body/eval_jaxpr/dot_general | solution.py:135
  138.5 2.0 %fusion.177 = (f32[480]{0:T(512)S(1)}, f32[480,1440]{1,0:T(8,128)S(1)}) fusion(bf16[1440,768]{1,0:T(8,128)(2,1)S(1)} %get-tuple-element.238, s32[]{:T(128)S(6)} %select_n.176, bf16[480,768]{1,0:T(8,128)(2,1)} %get-tuple-element.237, pred[1440]{0:T(1024)(128)(4,1)S(1)} %get-tuple-element.244, s32[480]{0:T(512)S(1)} %get-tuple-element.242, ...), kind=kOutput, calls=%fused_computation.167.clone.1 | convolution fusion | flops 181785120 | bytes 3281792 | tf_op jit(solution)/shard_map/while/body/eval_jaxpr/qd,kd->qk/dot_general | solution.py:127
  141.1 2.3 %fusion.179 = bf16[6,480,128]{2,1,0:T(8,128)(2,1)} fusion(bf16[6,480,128]{2,1,0:T(8,128)(2,1)} %get-tuple-element.220, s32[]{:T(128)} %get-tuple-element.219, f32[480,1440]{1,0:T(8,128)S(1)} %get-tuple-element.202, f32[480]{0:T(512)S(1)} %get-tuple-element.203, bf16[1440,768]{1,0:T(8,128)(2,1)} %get-tuple-element.239, s32[]{:T(128)S(6)} %select_n.176, ...), kind=kOutput, calls=%fused_computation.11.clone.1 | convolution fusion | flops 178452480 | bytes 3260676 | tf_op jit(solution)/shard_map/while/body/eval_jaxpr/dot_general | solution.py:135
  144.7 2.0 %fusion.177 = (f32[480]{0:T(512)S(1)}, f32[480,1440]{1,0:T(8,128)S(1)}) fusion(bf16[1440,768]{1,0:T(8,128)(2,1)S(1)} %get-tuple-element.238, s32[]{:T(128)S(6)} %select_n.176, bf16[480,768]{1,0:T(8,128)(2,1)} %get-tuple-element.237, pred[1440]{0:T(1024)(128)(4,1)S(1)} %get-tuple-element.244, s32[480]{0:T(512)S(1)} %get-tuple-element.242, ...), kind=kOutput, calls=%fused_computation.167.clone.1 | convolution fusion | flops 181785120 | bytes 3281792 | tf_op jit(solution)/shard_map/while/body/eval_jaxpr/qd,kd->qk/dot_general | solution.py:127
  147.3 2.2 %fusion.179 = bf16[6,480,128]{2,1,0:T(8,128)(2,1)} fusion(bf16[6,480,128]{2,1,0:T(8,128)(2,1)} %get-tuple-element.220, s32[]{:T(128)} %get-tuple-element.219, f32[480,1440]{1,0:T(8,128)S(1)} %get-tuple-element.202, f32[480]{0:T(512)S(1)} %get-tuple-element.203, bf16[1440,768]{1,0:T(8,128)(2,1)} %get-tuple-element.239, s32[]{:T(128)S(6)} %select_n.176, ...), kind=kOutput, calls=%fused_computation.11.clone.1 | convolution fusion | flops 178452480 | bytes 3260676 | tf_op jit(solution)/shard_map/while/body/eval_jaxpr/dot_general | solution.py:135
  150.9 2.0 %fusion.177 = (f32[480]{0:T(512)S(1)}, f32[480,1440]{1,0:T(8,128)S(1)}) fusion(bf16[1440,768]{1,0:T(8,128)(2,1)S(1)} %get-tuple-element.238, s32[]{:T(128)S(6)} %select_n.176, bf16[480,768]{1,0:T(8,128)(2,1)} %get-tuple-element.237, pred[1440]{0:T(1024)(128)(4,1)S(1)} %get-tuple-element.244, s32[480]{0:T(512)S(1)} %get-tuple-element.242, ...), kind=kOutput, calls=%fused_computation.167.clone.1 | convolution fusion | flops 181785120 | bytes 3281792 | tf_op jit(solution)/shard_map/while/body/eval_jaxpr/qd,kd->qk/dot_general | solution.py:127
  153.4 2.3 %fusion.179 = bf16[6,480,128]{2,1,0:T(8,128)(2,1)} fusion(bf16[6,480,128]{2,1,0:T(8,128)(2,1)} %get-tuple-element.220, s32[]{:T(128)} %get-tuple-element.219, f32[480,1440]{1,0:T(8,128)S(1)} %get-tuple-element.202, f32[480]{0:T(512)S(1)} %get-tuple-element.203, bf16[1440,768]{1,0:T(8,128)(2,1)} %get-tuple-element.239, s32[]{:T(128)S(6)} %select_n.176, ...), kind=kOutput, calls=%fused_computation.11.clone.1 | convolution fusion | flops 178452480 | bytes 3260676 | tf_op jit(solution)/shard_map/while/body/eval_jaxpr/dot_general | solution.py:135
  157.0 2.0 %fusion.177 = (f32[480]{0:T(512)S(1)}, f32[480,1440]{1,0:T(8,128)S(1)}) fusion(bf16[1440,768]{1,0:T(8,128)(2,1)S(1)} %get-tuple-element.238, s32[]{:T(128)S(6)} %select_n.176, bf16[480,768]{1,0:T(8,128)(2,1)} %get-tuple-element.237, pred[1440]{0:T(1024)(128)(4,1)S(1)} %get-tuple-element.244, s32[480]{0:T(512)S(1)} %get-tuple-element.242, ...), kind=kOutput, calls=%fused_computation.167.clone.1 | convolution fusion | flops 181785120 | bytes 3281792 | tf_op jit(solution)/shard_map/while/body/eval_jaxpr/qd,kd->qk/dot_general | solution.py:127
  159.6 2.2 %fusion.179 = bf16[6,480,128]{2,1,0:T(8,128)(2,1)} fusion(bf16[6,480,128]{2,1,0:T(8,128)(2,1)} %get-tuple-element.220, s32[]{:T(128)} %get-tuple-element.219, f32[480,1440]{1,0:T(8,128)S(1)} %get-tuple-element.202, f32[480]{0:T(512)S(1)} %get-tuple-element.203, bf16[1440,768]{1,0:T(8,128)(2,1)} %get-tuple-element.239, s32[]{:T(128)S(6)} %select_n.176, ...), kind=kOutput, calls=%fused_computation.11.clone.1 | convolution fusion | flops 178452480 | bytes 3260676 | tf_op jit(solution)/shard_map/while/body/eval_jaxpr/dot_general | solution.py:135
  162.6 6.2 %all-to-all-start.2 = ((f32[8,1,6]{2,1,0:T(1,128)}), f32[8,1,6]{2,1,0:T(1,128)S(1)}, u32[]{:S(2)}, u32[]{:S(2)}) async-start(f32[8,1,6]{2,1,0:T(1,128)} %broadcast_in_dim.57), calls=%async_computation.2 | async-start | bytes 8192 | tf_op jit(solution)/shard_map/all_to_all | solution.py:43
  171.3 2.0 %all-to-all-done.2 = f32[8,1,6]{2,1,0:T(1,128)S(1)} async-done(((f32[8,1,6]{2,1,0:T(1,128)}), f32[8,1,6]{2,1,0:T(1,128)S(1)}, u32[]{:S(2)}, u32[]{:S(2)}) %all-to-all-start.2) | async-done | bytes 224 | tf_op jit(solution)/shard_map/all_to_all | solution.py:43
  (100 shorter events, 45.3 us)
Async XLA Ops:
  3.9 15.0 %copy-start = (bf16[480,768]{1,0:T(8,128)(2,1)S(1)}, bf16[480,768]{1,0:T(8,128)(2,1)}, u32[]{:S(2)}) copy-start(bf16[480,768]{1,0:T(8,128)(2,1)} %param.9) | copy-start | bytes 2211844
  3.9 16.4 %copy-start.1 = (bf16[480,768]{1,0:T(8,128)(2,1)S(1)}, bf16[480,768]{1,0:T(8,128)(2,1)}, u32[]{:S(2)}) copy-start(bf16[480,768]{1,0:T(8,128)(2,1)} %param.10) | copy-start | bytes 2211844
  3.9 17.7 %copy-start.6 = (s32[480]{0:T(512)S(1)}, s32[480]{0:T(512)}, u32[]{:S(2)}) copy-start(s32[480]{0:T(512)} %param.11) | copy-start | bytes 5764
  3.9 68.7 %all-to-all-start = ((bf16[8,2,16,7168]{3,2,1,0:T(8,128)(2,1)}), bf16[8,2,16,7168]{3,2,1,0:T(8,128)(2,1)}, u32[]{:S(2)}, u32[]{:S(2)}) async-start(bf16[8,2,16,7168]{3,2,1,0:T(8,128)(2,1)} %broadcast_in_dim.53), calls=%async_computation | async-start | bytes 7340032 | tf_op jit(solution)/shard_map/all_to_all | solution.py:43
  18.9 33.1 %collective-permute-start = (bf16[480,768]{1,0:T(8,128)(2,1)S(1)}, bf16[480,768]{1,0:T(8,128)(2,1)S(1)}, u32[]{:S(2)}, u32[]{:S(2)}) collective-permute-start(bf16[480,768]{1,0:T(8,128)(2,1)S(1)} %copy-done), channel_id=1, source_target_pairs={{0,8},{8,16},{16,24},{24,32},{32,40},{40,48},{48,56},{56,64},{64,7... | collective-permute-start | bytes 2211848 | tf_op jit(solution)/shard_map/ppermute | solution.py:28
  20.3 31.8 %collective-permute-start.1 = (bf16[480,768]{1,0:T(8,128)(2,1)S(1)}, bf16[480,768]{1,0:T(8,128)(2,1)S(1)}, u32[]{:S(2)}, u32[]{:S(2)}) collective-permute-start(bf16[480,768]{1,0:T(8,128)(2,1)S(1)} %copy-done.1), channel_id=1, source_target_pairs={{0,8},{8,16},{16,24},{24,32},{32,40},{40,48},{48,56},{56,64},{64,7... | collective-permute-start | bytes 2211848 | tf_op jit(solution)/shard_map/ppermute | solution.py:28
  21.6 30.4 %collective-permute-start.2 = (s32[480]{0:T(512)S(1)}, s32[480]{0:T(512)S(1)}, u32[]{:S(2)}, u32[]{:S(2)}) collective-permute-start(s32[480]{0:T(512)S(1)} %copy-done.6), channel_id=1, source_target_pairs={{0,8},{8,16},{16,24},{24,32},{32,40},{40,48},{48,56},{56,64},{64,7... | collective-permute-start | bytes 5768 | tf_op jit(solution)/shard_map/ppermute | solution.py:28
  39.0 25.5 %copy-start.7 = (bf16[480,768]{1,0:T(8,128)(2,1)S(1)}, bf16[480,768]{1,0:T(8,128)(2,1)}, u32[]{:S(2)}) copy-start(bf16[480,768]{1,0:T(8,128)(2,1)} %param.8) | copy-start | bytes 2211844
  52.0 15.7 %copy-start.2 = (bf16[480,768]{1,0:T(8,128)(2,1)}, bf16[480,768]{1,0:T(8,128)(2,1)S(1)}, u32[]{:S(2)}) copy-start(bf16[480,768]{1,0:T(8,128)(2,1)S(1)} %collective-permute-done) | copy-start | bytes 2211844
  52.0 13.5 %copy-start.3 = (bf16[480,768]{1,0:T(8,128)(2,1)}, bf16[480,768]{1,0:T(8,128)(2,1)S(1)}, u32[]{:S(2)}) copy-start(bf16[480,768]{1,0:T(8,128)(2,1)S(1)} %collective-permute-done.1) | copy-start | bytes 2211844
  52.0 36.2 %collective-permute-start.3 = (bf16[480,768]{1,0:T(8,128)(2,1)S(1)}, bf16[480,768]{1,0:T(8,128)(2,1)}, u32[]{:S(2)}, u32[]{:S(2)}) collective-permute-start(bf16[480,768]{1,0:T(8,128)(2,1)S(1)} %collective-permute-done), channel_id=1, source_target_pairs={{0,8},{8,16},{16,24},{24,32},{32,40},{40,48},{48,56},{56,64},{64,7... | collective-permute-start | bytes 2211848 | tf_op jit(solution)/shard_map/ppermute | solution.py:28
  57.2 31.0 %collective-permute-start.4 = (bf16[480,768]{1,0:T(8,128)(2,1)S(1)}, bf16[480,768]{1,0:T(8,128)(2,1)}, u32[]{:S(2)}, u32[]{:S(2)}) collective-permute-start(bf16[480,768]{1,0:T(8,128)(2,1)S(1)} %collective-permute-done.1), channel_id=1, source_target_pairs={{0,8},{8,16},{16,24},{24,32},{32,40},{40,48},{48,56},{56,64},{64,7... | collective-permute-start | bytes 2211848 | tf_op jit(solution)/shard_map/ppermute | solution.py:28
  59.4 28.9 %collective-permute-start.5 = (s32[480]{0:T(512)S(1)}, s32[480]{0:T(512)S(1)}, u32[]{:S(2)}, u32[]{:S(2)}) collective-permute-start(s32[480]{0:T(512)S(1)} %collective-permute-done.2), channel_id=1, source_target_pairs={{0,8},{8,16},{16,24},{24,32},{32,40},{40,48},{48,56},{56,64},{64,7... | collective-permute-start | bytes 5768 | tf_op jit(solution)/shard_map/ppermute | solution.py:28
  83.8 4.4 %copy-start.8 = (bf16[480,768]{1,0:T(8,128)(2,1)S(1)}, bf16[480,768]{1,0:T(8,128)(2,1)}, u32[]{:S(2)}) copy-start(bf16[480,768]{1,0:T(8,128)(2,1)} %param.8) | copy-start | bytes 2211844
  104.7 57.2 %all-to-all-start.1 = ((f32[96,1,6]{2,1,0:T(1,128)}), f32[96,1,6]{2,1,0:T(1,128)S(1)}, u32[]{:S(2)}, u32[]{:S(2)}) async-start(f32[96,1,6]{2,1,0:T(1,128)} %broadcast_in_dim.56), calls=%async_computation.1 | async-start | bytes 98304 | tf_op jit(solution)/shard_map/all_to_all | solution.py:43
  161.9 11.7 %copy-start.4 = (bf16[2,128,896]{2,1,0:T(8,128)(2,1)S(1)}, bf16[2,128,896]{2,1,0:T(8,128)(2,1)}, u32[]{:S(2)}) copy-start(bf16[2,128,896]{2,1,0:T(8,128)(2,1)} %param.13) | copy-start | bytes 1376260
  161.9 11.7 %copy-start.5 = (bf16[2,128,896]{2,1,0:T(8,128)(2,1)S(1)}, bf16[2,128,896]{2,1,0:T(8,128)(2,1)}, u32[]{:S(2)}) copy-start(bf16[2,128,896]{2,1,0:T(8,128)(2,1)} %fusion.59) | copy-start | bytes 1376260
  162.6 10.7 %all-to-all-start.2 = ((f32[8,1,6]{2,1,0:T(1,128)}), f32[8,1,6]{2,1,0:T(1,128)S(1)}, u32[]{:S(2)}, u32[]{:S(2)}) async-start(f32[8,1,6]{2,1,0:T(1,128)} %broadcast_in_dim.57), calls=%async_computation.2 | async-start | bytes 8192 | tf_op jit(solution)/shard_map/all_to_all | solution.py:43

commit v4 on v3

--- a/solution.py
+++ b/solution.py
@@ -88,22 +88,20 @@
             & (place_blk[None, :] <= query_place[:, None])
             & (place_blk[None, :] >= 0)
         )
-        found = []
-        for head_slot in range(heads_here):
-            cols = slice(head_slot * HD, (head_slot + 1) * HD)
-            scores = jnp.einsum(
-                "qd,kd->qk", query_vectors[:, cols], keys_blk[:, cols],
-                preferred_element_type=jnp.float32,
-            ) / math.sqrt(HD)
-            found.append(jnp.max(jnp.where(allowed, scores, masked_fill)))
-        return jnp.stack(found)
+        scores = jnp.einsum(
+            "qhd,khd->hqk",
+            query_vectors.reshape(tokens_here, heads_here, HD),
+            keys_blk.reshape(tokens_here, heads_here, HD),
+            preferred_element_type=jnp.float32,
+        ) / math.sqrt(HD)
+        return jnp.max(jnp.where(allowed[None], scores, masked_fill), axis=(1, 2))
 
     first = shifted(local_block, "seq", 1)
     local_max = block_max(local_block, REACH)
-    first, local_max = lax.optimization_barrier((first, local_max))
+    first, local_max, update = lax.optimization_barrier((first, local_max, update))
     second = shifted(first, "seq", 1)
     first_max = block_max(first, REACH - 1)
-    second, first_max, update = lax.optimization_barrier((second, first_max, update))
+    second, first_max = lax.optimization_barrier((second, first_max))
     head_max = jnp.maximum(jnp.maximum(local_max, first_max), block_max(second, REACH - 2))
     earlier = [first, second]
     ordered = [earlier[REACH - 1 - position] for position in range(REACH)] + [local_block]

time: 176 us -> 182 us (1.034)
  waiting for transfers between devices: 15 us -> 61.6 us
  matrix products: 72.2 us -> 43.7 us
  local copies, waits for them, and re-layouts: 23.4 us -> 14.3 us
  starting transfers between devices: 50.6 us -> 46.4 us
    all_to_all x3, waiting for transfers between devices: 1.98 us -> 38.1 us  [gathered(): return lax.all_to_all(spread, axis, 0, 0, tiled=True)]
    dot_general x18 -> x3, matrix products: 31.7 us -> 6.13 us  [block_max(): jnp.einsum('qhd,khd->hqk', query_vectors.reshape(tokens_here, heads_here,...]
    another operation x3 -> x0, local copies, waits for them, and re-layouts: 11.6 us -> none  [block_max(): return jnp.stack(found)]
    ppermute x6, waiting for transfers between devices: 13.1 us -> 23.6 us  [shifted(): return lax.ppermute(shard, axis, pairs)]
    dot_general x6, matrix products: 13.5 us -> 9.89 us  [one_head(): jnp.dot(exp_scores.astype(jnp.bfloat16), value_cols, preferred_element_ty...]
    ppermute x6, starting transfers between devices: 12.6 us -> 9.72 us  [shifted(): return lax.ppermute(shard, axis, pairs)]
    optimization_barrier x0 -> x2, local copies, waits for them, and re-layouts: none -> 2.31 us  [the longest x1 1.16 us: shards(): second, first_max = lax.optimization_barrier((second, first_max))]
  transfers between devices with their start and end apart: 9 -> 9, of which waited for: 2 -> 3; matrix products, arithmetic and copies ran while one was open for 47% -> 32% of each run, Pallas kernels for 0% -> 0%
where the time goes in v4:
time: 182 us; the launch traced here: 181 us
  waiting for transfers between devices  61.6 us (34%)
  starting transfers between devices  46.4 us (25%)
  matrix products  43.7 us (24%)
  local copies, waits for them, and re-layouts  14.3 us (8%)
  other arithmetic  9.44 us (5%)
  loops' own time  4.05 us (2%)
    all_to_all x3, waiting for transfers between devices, gathered(): return lax.all_to_all(spread, axis, 0, 0, tiled=True)  38.1 us
    all_to_all x3, starting transfers between devices, gathered(): return lax.all_to_all(spread, axis, 0, 0, tiled=True)  36.7 us
    ppermute x6, waiting for transfers between devices, shifted(): return lax.ppermute(shard, axis, pairs)  23.6 us
    dot_general x6, matrix products, one_head(): jnp.einsum('qd,kd->qk', query_cols, key_cols, preferred_element_type=jnp....  13 us
    dot_general x6, matrix products, one_head(): jnp.dot(exp_scores.astype(jnp.bfloat16), value_cols, preferred_element_ty...  9.89 us
    ppermute x6, starting transfers between devices, shifted(): return lax.ppermute(shard, axis, pairs)  9.72 us
    dot_general x1, matrix products, shards(): jnp.einsum('jmrd,kmsd->mjrks', pieces, pieces, preferred_element_type=jnp...  6.89 us
    dot_general x3, matrix products, block_max(): jnp.einsum('qhd,khd->hqk', query_vectors.reshape(tokens_here, heads_here,...  6.13 us
  transfers between devices with their start and end apart: 9, of which 3 were waited for; matrix products, arithmetic and copies ran while one was open for 32% of the time, Pallas kernels for 0%

profile of v4, /device:TPU:1, one launch (start us, length us, event | category | flops | bytes accessed | tf_op | source)
XLA Modules:
  0.0 180.5 jit_solution(11705302671762779672)
XLA Ops:
  0.6 3.3 %broadcast_in_dim.57 = bf16[8,2,16,7168]{3,2,1,0:T(8,128)(2,1)} broadcast(bf16[2,16,7168]{2,1,0:T(8,128)(2,1)} %param.12), dimensions={1,2,3} | broadcast | bytes 4128768 | tf_op jit(solution)/shard_map/broadcast_in_dim | solution.py:42
  3.9 15.0 %all-to-all-start = ((bf16[8,2,16,7168]{3,2,1,0:T(8,128)(2,1)}), bf16[8,2,16,7168]{3,2,1,0:T(8,128)(2,1)}, u32[]{:S(2)}, u32[]{:S(2)}) async-start(bf16[8,2,16,7168]{3,2,1,0:T(8,128)(2,1)} %broadcast_in_dim.57), calls=%async_computation | async-start | bytes 7340032 | tf_op jit(solution)/shard_map/all_to_all | solution.py:43
  18.9 1.3 collective-permute-start
  20.3 2.2 %collective-permute-start.1 = (bf16[480,768]{1,0:T(8,128)(2,1)}, bf16[480,768]{1,0:T(8,128)(2,1)}, u32[]{:S(2)}, u32[]{:S(2)}) collective-permute-start(bf16[480,768]{1,0:T(8,128)(2,1)} %param.10), channel_id=1, source_target_pairs={{0,8},{8,16},{16,24},{24,32},{32,40},{40,48},{48,56},{56,64},{64,7... | collective-permute-start | bytes 2211848 | tf_op jit(solution)/shard_map/ppermute | solution.py:28
  24.0 1.4 copy.96
  26.0 1.3 select_reduce_fusion
  27.3 35.0 %all-to-all-done = bf16[8,2,16,7168]{3,2,1,0:T(8,128)(2,1)} async-done(((bf16[8,2,16,7168]{3,2,1,0:T(8,128)(2,1)}), bf16[8,2,16,7168]{3,2,1,0:T(8,128)(2,1)}, u32[]{:S(2)}, u32[]{:S(2)}) %all-to-all-start) | async-done | bytes 3670048 | tf_op jit(solution)/shard_map/all_to_all | solution.py:43
  62.2 6.9 %select_reduce_fusion.1 = (f32[2]{0:T(128)S(1)}, f32[2,8,16,8,16]{4,2,3,1,0:T(8,128)S(1)}) fusion(pred[8,16,8,16]{3,1,2,0:T(8,128)(4,1)S(1)} %broadcast_compare_fusion, bf16[8,2,16,7168]{3,2,1,0:T(8,128)(2,1)} %all-to-all-done), kind=kOutput, calls=%fused_computation.40 | convolution fusion | flops 469827584 | bytes 3817480 | tf_op jit(solution)/shard_map/jmrd,kmsd->mjrks/dot_general | solution.py:56
  74.9 2.8 %fusion.31 = bf16[2,128,896]{2,1,0:T(8,128)(2,1)} fusion(f32[2,128,8,16]{1,3,2,0:T(8,128)S(1)} %bitcast.86, f32[2]{0:T(128)S(1)} %get-tuple-element.127, bf16[8,2,16,7168]{3,2,1,0:T(8,128)(2,1)} %all-to-all-done, s32[]{:T(128)S(6)} %select_n.50), kind=kOutput, calls=%fused_computation.29 | convolution fusion | flops 353239040 | bytes 1048588 | tf_op jit(solution)/shard_map/mijr,jmrd->mid/dot_general | solution.py:72
  77.7 1.3 collective-permute-start.3
  79.0 2.2 %collective-permute-start.4 = (bf16[480,768]{1,0:T(8,128)(2,1)}, bf16[480,768]{1,0:T(8,128)(2,1)}, u32[]{:S(2)}, u32[]{:S(2)}) collective-permute-start(bf16[480,768]{1,0:T(8,128)(2,1)} %collective-permute-done.1), channel_id=1, source_target_pairs={{0,8},{8,16},{16,24},{24,32},{32,40},{40,48},{48,56},{56,64},{64,7... | collective-permute-start | bytes 2211848 | tf_op jit(solution)/shard_map/ppermute | solution.py:28
  82.4 1.5 collective-permute-start.5
  84.1 2.4 %fusion.26 = f32[6]{0:T(128)S(1)} fusion(pred[480,480]{1,0:T(8,128)(4,1)S(1)} %and_and_fusion.1, bf16[480,6,128]{0,2,1:T(8,128)(2,1)} %bitcast.83, bf16[480,6,128]{0,2,1:T(8,128)(2,1)S(1)} %bitcast.80), kind=kOutput, calls=%fused_computation.20 | convolution fusion | flops 358041600 | bytes 1704984 | tf_op jit(solution)/shard_map/qhd,khd->hqk/dot_general | solution.py:91
  86.5 23.6 %collective-permute-done.5 = s32[480]{0:T(512)S(1)} collective-permute-done((s32[480]{0:T(512)S(1)}, s32[480]{0:T(512)S(1)}, u32[]{:S(2)}, u32[]{:S(2)}) %collective-permute-start.5) | collective-permute-done | bytes 1952 | tf_op jit(solution)/shard_map/ppermute | solution.py:28
  111.6 2.4 %fusion.25 = f32[6]{0:T(128)S(1)} fusion(pred[480,480]{1,0:T(8,128)(4,1)S(1)} %and_and_fusion, bf16[480,6,128]{0,2,1:T(8,128)(2,1)} %bitcast.84, bf16[480,6,128]{0,2,1:T(8,128)(2,1)S(1)} %bitcast.81), kind=kOutput, calls=%fused_computation.18 | convolution fusion | flops 358041600 | bytes 1704984 | tf_op jit(solution)/shard_map/qhd,khd->hqk/dot_general | solution.py:91
  114.7 16.5 %all-to-all-start.1 = ((f32[96,1,6]{2,1,0:T(1,128)}), f32[96,1,6]{2,1,0:T(1,128)S(1)}, u32[]{:S(2)}, u32[]{:S(2)}) async-start(f32[96,1,6]{2,1,0:T(1,128)} %broadcast_in_dim.62), calls=%async_computation.1 | async-start | bytes 98304 | tf_op jit(solution)/shard_map/all_to_all | solution.py:43
  131.2 3.7 %pad_maximum_fusion = (bf16[1440,768]{1,0:T(8,128)(2,1)}, bf16[1440,768]{1,0:T(8,128)(2,1)}) fusion(bf16[480,768]{1,0:T(8,128)(2,1)S(1)} %copy-done, bf16[480,768]{1,0:T(8,128)(2,1)S(1)} %collective-permute-done, bf16[480,768]{1,0:T(8,128)(2,1)S(1)} %collective-permute-done.3, bf16[480,768]{1,0:T(8,128)(2,1)} %param.10, ...), kind=kLoop, calls=%fused_computation.25 | loop fusion | flops 13271040 | bytes 8847360 | tf_op jit(solution)/shard_map/concatenate | solution.py:108
  134.9 33.8 %while.11 = (s32[]{:T(128)}, bf16[6,480,128]{2,1,0:T(8,128)(2,1)S(1)}, s32[6]{0:T(128)S(1)}, bf16[480,768]{1,0:T(8,128)(2,1)}, bf16[1440,768]{1,0:T(8,128)(2,1)}...) while((s32[]{:T(128)}, ...), condition=%wide.region_6.7_spmd.clone, body=%wide.region_3.6_spmd.clone.sunk | while | flops 361619520 | bytes 9490155 | solution.py:138
  136.2 2.2 %fusion.101 = (f32[480]{0:T(512)S(1)}, f32[480,1440]{1,0:T(8,128)S(1)}) fusion(bf16[1440,768]{1,0:T(8,128)(2,1)} %get-tuple-element.238, s32[]{:T(128)S(6)} %select_n.69, bf16[480,768]{1,0:T(8,128)(2,1)} %get-tuple-element.237, pred[1440]{0:T(1024)(128)(4,1)S(1)} %get-tuple-element.244, s32[480]{0:T(512)S(1)} %get-tuple-element.242, ...), kind=kOutput, calls=%fused_computation.70.clone.1 | convolution fusion | flops 181785120 | bytes 3276064 | tf_op jit(solution)/shard_map/while/body/eval_jaxpr/qd,kd->qk/dot_general | solution.py:125
  138.9 1.7 fusion.103
  141.8 2.2 %fusion.101 = (f32[480]{0:T(512)S(1)}, f32[480,1440]{1,0:T(8,128)S(1)}) fusion(bf16[1440,768]{1,0:T(8,128)(2,1)} %get-tuple-element.238, s32[]{:T(128)S(6)} %select_n.69, bf16[480,768]{1,0:T(8,128)(2,1)} %get-tuple-element.237, pred[1440]{0:T(1024)(128)(4,1)S(1)} %get-tuple-element.244, s32[480]{0:T(512)S(1)} %get-tuple-element.242, ...), kind=kOutput, calls=%fused_computation.70.clone.1 | convolution fusion | flops 181785120 | bytes 3276064 | tf_op jit(solution)/shard_map/while/body/eval_jaxpr/qd,kd->qk/dot_general | solution.py:125
  144.5 1.6 fusion.103
  147.4 2.2 %fusion.101 = (f32[480]{0:T(512)S(1)}, f32[480,1440]{1,0:T(8,128)S(1)}) fusion(bf16[1440,768]{1,0:T(8,128)(2,1)} %get-tuple-element.238, s32[]{:T(128)S(6)} %select_n.69, bf16[480,768]{1,0:T(8,128)(2,1)} %get-tuple-element.237, pred[1440]{0:T(1024)(128)(4,1)S(1)} %get-tuple-element.244, s32[480]{0:T(512)S(1)} %get-tuple-element.242, ...), kind=kOutput, calls=%fused_computation.70.clone.1 | convolution fusion | flops 181785120 | bytes 3276064 | tf_op jit(solution)/shard_map/while/body/eval_jaxpr/qd,kd->qk/dot_general | solution.py:125
  150.2 1.6 fusion.103
  153.1 2.2 %fusion.101 = (f32[480]{0:T(512)S(1)}, f32[480,1440]{1,0:T(8,128)S(1)}) fusion(bf16[1440,768]{1,0:T(8,128)(2,1)} %get-tuple-element.238, s32[]{:T(128)S(6)} %select_n.69, bf16[480,768]{1,0:T(8,128)(2,1)} %get-tuple-element.237, pred[1440]{0:T(1024)(128)(4,1)S(1)} %get-tuple-element.244, s32[480]{0:T(512)S(1)} %get-tuple-element.242, ...), kind=kOutput, calls=%fused_computation.70.clone.1 | convolution fusion | flops 181785120 | bytes 3276064 | tf_op jit(solution)/shard_map/while/body/eval_jaxpr/qd,kd->qk/dot_general | solution.py:125
  155.8 1.7 fusion.103
  158.7 2.2 %fusion.101 = (f32[480]{0:T(512)S(1)}, f32[480,1440]{1,0:T(8,128)S(1)}) fusion(bf16[1440,768]{1,0:T(8,128)(2,1)} %get-tuple-element.238, s32[]{:T(128)S(6)} %select_n.69, bf16[480,768]{1,0:T(8,128)(2,1)} %get-tuple-element.237, pred[1440]{0:T(1024)(128)(4,1)S(1)} %get-tuple-element.244, s32[480]{0:T(512)S(1)} %get-tuple-element.242, ...), kind=kOutput, calls=%fused_computation.70.clone.1 | convolution fusion | flops 181785120 | bytes 3276064 | tf_op jit(solution)/shard_map/while/body/eval_jaxpr/qd,kd->qk/dot_general | solution.py:125
  161.4 1.6 fusion.103
  164.3 2.2 %fusion.101 = (f32[480]{0:T(512)S(1)}, f32[480,1440]{1,0:T(8,128)S(1)}) fusion(bf16[1440,768]{1,0:T(8,128)(2,1)} %get-tuple-element.238, s32[]{:T(128)S(6)} %select_n.69, bf16[480,768]{1,0:T(8,128)(2,1)} %get-tuple-element.237, pred[1440]{0:T(1024)(128)(4,1)S(1)} %get-tuple-element.244, s32[480]{0:T(512)S(1)} %get-tuple-element.242, ...), kind=kOutput, calls=%fused_computation.70.clone.1 | convolution fusion | flops 181785120 | bytes 3276064 | tf_op jit(solution)/shard_map/while/body/eval_jaxpr/qd,kd->qk/dot_general | solution.py:125
  167.1 1.6 fusion.103
  169.5 5.2 %all-to-all-start.2 = ((f32[8,1,6]{2,1,0:T(1,128)}), f32[8,1,6]{2,1,0:T(1,128)S(1)}, u32[]{:S(2)}, u32[]{:S(2)}) async-start(f32[8,1,6]{2,1,0:T(1,128)} %broadcast_in_dim.63), calls=%async_computation.2 | async-start | bytes 8192 | tf_op jit(solution)/shard_map/all_to_all | solution.py:43
  176.1 3.1 %all-to-all-done.2 = f32[8,1,6]{2,1,0:T(1,128)S(1)} async-done(((f32[8,1,6]{2,1,0:T(1,128)}), f32[8,1,6]{2,1,0:T(1,128)S(1)}, u32[]{:S(2)}, u32[]{:S(2)}) %all-to-all-start.2) | async-done | bytes 224 | tf_op jit(solution)/shard_map/all_to_all | solution.py:43
  (81 shorter events, 21.6 us)
Async XLA Ops:
  3.9 15.0 %copy-start = (bf16[480,768]{1,0:T(8,128)(2,1)S(1)}, bf16[480,768]{1,0:T(8,128)(2,1)}, u32[]{:S(2)}) copy-start(bf16[480,768]{1,0:T(8,128)(2,1)} %param.9) | copy-start | bytes 2211844
  3.9 18.5 %copy-start.4 = (s32[480]{0:T(512)S(1)}, s32[480]{0:T(512)}, u32[]{:S(2)}) copy-start(s32[480]{0:T(512)} %param.11) | copy-start | bytes 5764
  3.9 58.3 %all-to-all-start = ((bf16[8,2,16,7168]{3,2,1,0:T(8,128)(2,1)}), bf16[8,2,16,7168]{3,2,1,0:T(8,128)(2,1)}, u32[]{:S(2)}, u32[]{:S(2)}) async-start(bf16[8,2,16,7168]{3,2,1,0:T(8,128)(2,1)} %broadcast_in_dim.57), calls=%async_computation | async-start | bytes 7340032 | tf_op jit(solution)/shard_map/all_to_all | solution.py:43
  18.9 58.7 %collective-permute-start = (bf16[480,768]{1,0:T(8,128)(2,1)S(1)}, bf16[480,768]{1,0:T(8,128)(2,1)S(1)}, u32[]{:S(2)}, u32[]{:S(2)}) collective-permute-start(bf16[480,768]{1,0:T(8,128)(2,1)S(1)} %copy-done), channel_id=1, source_target_pairs={{0,8},{8,16},{16,24},{24,32},{32,40},{40,48},{48,56},{56,64},{64,7... | collective-permute-start | bytes 2211848 | tf_op jit(solution)/shard_map/ppermute | solution.py:28
  20.3 57.4 %collective-permute-start.1 = (bf16[480,768]{1,0:T(8,128)(2,1)}, bf16[480,768]{1,0:T(8,128)(2,1)}, u32[]{:S(2)}, u32[]{:S(2)}) collective-permute-start(bf16[480,768]{1,0:T(8,128)(2,1)} %param.10), channel_id=1, source_target_pairs={{0,8},{8,16},{16,24},{24,32},{32,40},{40,48},{48,56},{56,64},{64,7... | collective-permute-start | bytes 2211848 | tf_op jit(solution)/shard_map/ppermute | solution.py:28
  22.4 55.2 %collective-permute-start.2 = (s32[480]{0:T(512)S(1)}, s32[480]{0:T(512)S(1)}, u32[]{:S(2)}, u32[]{:S(2)}) collective-permute-start(s32[480]{0:T(512)S(1)} %copy-done.4), channel_id=1, source_target_pairs={{0,8},{8,16},{16,24},{24,32},{32,40},{40,48},{48,56},{56,64},{64,7... | collective-permute-start | bytes 5768 | tf_op jit(solution)/shard_map/ppermute | solution.py:28
  77.7 32.4 %collective-permute-start.3 = (bf16[480,768]{1,0:T(8,128)(2,1)S(1)}, bf16[480,768]{1,0:T(8,128)(2,1)S(1)}, u32[]{:S(2)}, u32[]{:S(2)}) collective-permute-start(bf16[480,768]{1,0:T(8,128)(2,1)S(1)} %collective-permute-done), channel_id=1, source_target_pairs={{0,8},{8,16},{16,24},{24,32},{32,40},{40,48},{48,56},{56,64},{64,7... | collective-permute-start | bytes 2211848 | tf_op jit(solution)/shard_map/ppermute | solution.py:28
  79.0 31.1 %collective-permute-start.4 = (bf16[480,768]{1,0:T(8,128)(2,1)}, bf16[480,768]{1,0:T(8,128)(2,1)}, u32[]{:S(2)}, u32[]{:S(2)}) collective-permute-start(bf16[480,768]{1,0:T(8,128)(2,1)} %collective-permute-done.1), channel_id=1, source_target_pairs={{0,8},{8,16},{16,24},{24,32},{32,40},{40,48},{48,56},{56,64},{64,7... | collective-permute-start | bytes 2211848 | tf_op jit(solution)/shard_map/ppermute | solution.py:28
  82.4 27.7 %collective-permute-start.5 = (s32[480]{0:T(512)S(1)}, s32[480]{0:T(512)S(1)}, u32[]{:S(2)}, u32[]{:S(2)}) collective-permute-start(s32[480]{0:T(512)S(1)} %collective-permute-done.2), channel_id=1, source_target_pairs={{0,8},{8,16},{16,24},{24,32},{32,40},{40,48},{48,56},{56,64},{64,7... | collective-permute-start | bytes 5768 | tf_op jit(solution)/shard_map/ppermute | solution.py:28
  114.7 54.0 %all-to-all-start.1 = ((f32[96,1,6]{2,1,0:T(1,128)}), f32[96,1,6]{2,1,0:T(1,128)S(1)}, u32[]{:S(2)}, u32[]{:S(2)}) async-start(f32[96,1,6]{2,1,0:T(1,128)} %broadcast_in_dim.62), calls=%async_computation.1 | async-start | bytes 98304 | tf_op jit(solution)/shard_map/all_to_all | solution.py:43
  131.2 3.7 %copy-start.1 = (bf16[6,480,128]{2,1,0:T(8,128)(2,1)S(1)}, bf16[6,480,128]{2,1,0:T(8,128)(2,1)}, u32[]{:S(2)}) copy-start(bf16[6,480,128]{2,1,0:T(8,128)(2,1)} %custom-call) | copy-start | bytes 2211844
  134.9 44.7 %copy-start.2 = (bf16[2,128,896]{2,1,0:T(8,128)(2,1)S(1)}, bf16[2,128,896]{2,1,0:T(8,128)(2,1)}, u32[]{:S(2)}) copy-start(bf16[2,128,896]{2,1,0:T(8,128)(2,1)} %param.13) | copy-start | bytes 1376260
  134.9 44.7 %copy-start.3 = (bf16[2,128,896]{2,1,0:T(8,128)(2,1)S(1)}, bf16[2,128,896]{2,1,0:T(8,128)(2,1)}, u32[]{:S(2)}) copy-start(bf16[2,128,896]{2,1,0:T(8,128)(2,1)} %fusion.31) | copy-start | bytes 1376260
  169.5 9.8 %all-to-all-start.2 = ((f32[8,1,6]{2,1,0:T(1,128)}), f32[8,1,6]{2,1,0:T(1,128)S(1)}, u32[]{:S(2)}, u32[]{:S(2)}) async-start(f32[8,1,6]{2,1,0:T(1,128)} %broadcast_in_dim.63), calls=%async_computation.2 | async-start | bytes 8192 | tf_op jit(solution)/shard_map/all_to_all | solution.py:43

commit v5 on v4

--- a/solution.py
+++ b/solution.py
@@ -98,10 +98,10 @@
 
     first = shifted(local_block, "seq", 1)
     local_max = block_max(local_block, REACH)
-    first, local_max, update = lax.optimization_barrier((first, local_max, update))
+    first, local_max = lax.optimization_barrier((first, local_max))
     second = shifted(first, "seq", 1)
     first_max = block_max(first, REACH - 1)
-    second, first_max = lax.optimization_barrier((second, first_max))
+    second, first_max, update = lax.optimization_barrier((second, first_max, update))
     head_max = jnp.maximum(jnp.maximum(local_max, first_max), block_max(second, REACH - 2))
     earlier = [first, second]
     ordered = [earlier[REACH - 1 - position] for position in range(REACH)] + [local_block]

time: 182 us -> 163 us (0.90)
  waiting for transfers between devices: 61.6 us -> 31.8 us
  starting transfers between devices: 46.4 us -> 52.8 us
  other arithmetic: 9.44 us -> 11.7 us
    all_to_all x3, waiting for transfers between devices: 38.1 us -> 3.09 us  [gathered(): return lax.all_to_all(spread, axis, 0, 0, tiled=True)]
    ppermute x6, waiting for transfers between devices: 23.6 us -> 28.8 us  [shifted(): return lax.ppermute(shard, axis, pairs)]
    ppermute x6, starting transfers between devices: 9.72 us -> 13.7 us  [shifted(): return lax.ppermute(shard, axis, pairs)]
    all_to_all x3, starting transfers between devices: 36.7 us -> 39.1 us  [gathered(): return lax.all_to_all(spread, axis, 0, 0, tiled=True)]
    dot_general x3, matrix products: 6.13 us -> 8.32 us  [block_max(): jnp.einsum('qhd,khd->hqk', query_vectors.reshape(tokens_here, heads_here,...]
    unnamed x13 -> x27, local copies, waits for them, and re-layouts: 2.83 us -> 3.82 us
  transfers between devices with their start and end apart: 9 -> 9, of which waited for: 3 -> 3; matrix products, arithmetic and copies ran while one was open for 32% -> 38% of each run, Pallas kernels for 0% -> 0%
where the time goes in v5:
time: 163 us; the launch traced here: 162 us
  starting transfers between devices  52.8 us (32%)
  matrix products  45.1 us (28%)
  waiting for transfers between devices  31.8 us (20%)
  local copies, waits for them, and re-layouts  15.4 us (9%)
  other arithmetic  11.7 us (7%)
  loops' own time  4.05 us (2%)
    all_to_all x3, starting transfers between devices, gathered(): return lax.all_to_all(spread, axis, 0, 0, tiled=True)  39.1 us
    ppermute x6, waiting for transfers between devices, shifted(): return lax.ppermute(shard, axis, pairs)  28.8 us
    ppermute x6, starting transfers between devices, shifted(): return lax.ppermute(shard, axis, pairs)  13.7 us
    dot_general x6, matrix products, one_head(): jnp.einsum('qd,kd->qk', query_cols, key_cols, preferred_element_type=jnp....  13.1 us
    dot_general x6, matrix products, one_head(): jnp.dot(exp_scores.astype(jnp.bfloat16), value_cols, preferred_element_ty...  9.9 us
    dot_general x3, matrix products, block_max(): jnp.einsum('qhd,khd->hqk', query_vectors.reshape(tokens_here, heads_here,...  8.32 us
    dot_general x1, matrix products, shards(): jnp.einsum('jmrd,kmsd->mjrks', pieces, pieces, preferred_element_type=jnp...  6.89 us
    broadcast_in_dim x3, local copies, waits for them, and re-layouts, gathered(): spread = jnp.broadcast_to(values[None], (size,) + values.shape)  4.52 us
  transfers between devices with their start and end apart: 9, of which 3 were waited for; matrix products, arithmetic and copies ran while one was open for 38% of the time, Pallas kernels for 0%

profile of v5, /device:TPU:1, one launch (start us, length us, event | category | flops | bytes accessed | tf_op | source)
XLA Modules:
  0.0 162.0 jit_solution(4924492265991816548)
XLA Ops:
  0.6 3.3 %broadcast_in_dim.58 = bf16[8,2,16,7168]{3,2,1,0:T(8,128)(2,1)} broadcast(bf16[2,16,7168]{2,1,0:T(8,128)(2,1)} %param.12), dimensions={1,2,3} | broadcast | bytes 4128768 | tf_op jit(solution)/shard_map/broadcast_in_dim | solution.py:42
  3.9 15.0 %all-to-all-start = ((bf16[8,2,16,7168]{3,2,1,0:T(8,128)(2,1)}), bf16[8,2,16,7168]{3,2,1,0:T(8,128)(2,1)}, u32[]{:S(2)}, u32[]{:S(2)}) async-start(bf16[8,2,16,7168]{3,2,1,0:T(8,128)(2,1)} %broadcast_in_dim.58), calls=%async_computation | async-start | bytes 7340032 | tf_op jit(solution)/shard_map/all_to_all | solution.py:43
  18.9 1.3 collective-permute-start
  20.3 2.2 %collective-permute-start.1 = (bf16[480,768]{1,0:T(8,128)(2,1)S(1)}, bf16[480,768]{1,0:T(8,128)(2,1)}, u32[]{:S(2)}, u32[]{:S(2)}) collective-permute-start(bf16[480,768]{1,0:T(8,128)(2,1)S(1)} %copy-done.3), channel_id=1, source_target_pairs={{0,8},{8,16},{16,24},{24,32},{32,40},{40,48},{48,56},{56,64},{64,7... | collective-permute-start | bytes 2211848 | tf_op jit(solution)/shard_map/ppermute | solution.py:28
  25.9 1.4 copy.96
  27.6 3.0 %select_reduce_fusion = f32[6]{0:T(128)} fusion(pred[480,480]{1,0:T(8,128)(4,1)S(1)} %and_and_fusion.2, bf16[480,6,128]{0,2,1:T(8,128)(2,1)S(1)} %bitcast.79, bf16[480,6,128]{0,2,1:T(8,128)(2,1)} %bitcast.84), kind=kOutput, calls=%fused_computation.21 | convolution fusion | flops 358041600 | bytes 1704984 | tf_op jit(solution)/shard_map/qhd,khd->hqk/dot_general | solution.py:91
  31.1 20.9 %collective-permute-done.2 = s32[480]{0:T(512)S(1)} collective-permute-done((s32[480]{0:T(512)S(1)}, s32[480]{0:T(512)S(1)}, u32[]{:S(2)}, u32[]{:S(2)}) %collective-permute-start.2) | collective-permute-done | bytes 1952 | tf_op jit(solution)/shard_map/ppermute | solution.py:28
  53.3 4.2 %collective-permute-start.3 = (bf16[480,768]{1,0:T(8,128)(2,1)S(1)}, bf16[480,768]{1,0:T(8,128)(2,1)S(1)}, u32[]{:S(2)}, u32[]{:S(2)}) collective-permute-start(bf16[480,768]{1,0:T(8,128)(2,1)S(1)} %collective-permute-done), channel_id=1, source_target_pairs={{0,8},{8,16},{16,24},{24,32},{32,40},{40,48},{48,56},{56,64},{64,7... | collective-permute-start | bytes 2211848 | tf_op jit(solution)/shard_map/ppermute | solution.py:28
  57.5 1.9 %collective-permute-start.5 = (s32[480]{0:T(512)S(1)}, s32[480]{0:T(512)S(1)}, u32[]{:S(2)}, u32[]{:S(2)}) collective-permute-start(s32[480]{0:T(512)S(1)} %collective-permute-done.2), channel_id=1, source_target_pairs={{0,8},{8,16},{16,24},{24,32},{32,40},{40,48},{48,56},{56,64},{64,7... | collective-permute-start | bytes 5768 | tf_op jit(solution)/shard_map/ppermute | solution.py:28
  59.4 2.8 %collective-permute-start.4 = (bf16[480,768]{1,0:T(8,128)(2,1)}, bf16[480,768]{1,0:T(8,128)(2,1)}, u32[]{:S(2)}, u32[]{:S(2)}) collective-permute-start(bf16[480,768]{1,0:T(8,128)(2,1)} %collective-permute-done.1), channel_id=1, source_target_pairs={{0,8},{8,16},{16,24},{24,32},{32,40},{40,48},{48,56},{56,64},{64,7... | collective-permute-start | bytes 2211848 | tf_op jit(solution)/shard_map/ppermute | solution.py:28
  62.5 2.9 %fusion.26 = f32[6]{0:T(128)} fusion(pred[480,480]{1,0:T(8,128)(4,1)S(1)} %and_and_fusion.1, bf16[480,6,128]{0,2,1:T(8,128)(2,1)} %bitcast.82, bf16[480,6,128]{0,2,1:T(8,128)(2,1)S(1)} %bitcast.80), kind=kOutput, calls=%fused_computation.20 | convolution fusion | flops 358041600 | bytes 1704984 | tf_op jit(solution)/shard_map/qhd,khd->hqk/dot_general | solution.py:91
  65.4 6.9 %select_reduce_fusion.1 = (f32[2]{0:T(128)S(1)}, f32[2,8,16,8,16]{4,2,3,1,0:T(8,128)S(1)}) fusion(pred[8,16,8,16]{3,1,2,0:T(8,128)(4,1)S(1)} %broadcast_compare_fusion, bf16[8,2,16,7168]{3,2,1,0:T(8,128)(2,1)} %all-to-all-done), kind=kOutput, calls=%fused_computation.40 | convolution fusion | flops 469827584 | bytes 3817480 | tf_op jit(solution)/shard_map/jmrd,kmsd->mjrks/dot_general | solution.py:56
  78.6 2.0 %fusion.31 = bf16[2,128,896]{2,1,0:T(8,128)(2,1)S(1)} fusion(f32[2,128,8,16]{1,3,2,0:T(8,128)S(1)} %bitcast.86, f32[2]{0:T(128)S(1)} %copy-done.11, bf16[8,2,16,7168]{3,2,1,0:T(8,128)(2,1)} %all-to-all-done, s32[]{:T(128)S(6)} %select_n.51), kind=kOutput, calls=%fused_computation.29 | convolution fusion | flops 353239040 | bytes 1048588 | tf_op jit(solution)/shard_map/mijr,jmrd->mid/dot_general | solution.py:72
  80.7 7.9 %collective-permute-done.4 = bf16[480,768]{1,0:T(8,128)(2,1)} collective-permute-done((bf16[480,768]{1,0:T(8,128)(2,1)}, bf16[480,768]{1,0:T(8,128)(2,1)}, u32[]{:S(2)}, u32[]{:S(2)}) %collective-permute-start.4) | collective-permute-done | bytes 737312 | tf_op jit(solution)/shard_map/ppermute | solution.py:28
  90.8 2.4 %fusion.25 = f32[6]{0:T(128)S(1)} fusion(pred[480,480]{1,0:T(8,128)(4,1)S(1)} %and_and_fusion, bf16[480,6,128]{0,2,1:T(8,128)(2,1)} %bitcast.83, bf16[480,6,128]{0,2,1:T(8,128)(2,1)S(1)} %bitcast.81), kind=kOutput, calls=%fused_computation.18 | convolution fusion | flops 358041600 | bytes 1704984 | tf_op jit(solution)/shard_map/qhd,khd->hqk/dot_general | solution.py:91
  93.8 17.7 %all-to-all-start.1 = ((f32[96,1,6]{2,1,0:T(1,128)}), f32[96,1,6]{2,1,0:T(1,128)S(1)}, u32[]{:S(2)}, u32[]{:S(2)}) async-start(f32[96,1,6]{2,1,0:T(1,128)} %broadcast_in_dim.62), calls=%async_computation.1 | async-start | bytes 98304 | tf_op jit(solution)/shard_map/all_to_all | solution.py:43
  111.5 3.6 %pad_maximum_fusion = (bf16[1440,768]{1,0:T(8,128)(2,1)}, bf16[1440,768]{1,0:T(8,128)(2,1)}) fusion(bf16[480,768]{1,0:T(8,128)(2,1)S(1)} %copy-done, bf16[480,768]{1,0:T(8,128)(2,1)S(1)} %collective-permute-done, bf16[480,768]{1,0:T(8,128)(2,1)S(1)} %collective-permute-done.3, bf16[480,768]{1,0:T(8,128)(2,1)} %param.10, ...), kind=kLoop, calls=%fused_computation.25 | loop fusion | flops 13271040 | bytes 8847360 | tf_op jit(solution)/shard_map/concatenate | solution.py:108
  115.2 33.9 %while.11 = (s32[]{:T(128)}, bf16[6,480,128]{2,1,0:T(8,128)(2,1)S(1)}, s32[6]{0:T(128)S(1)}, bf16[480,768]{1,0:T(8,128)(2,1)}, bf16[1440,768]{1,0:T(8,128)(2,1)}...) while((s32[]{:T(128)}, ...), condition=%wide.region_6.7_spmd.clone, body=%wide.region_3.6_spmd.clone.sunk | while | flops 361619520 | bytes 9490155 | solution.py:138
  116.4 2.2 %fusion.101 = (f32[480]{0:T(512)S(1)}, f32[480,1440]{1,0:T(8,128)S(1)}) fusion(bf16[1440,768]{1,0:T(8,128)(2,1)} %get-tuple-element.238, s32[]{:T(128)S(6)} %select_n.69, bf16[480,768]{1,0:T(8,128)(2,1)} %get-tuple-element.237, pred[1440]{0:T(1024)(128)(4,1)S(1)} %get-tuple-element.244, s32[480]{0:T(512)S(1)} %get-tuple-element.242, ...), kind=kOutput, calls=%fused_computation.70.clone.1 | convolution fusion | flops 181785120 | bytes 3276064 | tf_op jit(solution)/shard_map/while/body/eval_jaxpr/qd,kd->qk/dot_general | solution.py:125
  119.2 1.6 %fusion.103 = bf16[6,480,128]{2,1,0:T(8,128)(2,1)S(1)} fusion(bf16[6,480,128]{2,1,0:T(8,128)(2,1)S(1)} %get-tuple-element.220, s32[]{:T(128)} %get-tuple-element.219, f32[480,1440]{1,0:T(8,128)S(1)} %get-tuple-element.202, f32[480]{0:T(512)S(1)} %get-tuple-element.203, bf16[1440,768]{1,0:T(8,128)(2,1)} %get-tuple-element.239, s32[]{:T(128)S(6)} %select_n.69, ...), kind=kOutput, calls=%fused_computation.11.clone.1 | convolution fusion | flops 178452480 | bytes 3445252 | tf_op jit(solution)/shard_map/while/body/eval_jaxpr/dot_general | solution.py:133
  122.1 2.2 %fusion.101 = (f32[480]{0:T(512)S(1)}, f32[480,1440]{1,0:T(8,128)S(1)}) fusion(bf16[1440,768]{1,0:T(8,128)(2,1)} %get-tuple-element.238, s32[]{:T(128)S(6)} %select_n.69, bf16[480,768]{1,0:T(8,128)(2,1)} %get-tuple-element.237, pred[1440]{0:T(1024)(128)(4,1)S(1)} %get-tuple-element.244, s32[480]{0:T(512)S(1)} %get-tuple-element.242, ...), kind=kOutput, calls=%fused_computation.70.clone.1 | convolution fusion | flops 181785120 | bytes 3276064 | tf_op jit(solution)/shard_map/while/body/eval_jaxpr/qd,kd->qk/dot_general | solution.py:125
  124.8 1.7 %fusion.103 = bf16[6,480,128]{2,1,0:T(8,128)(2,1)S(1)} fusion(bf16[6,480,128]{2,1,0:T(8,128)(2,1)S(1)} %get-tuple-element.220, s32[]{:T(128)} %get-tuple-element.219, f32[480,1440]{1,0:T(8,128)S(1)} %get-tuple-element.202, f32[480]{0:T(512)S(1)} %get-tuple-element.203, bf16[1440,768]{1,0:T(8,128)(2,1)} %get-tuple-element.239, s32[]{:T(128)S(6)} %select_n.69, ...), kind=kOutput, calls=%fused_computation.11.clone.1 | convolution fusion | flops 178452480 | bytes 3445252 | tf_op jit(solution)/shard_map/while/body/eval_jaxpr/dot_general | solution.py:133
  127.7 2.2 %fusion.101 = (f32[480]{0:T(512)S(1)}, f32[480,1440]{1,0:T(8,128)S(1)}) fusion(bf16[1440,768]{1,0:T(8,128)(2,1)} %get-tuple-element.238, s32[]{:T(128)S(6)} %select_n.69, bf16[480,768]{1,0:T(8,128)(2,1)} %get-tuple-element.237, pred[1440]{0:T(1024)(128)(4,1)S(1)} %get-tuple-element.244, s32[480]{0:T(512)S(1)} %get-tuple-element.242, ...), kind=kOutput, calls=%fused_computation.70.clone.1 | convolution fusion | flops 181785120 | bytes 3276064 | tf_op jit(solution)/shard_map/while/body/eval_jaxpr/qd,kd->qk/dot_general | solution.py:125
  130.5 1.7 %fusion.103 = bf16[6,480,128]{2,1,0:T(8,128)(2,1)S(1)} fusion(bf16[6,480,128]{2,1,0:T(8,128)(2,1)S(1)} %get-tuple-element.220, s32[]{:T(128)} %get-tuple-element.219, f32[480,1440]{1,0:T(8,128)S(1)} %get-tuple-element.202, f32[480]{0:T(512)S(1)} %get-tuple-element.203, bf16[1440,768]{1,0:T(8,128)(2,1)} %get-tuple-element.239, s32[]{:T(128)S(6)} %select_n.69, ...), kind=kOutput, calls=%fused_computation.11.clone.1 | convolution fusion | flops 178452480 | bytes 3445252 | tf_op jit(solution)/shard_map/while/body/eval_jaxpr/dot_general | solution.py:133
  133.4 2.2 %fusion.101 = (f32[480]{0:T(512)S(1)}, f32[480,1440]{1,0:T(8,128)S(1)}) fusion(bf16[1440,768]{1,0:T(8,128)(2,1)} %get-tuple-element.238, s32[]{:T(128)S(6)} %select_n.69, bf16[480,768]{1,0:T(8,128)(2,1)} %get-tuple-element.237, pred[1440]{0:T(1024)(128)(4,1)S(1)} %get-tuple-element.244, s32[480]{0:T(512)S(1)} %get-tuple-element.242, ...), kind=kOutput, calls=%fused_computation.70.clone.1 | convolution fusion | flops 181785120 | bytes 3276064 | tf_op jit(solution)/shard_map/while/body/eval_jaxpr/qd,kd->qk/dot_general | solution.py:125
  136.1 1.6 %fusion.103 = bf16[6,480,128]{2,1,0:T(8,128)(2,1)S(1)} fusion(bf16[6,480,128]{2,1,0:T(8,128)(2,1)S(1)} %get-tuple-element.220, s32[]{:T(128)} %get-tuple-element.219, f32[480,1440]{1,0:T(8,128)S(1)} %get-tuple-element.202, f32[480]{0:T(512)S(1)} %get-tuple-element.203, bf16[1440,768]{1,0:T(8,128)(2,1)} %get-tuple-element.239, s32[]{:T(128)S(6)} %select_n.69, ...), kind=kOutput, calls=%fused_computation.11.clone.1 | convolution fusion | flops 178452480 | bytes 3445252 | tf_op jit(solution)/shard_map/while/body/eval_jaxpr/dot_general | solution.py:133
  139.0 2.2 %fusion.101 = (f32[480]{0:T(512)S(1)}, f32[480,1440]{1,0:T(8,128)S(1)}) fusion(bf16[1440,768]{1,0:T(8,128)(2,1)} %get-tuple-element.238, s32[]{:T(128)S(6)} %select_n.69, bf16[480,768]{1,0:T(8,128)(2,1)} %get-tuple-element.237, pred[1440]{0:T(1024)(128)(4,1)S(1)} %get-tuple-element.244, s32[480]{0:T(512)S(1)} %get-tuple-element.242, ...), kind=kOutput, calls=%fused_computation.70.clone.1 | convolution fusion | flops 181785120 | bytes 3276064 | tf_op jit(solution)/shard_map/while/body/eval_jaxpr/qd,kd->qk/dot_general | solution.py:125
  141.7 1.7 %fusion.103 = bf16[6,480,128]{2,1,0:T(8,128)(2,1)S(1)} fusion(bf16[6,480,128]{2,1,0:T(8,128)(2,1)S(1)} %get-tuple-element.220, s32[]{:T(128)} %get-tuple-element.219, f32[480,1440]{1,0:T(8,128)S(1)} %get-tuple-element.202, f32[480]{0:T(512)S(1)} %get-tuple-element.203, bf16[1440,768]{1,0:T(8,128)(2,1)} %get-tuple-element.239, s32[]{:T(128)S(6)} %select_n.69, ...), kind=kOutput, calls=%fused_computation.11.clone.1 | convolution fusion | flops 178452480 | bytes 3445252 | tf_op jit(solution)/shard_map/while/body/eval_jaxpr/dot_general | solution.py:133
  144.6 2.2 %fusion.101 = (f32[480]{0:T(512)S(1)}, f32[480,1440]{1,0:T(8,128)S(1)}) fusion(bf16[1440,768]{1,0:T(8,128)(2,1)} %get-tuple-element.238, s32[]{:T(128)S(6)} %select_n.69, bf16[480,768]{1,0:T(8,128)(2,1)} %get-tuple-element.237, pred[1440]{0:T(1024)(128)(4,1)S(1)} %get-tuple-element.244, s32[480]{0:T(512)S(1)} %get-tuple-element.242, ...), kind=kOutput, calls=%fused_computation.70.clone.1 | convolution fusion | flops 181785120 | bytes 3276064 | tf_op jit(solution)/shard_map/while/body/eval_jaxpr/qd,kd->qk/dot_general | solution.py:125
  147.4 1.7 %fusion.103 = bf16[6,480,128]{2,1,0:T(8,128)(2,1)S(1)} fusion(bf16[6,480,128]{2,1,0:T(8,128)(2,1)S(1)} %get-tuple-element.220, s32[]{:T(128)} %get-tuple-element.219, f32[480,1440]{1,0:T(8,128)S(1)} %get-tuple-element.202, f32[480]{0:T(512)S(1)} %get-tuple-element.203, bf16[1440,768]{1,0:T(8,128)(2,1)} %get-tuple-element.239, s32[]{:T(128)S(6)} %select_n.69, ...), kind=kOutput, calls=%fused_computation.11.clone.1 | convolution fusion | flops 178452480 | bytes 3445252 | tf_op jit(solution)/shard_map/while/body/eval_jaxpr/dot_general | solution.py:133
  149.8 6.4 %all-to-all-start.2 = ((f32[8,1,6]{2,1,0:T(1,128)}), f32[8,1,6]{2,1,0:T(1,128)S(1)}, u32[]{:S(2)}, u32[]{:S(2)}) async-start(f32[8,1,6]{2,1,0:T(1,128)} %broadcast_in_dim.63), calls=%async_computation.2 | async-start | bytes 8192 | tf_op jit(solution)/shard_map/all_to_all | solution.py:43
  157.6 3.1 %all-to-all-done.2 = f32[8,1,6]{2,1,0:T(1,128)S(1)} async-done(((f32[8,1,6]{2,1,0:T(1,128)}), f32[8,1,6]{2,1,0:T(1,128)S(1)}, u32[]{:S(2)}, u32[]{:S(2)}) %all-to-all-start.2) | async-done | bytes 224 | tf_op jit(solution)/shard_map/all_to_all | solution.py:43
  (95 shorter events, 24.9 us)
Async XLA Ops:
  3.9 15.0 %copy-start = (bf16[480,768]{1,0:T(8,128)(2,1)S(1)}, bf16[480,768]{1,0:T(8,128)(2,1)}, u32[]{:S(2)}) copy-start(bf16[480,768]{1,0:T(8,128)(2,1)} %param.9) | copy-start | bytes 2211844
  3.9 16.4 %copy-start.3 = (bf16[480,768]{1,0:T(8,128)(2,1)S(1)}, bf16[480,768]{1,0:T(8,128)(2,1)}, u32[]{:S(2)}) copy-start(bf16[480,768]{1,0:T(8,128)(2,1)} %param.10) | copy-start | bytes 2211844
  3.9 18.6 %copy-start.7 = (s32[480]{0:T(512)S(1)}, s32[480]{0:T(512)}, u32[]{:S(2)}) copy-start(s32[480]{0:T(512)} %param.11) | copy-start | bytes 5764
  3.9 61.5 %all-to-all-start = ((bf16[8,2,16,7168]{3,2,1,0:T(8,128)(2,1)}), bf16[8,2,16,7168]{3,2,1,0:T(8,128)(2,1)}, u32[]{:S(2)}, u32[]{:S(2)}) async-start(bf16[8,2,16,7168]{3,2,1,0:T(8,128)(2,1)} %broadcast_in_dim.58), calls=%async_computation | async-start | bytes 7340032 | tf_op jit(solution)/shard_map/all_to_all | solution.py:43
  18.9 33.1 %collective-permute-start = (bf16[480,768]{1,0:T(8,128)(2,1)S(1)}, bf16[480,768]{1,0:T(8,128)(2,1)S(1)}, u32[]{:S(2)}, u32[]{:S(2)}) collective-permute-start(bf16[480,768]{1,0:T(8,128)(2,1)S(1)} %copy-done), channel_id=1, source_target_pairs={{0,8},{8,16},{16,24},{24,32},{32,40},{40,48},{48,56},{56,64},{64,7... | collective-permute-start | bytes 2211848 | tf_op jit(solution)/shard_map/ppermute | solution.py:28
  20.3 31.7 %collective-permute-start.1 = (bf16[480,768]{1,0:T(8,128)(2,1)S(1)}, bf16[480,768]{1,0:T(8,128)(2,1)}, u32[]{:S(2)}, u32[]{:S(2)}) collective-permute-start(bf16[480,768]{1,0:T(8,128)(2,1)S(1)} %copy-done.3), channel_id=1, source_target_pairs={{0,8},{8,16},{16,24},{24,32},{32,40},{40,48},{48,56},{56,64},{64,7... | collective-permute-start | bytes 2211848 | tf_op jit(solution)/shard_map/ppermute | solution.py:28
  22.5 29.5 %collective-permute-start.2 = (s32[480]{0:T(512)S(1)}, s32[480]{0:T(512)S(1)}, u32[]{:S(2)}, u32[]{:S(2)}) collective-permute-start(s32[480]{0:T(512)S(1)} %copy-done.7), channel_id=1, source_target_pairs={{0,8},{8,16},{16,24},{24,32},{32,40},{40,48},{48,56},{56,64},{64,7... | collective-permute-start | bytes 5768 | tf_op jit(solution)/shard_map/ppermute | solution.py:28
  27.3 35.2 %copy-start.1 = (bf16[480,768]{0,1:T(8,128)(2,1)}, bf16[480,768]{0,1:T(8,128)(2,1)S(1)}, u32[]{:S(2)}) copy-start(bf16[480,768]{0,1:T(8,128)(2,1)S(1)} %copy.96) | copy-start | bytes 2211844
  53.3 27.4 %collective-permute-start.3 = (bf16[480,768]{1,0:T(8,128)(2,1)S(1)}, bf16[480,768]{1,0:T(8,128)(2,1)S(1)}, u32[]{:S(2)}, u32[]{:S(2)}) collective-permute-start(bf16[480,768]{1,0:T(8,128)(2,1)S(1)} %collective-permute-done), channel_id=1, source_target_pairs={{0,8},{8,16},{16,24},{24,32},{32,40},{40,48},{48,56},{56,64},{64,7... | collective-permute-start | bytes 2211848 | tf_op jit(solution)/shard_map/ppermute | solution.py:28
  57.5 23.1 %collective-permute-start.5 = (s32[480]{0:T(512)S(1)}, s32[480]{0:T(512)S(1)}, u32[]{:S(2)}, u32[]{:S(2)}) collective-permute-start(s32[480]{0:T(512)S(1)} %collective-permute-done.2), channel_id=1, source_target_pairs={{0,8},{8,16},{16,24},{24,32},{32,40},{40,48},{48,56},{56,64},{64,7... | collective-permute-start | bytes 5768 | tf_op jit(solution)/shard_map/ppermute | solution.py:28
  59.4 29.1 %collective-permute-start.4 = (bf16[480,768]{1,0:T(8,128)(2,1)}, bf16[480,768]{1,0:T(8,128)(2,1)}, u32[]{:S(2)}, u32[]{:S(2)}) collective-permute-start(bf16[480,768]{1,0:T(8,128)(2,1)} %collective-permute-done.1), channel_id=1, source_target_pairs={{0,8},{8,16},{16,24},{24,32},{32,40},{40,48},{48,56},{56,64},{64,7... | collective-permute-start | bytes 2211848 | tf_op jit(solution)/shard_map/ppermute | solution.py:28
  73.5 5.1 %copy-start.11 = (f32[2]{0:T(128)S(1)}, f32[2]{0:T(128)}, u32[]{:S(2)}) copy-start(f32[2]{0:T(128)} %get-tuple-element.127) | copy-start | bytes 28
  77.2 13.5 %copy-start.2 = (bf16[480,768]{0,1:T(8,128)(2,1)S(1)}, bf16[480,768]{0,1:T(8,128)(2,1)}, u32[]{:S(2)}) copy-start(bf16[480,768]{0,1:T(8,128)(2,1)} %copy-done.1) | copy-start | bytes 2211844
  80.6 80.3 %copy-start.6 = (bf16[2,128,896]{2,1,0:T(8,128)(2,1)}, bf16[2,128,896]{2,1,0:T(8,128)(2,1)S(1)}, u32[]{:S(2)}) copy-start(bf16[2,128,896]{2,1,0:T(8,128)(2,1)S(1)} %fusion.31) | copy-start | bytes 1376260
  89.8 3.4 %copy-start.8 = (f32[6]{0:T(128)S(1)}, f32[6]{0:T(128)}, u32[]{:S(2)}) copy-start(f32[6]{0:T(128)} %select_reduce_fusion) | copy-start | bytes 76
  89.8 3.4 %copy-start.9 = (f32[6]{0:T(128)S(1)}, f32[6]{0:T(128)}, u32[]{:S(2)}) copy-start(f32[6]{0:T(128)} %fusion.26) | copy-start | bytes 76
  93.8 55.2 %all-to-all-start.1 = ((f32[96,1,6]{2,1,0:T(1,128)}), f32[96,1,6]{2,1,0:T(1,128)S(1)}, u32[]{:S(2)}, u32[]{:S(2)}) async-start(f32[96,1,6]{2,1,0:T(1,128)} %broadcast_in_dim.62), calls=%async_computation.1 | async-start | bytes 98304 | tf_op jit(solution)/shard_map/all_to_all | solution.py:43
  111.5 3.7 %copy-start.4 = (bf16[6,480,128]{2,1,0:T(8,128)(2,1)S(1)}, bf16[6,480,128]{2,1,0:T(8,128)(2,1)}, u32[]{:S(2)}) copy-start(bf16[6,480,128]{2,1,0:T(8,128)(2,1)} %custom-call) | copy-start | bytes 2211844
  115.2 45.6 %copy-start.10 = (s32[2]{0:T(128)S(1)}, s32[2]{0:T(128)}, u32[]{:S(2)}) copy-start(s32[2]{0:T(128)} %and_select_fusion) | copy-start | bytes 28
  115.2 45.8 %copy-start.5 = (bf16[2,128,896]{2,1,0:T(8,128)(2,1)S(1)}, bf16[2,128,896]{2,1,0:T(8,128)(2,1)}, u32[]{:S(2)}) copy-start(bf16[2,128,896]{2,1,0:T(8,128)(2,1)} %param.13) | copy-start | bytes 1376260
  149.8 10.9 %all-to-all-start.2 = ((f32[8,1,6]{2,1,0:T(1,128)}), f32[8,1,6]{2,1,0:T(1,128)S(1)}, u32[]{:S(2)}, u32[]{:S(2)}) async-start(f32[8,1,6]{2,1,0:T(1,128)} %broadcast_in_dim.63), calls=%async_computation.2 | async-start | bytes 8192 | tf_op jit(solution)/shard_map/all_to_all | solution.py:43

commit v6 on v5

--- a/solution.py
+++ b/solution.py
@@ -37,6 +37,18 @@
     )
 
 
+def packed(arrays, docs):
+    digits = jnp.stack([docs // 256, docs % 256], axis=1).astype(jnp.bfloat16)
+    tail = jnp.pad(digits, ((0, 0), (0, HD - 2)))
+    return jnp.concatenate(list(arrays) + [tail], axis=1)
+
+
+def unpacked(block, parts, width):
+    arrays = [block[:, i * width:(i + 1) * width] for i in range(parts)]
+    digits = block[:, parts * width:parts * width + 2].astype(jnp.int32)
+    return arrays, digits[:, 0] * 256 + digits[:, 1]
+
+
 def gathered(values, axis):
     size = lax.axis_size(axis)
     spread = jnp.broadcast_to(values[None], (size,) + values.shape)
@@ -50,12 +62,12 @@
     seq_index = lax.axis_index("seq")
     head_index = lax.axis_index("head")
     head_count = lax.axis_size("head")
-    pieces = gathered(gradients, "head")
+    owned = lax.all_to_all(gradients, "head", split_axis=2, concat_axis=1, tiled=True)
     mats_here, rows_here = gradients.shape[0], gradients.shape[1]
-    cols_here = weights.shape[2]
-    gram = jnp.einsum(
-        "jmrd,kmsd->mjrks", pieces, pieces, preferred_element_type=jnp.float32
-    ).reshape(mats_here, HD, HD)
+    gram_part = jnp.einsum("mid,mjd->mij", owned, owned, preferred_element_type=jnp.float32)
+    chunks = jnp.transpose(gram_part.reshape(mats_here, head_count, rows_here, HD), (1, 0, 2, 3))
+    rows_mine = jnp.sum(lax.all_to_all(chunks, "head", 0, 0, tiled=True), axis=0)
+    gram = jnp.transpose(gathered(rows_mine, "head"), (1, 0, 2, 3)).reshape(mats_here, HD, HD)
     norm_value = jnp.sqrt(jnp.trace(gram, axis1=1, axis2=2)) + norm_eps
     square = gram / (norm_value * norm_value)[:, None, None]
     identity = jnp.eye(HD, dtype=jnp.float32)
@@ -67,42 +79,46 @@
             square = jnp.matmul(
                 poly, jnp.matmul(square, poly, precision=highest), precision=highest
             )
-    own_cols = lax.dynamic_slice_in_dim(pieces, head_index * cols_here, cols_here, 3)
-    start = own_cols.astype(jnp.float32) / norm_value[None, :, None, None]
-    current = jnp.einsum(
-        "mijr,jmrd->mid",
-        total.reshape(mats_here, HD, head_count, rows_here),
-        start,
-        precision=highest,
-    )
+    start = owned.astype(jnp.float32) / norm_value[:, None, None]
+    current = jnp.matmul(total, start, precision=highest)
     update = (current * (update_gain * math.sqrt(D))).astype(jnp.bfloat16)
     local_block = (key_vectors, value_vectors, doc_ids)
     query_place = seq_index * tokens_here + jnp.arange(tokens_here, dtype=jnp.int32)
-    def block_max(member, block):
+    def block_max(queries, query_docs, query_at, member, block):
         keys_blk, docs_blk = member[0], member[2]
         place_blk = (seq_index - REACH + block) * tokens_here + jnp.arange(
             tokens_here, dtype=jnp.int32
         )
         allowed = (
-            (doc_ids[:, None] == docs_blk[None, :])
-            & (place_blk[None, :] <= query_place[:, None])
+            (query_docs[:, None] == docs_blk[None, :])
+            & (place_blk[None, :] <= query_at[:, None])
             & (place_blk[None, :] >= 0)
+            & (query_at[:, None] < lax.axis_size("seq") * tokens_here)
         )
         scores = jnp.einsum(
             "qhd,khd->hqk",
-            query_vectors.reshape(tokens_here, heads_here, HD),
+            queries.reshape(tokens_here, heads_here, HD),
             keys_blk.reshape(tokens_here, heads_here, HD),
             preferred_element_type=jnp.float32,
         ) / math.sqrt(HD)
         return jnp.max(jnp.where(allowed[None], scores, masked_fill), axis=(1, 2))
 
-    first = shifted(local_block, "seq", 1)
-    local_max = block_max(local_block, REACH)
-    first, local_max = lax.optimization_barrier((first, local_max))
-    second = shifted(first, "seq", 1)
-    first_max = block_max(first, REACH - 1)
-    second, first_max, update = lax.optimization_barrier((second, first_max, update))
-    head_max = jnp.maximum(jnp.maximum(local_max, first_max), block_max(second, REACH - 2))
+    cols = key_vectors.shape[1]
+    first_packed = shifted(packed((key_vectors, value_vectors), doc_ids), "seq", 1)
+    back = shifted(packed((query_vectors,), doc_ids), "seq", -1)
+    local_max = block_max(query_vectors, doc_ids, query_place, local_block, REACH)
+    first_packed, local_max = lax.optimization_barrier((first_packed, local_max))
+    second_packed = shifted(first_packed, "seq", 1)
+    (first_keys, first_values), first_docs = unpacked(first_packed, 2, cols)
+    first = (first_keys, first_values, first_docs)
+    (next_queries,), next_docs = unpacked(back, 1, cols)
+    first_max = block_max(query_vectors, doc_ids, query_place, first, REACH - 1)
+    far_max = block_max(next_queries, next_docs, query_place + tokens_here, first, REACH - 1)
+    head_max = jnp.maximum(jnp.maximum(local_max, first_max), far_max)
+    seq_max = jnp.max(gathered(head_max, "seq"), axis=0)
+    second_packed, seq_max = lax.optimization_barrier((second_packed, seq_max))
+    (second_keys, second_values), second_docs = unpacked(second_packed, 2, cols)
+    second = (second_keys, second_values, second_docs)
     earlier = [first, second]
     ordered = [earlier[REACH - 1 - position] for position in range(REACH)] + [local_block]
     keys_all = jnp.concatenate([member[0] for member in ordered], axis=0)
@@ -139,7 +155,6 @@
     attention_out = jnp.transpose(mixed_heads, (1, 0, 2)).reshape(tokens_here, heads_here * HD)
     heads_all = heads_here * head_count
     head_slots = jnp.arange(heads_all, dtype=jnp.int32)
-    seq_max = jnp.max(gathered(head_max, "seq"), axis=0)
     max_logit = gathered(seq_max, "head").reshape(heads_all)
     root_gamma = jnp.sqrt(clip_tau / jnp.maximum(max_logit, clip_tau))
 

time: 163 us -> 192 us (1.18)
  local copies, waits for them, and re-layouts: 15.4 us -> 42.5 us
  other arithmetic: 11.7 us -> 21 us
  matrix products: 45.1 us -> 37.9 us
    ppermute x6 -> x3, waiting for transfers between devices: 28.8 us -> 0.01 us  [shifted(): return lax.ppermute(shard, axis, pairs)]
    all_to_all x3, waiting for transfers between devices: 3.09 us -> 27.9 us  [gathered(): return lax.all_to_all(spread, axis, 0, 0, tiled=True)]
    unnamed x27 -> x47, local copies, waits for them, and re-layouts: 3.82 us -> 19.6 us
    all_to_all x3, starting transfers between devices: 39.1 us -> 23.6 us  [gathered(): return lax.all_to_all(spread, axis, 0, 0, tiled=True)]
    all_to_all x0 -> x2, starting transfers between devices: none -> 15.4 us  [the longest x1 11.3 us: shards(): lax.all_to_all(gradients, 'head', split_axis=2, concat_axis=1, tiled=True)]
    all_to_all x0 -> x1, local copies, waits for them, and re-layouts: none -> 7.87 us  [shards(): lax.all_to_all(gradients, 'head', split_axis=2, concat_axis=1, tiled=True)]
    dot_general x5, matrix products: 17.3 us -> 9.4 us  [the longest x3 7.03 us: block_max(): jnp.einsum('qhd,khd->hqk', queries.reshape(tokens_here, heads_here, HD),...]
    slice x0 -> x5, local copies, waits for them, and re-layouts: none -> 7.01 us  [unpacked(): arrays = [block[:, i * width:(i + 1) * width] for i in range(parts)]]
  transfers between devices with their start and end apart: 9 -> 8, of which waited for: 3 -> 5; matrix products, arithmetic and copies ran while one was open for 38% -> 30% of each run, Pallas kernels for 0% -> 0%
where the time goes in v6:
time: 192 us; the launch traced here: 191 us
  starting transfers between devices  50.9 us (27%)
  local copies, waits for them, and re-layouts  42.5 us (22%)
  matrix products  37.9 us (20%)
  waiting for transfers between devices  33.4 us (17%)
  other arithmetic  21 us (11%)
  loops' own time  4.05 us (2%)
    all_to_all x3, waiting for transfers between devices, gathered(): return lax.all_to_all(spread, axis, 0, 0, tiled=True)  27.9 us
    all_to_all x3, starting transfers between devices, gathered(): return lax.all_to_all(spread, axis, 0, 0, tiled=True)  23.6 us
    unnamed x47, local copies, waits for them, and re-layouts  19.6 us
    dot_general x6, matrix products, one_head(): jnp.einsum('qd,kd->qk', query_cols, key_cols, preferred_element_type=jnp....  12.7 us
    ppermute x3, starting transfers between devices, shifted(): return lax.ppermute(shard, axis, pairs)  11.9 us
    all_to_all x1, starting transfers between devices, shards(): lax.all_to_all(gradients, 'head', split_axis=2, concat_axis=1, tiled=True)  11.3 us
    dot_general x6, matrix products, one_head(): jnp.dot(exp_scores.astype(jnp.bfloat16), value_cols, preferred_element_ty...  9.9 us
    all_to_all x1, local copies, waits for them, and re-layouts, shards(): lax.all_to_all(gradients, 'head', split_axis=2, concat_axis=1, tiled=True)  7.87 us
  transfers between devices with their start and end apart: 8, of which 5 were waited for; matrix products, arithmetic and copies ran while one was open for 30% of the time, Pallas kernels for 0%

profile of v6, /device:TPU:1, one launch (start us, length us, event | category | flops | bytes accessed | tf_op | source)
XLA Modules:
  0.0 190.8 jit_solution(3943512650222996047)
XLA Ops:
  1.7 2.7 %pad_maximum_fusion.2 = bf16[480,1664]{1,0:T(8,128)(2,1)} fusion(bf16[480,128]{1,0:T(8,128)(2,1)S(1)} %pad.5.clone, bf16[480,768]{1,0:T(8,128)(2,1)} %param.10, bf16[480,768]{1,0:T(8,128)(2,1)} %param.9), kind=kLoop, calls=%fused_computation.23 | loop fusion | flops 4792320 | bytes 3194880 | tf_op jit(solution)/shard_map/concatenate | solution.py:43
  4.4 5.2 %collective-permute-start = (bf16[480,1664]{1,0:T(8,128)(2,1)}, bf16[480,1664]{1,0:T(8,128)(2,1)}, u32[]{:S(2)}, u32[]{:S(2)}) collective-permute-start(bf16[480,1664]{1,0:T(8,128)(2,1)} %pad_maximum_fusion.2), channel_id=1, source_target_pairs={{0,8},{8,16},{16,24},{24,32},{32,40},{40,48},{48,56},{56,64},{64,7... | collective-permute-start | bytes 4792328 | tf_op jit(solution)/shard_map/ppermute | solution.py:28
  11.8 6.0 %copy.116 = bf16[2,16,7168]{1,0,2:T(2,128)(2,1)} copy(bf16[2,16,7168]{2,1,0:T(8,128)(2,1)S(1)} %copy-done.9) | data formatting | bytes 917504 | tf_op args[4]
  17.8 6.0 %reshape.430 = bf16[8,2,14336]{2,1,0:T(2,128)(2,1)} reshape(bf16[7168,2,16]{2,1,0:T(2,128)(2,1)} %bitcast.77) | data formatting | bytes 917504
  23.9 11.3 %all-to-all-start.1 = ((bf16[8,2,14336]{2,1,0:T(2,128)(2,1)}), bf16[8,2,14336]{2,1,0:T(2,128)(2,1)S(1)}, u32[]{:S(2)}, u32[]{:S(2)}) async-start(bf16[8,2,14336]{2,1,0:T(2,128)(2,1)} %reshape.430), calls=%async_computation.1 | async-start | bytes 917504 | tf_op jit(solution)/shard_map/all_to_all | solution.py:65
  39.6 3.1 %select_reduce_fusion.1 = f32[6]{0:T(128)} fusion(pred[480,480]{1,0:T(8,128)(4,1)S(1)} %copy.100, bf16[480,6,128]{0,2,1:T(8,128)(2,1)} %bitcast.82, bf16[480,6,128]{0,2,1:T(8,128)(2,1)} %bitcast.85), kind=kOutput, calls=%fused_computation.20 | convolution fusion | flops 358041600 | bytes 1704984 | tf_op jit(solution)/shard_map/qhd,khd->hqk/dot_general | solution.py:98
  44.0 3.8 %reshape.431 = bf16[7168,2,16]{2,1,0:T(2,128)(2,1)} reshape(bf16[8,2,14336]{2,1,0:T(2,128)(2,1)S(1)} %all-to-all-done.1) | data formatting | bytes 917504
  47.8 7.9 %copy.117 = bf16[2,16,8,896]{3,1,2,0:T(8,128)(2,1)S(1)} copy(bf16[2,16,8,896]{1,0,3,2:T(2,128)(2,1)} %bitcast.76) | data formatting | bytes 917504 | tf_op jit(solution)/shard_map/all_to_all | solution.py:65
  56.7 4.1 %all-to-all-start.2 = ((f32[8,2,16,128]{3,2,1,0:T(8,128)}), f32[8,2,16,128]{3,2,1,0:T(8,128)S(1)}, u32[]{:S(2)}, u32[]{:S(2)}) async-start(f32[8,2,16,128]{3,2,1,0:T(8,128)} %bitcast.71), calls=%async_computation.2 | async-start | bytes 262144 | tf_op jit(solution)/shard_map/all_to_all | solution.py:69
  61.9 4.2 %all-to-all-done.2 = f32[8,2,16,128]{3,2,1,0:T(8,128)S(1)} async-done(((f32[8,2,16,128]{3,2,1,0:T(8,128)}), f32[8,2,16,128]{3,2,1,0:T(8,128)S(1)}, u32[]{:S(2)}, u32[]{:S(2)}) %all-to-all-start.2) | async-done | bytes 131104 | tf_op jit(solution)/shard_map/all_to_all | solution.py:69
  66.8 4.1 %all-to-all-start.3 = ((f32[8,2,16,128]{3,2,1,0:T(8,128)}), f32[8,2,16,128]{3,2,1,0:T(8,128)S(1)}, u32[]{:S(2)}, u32[]{:S(2)}) async-start(f32[8,2,16,128]{3,2,1,0:T(8,128)} %broadcast_in_dim.57), calls=%async_computation.3 | async-start | bytes 262144 | tf_op jit(solution)/shard_map/all_to_all | solution.py:55
  71.5 4.7 %all-to-all-done.3 = f32[8,2,16,128]{3,2,1,0:T(8,128)S(1)} async-done(((f32[8,2,16,128]{3,2,1,0:T(8,128)}), f32[8,2,16,128]{3,2,1,0:T(8,128)S(1)}, u32[]{:S(2)}, u32[]{:S(2)}) %all-to-all-start.3) | async-done | bytes 131104 | tf_op jit(solution)/shard_map/all_to_all | solution.py:55
  84.1 5.4 %collective-permute-start.1 = (bf16[480,1664]{1,0:T(8,128)(2,1)}, bf16[480,1664]{1,0:T(8,128)(2,1)}, u32[]{:S(2)}, u32[]{:S(2)}) collective-permute-start(bf16[480,1664]{1,0:T(8,128)(2,1)} %collective-permute-done), channel_id=1, source_target_pairs={{0,8},{8,16},{16,24},{24,32},{32,40},{40,48},{48,56},{56,64},{64,7... | collective-permute-start | bytes 4792328 | tf_op jit(solution)/shard_map/ppermute | solution.py:28
  90.7 2.0 %and_and_fusion.1 = (pred[480,480]{0,1:T(8,128)(4,1)}, pred[480,480]{0,1:T(8,128)(4,1)S(1)}) fusion(s32[480]{0:T(512)S(1)} %get-tuple-element.212, s32[480]{0:T(512)S(1)} %copy-done.11, s32[480]{0:T(512)S(1)} %iota_add_fusion.1, s32[480]{0:T(512)S(1)} %fusion.37, pred[480]{0:T(512)(128)(4,1)} %broadcast_compare_fusion.2, pred[480]{0:T(512)(128)(4,1)S(1)} %copy-done.14, ...), kind=kLoop, calls=%fused_computation.37 | loop fusion | flops 2304000 | bytes 473760 | tf_op jit(solution)/shard_map/and | solution.py:93
  93.7 2.3 %fusion.49 = (bf16[480,768]{1,0:T(8,128)(2,1)}, bf16[480,768]{1,0:T(8,128)(2,1)S(1)}) fusion(bf16[480,1664]{1,0:T(8,128)(2,1)} %collective-permute-done), kind=kLoop, calls=%fused_computation.94 | loop fusion | bytes 2949120 | tf_op jit(solution)/shard_map/slice | solution.py:47
  97.2 2.6 %fusion.25 = f32[6]{0:T(128)S(1)} fusion(pred[480,480]{0,1:T(8,128)(4,1)} %get-tuple-element.121, bf16[480,6,128]{0,2,1:T(8,128)(2,1)} %bitcast.86, bf16[480,6,128]{0,2,1:T(8,128)(2,1)S(1)} %bitcast.83), kind=kOutput, calls=%fused_computation.18 | convolution fusion | flops 358041600 | bytes 1704984 | tf_op jit(solution)/shard_map/qhd,khd->hqk/dot_general | solution.py:98
  101.8 13.9 %all-to-all-start = ((f32[96,1,6]{2,1,0:T(1,128)}), f32[96,1,6]{2,1,0:T(1,128)S(1)}, u32[]{:S(2)}, u32[]{:S(2)}) async-start(f32[96,1,6]{2,1,0:T(1,128)} %broadcast_in_dim.56), calls=%async_computation | async-start | bytes 98304 | tf_op jit(solution)/shard_map/all_to_all | solution.py:55
  116.0 20.1 %all-to-all-done = f32[96,1,6]{2,1,0:T(1,128)S(1)} async-done(((f32[96,1,6]{2,1,0:T(1,128)}), f32[96,1,6]{2,1,0:T(1,128)S(1)}, u32[]{:S(2)}, u32[]{:S(2)}) %all-to-all-start) | async-done | bytes 2336 | tf_op jit(solution)/shard_map/all_to_all | solution.py:55
  136.2 2.3 %fusion.48 = (bf16[480,768]{1,0:T(8,128)(2,1)}, bf16[480,768]{1,0:T(8,128)(2,1)S(1)}) fusion(bf16[480,1664]{1,0:T(8,128)(2,1)} %collective-permute-done.1), kind=kLoop, calls=%fused_computation.93 | loop fusion | bytes 2949120 | tf_op jit(solution)/shard_map/slice | solution.py:47
  141.3 2.8 %pad_maximum_fusion.1 = bf16[1440,768]{1,0:T(8,128)(2,1)} fusion(bf16[480,768]{1,0:T(8,128)(2,1)S(1)} %copy-done.1, bf16[480,768]{1,0:T(8,128)(2,1)} %get-tuple-element.119, bf16[480,768]{1,0:T(8,128)(2,1)} %get-tuple-element.117), kind=kLoop, calls=%fused_computation.22 | loop fusion | flops 6635520 | bytes 4423680 | tf_op jit(solution)/shard_map/concatenate | solution.py:125
  144.2 33.5 %while.11 = (s32[]{:T(128)}, bf16[6,480,128]{2,1,0:T(8,128)(2,1)S(1)}, s32[6]{0:T(128)S(1)}, bf16[480,768]{1,0:T(8,128)(2,1)S(1)}, bf16[1440,768]{1,0:T(8,128)(2...) while((s32[]{:T(128)}, ...), condition=%wide.region_7.8_spmd.clone, body=%wide.region_4.7_spmd.clone.sunk | while | flops 361619520 | bytes 9495383 | solution.py:154
  145.5 2.1 %fusion.113 = (f32[480]{0:T(512)S(1)}, f32[480,1440]{1,0:T(8,128)S(1)}) fusion(bf16[1440,768]{1,0:T(8,128)(2,1)} %get-tuple-element.238, s32[]{:T(128)S(6)} %select_n.85, bf16[480,768]{1,0:T(8,128)(2,1)S(1)} %get-tuple-element.237, pred[1440]{0:T(1024)(128)(4,1)S(1)} %get-tuple-element.244, s32[480]{0:T(512)S(1)} %get-tuple-element.242, ...), kind=kOutput, calls=%fused_computation.92.clone.1 | convolution fusion | flops 181785120 | bytes 3281792 | tf_op jit(solution)/shard_map/while/body/eval_jaxpr/qd,kd->qk/dot_general | solution.py:141
  151.0 2.1 %fusion.113 = (f32[480]{0:T(512)S(1)}, f32[480,1440]{1,0:T(8,128)S(1)}) fusion(bf16[1440,768]{1,0:T(8,128)(2,1)} %get-tuple-element.238, s32[]{:T(128)S(6)} %select_n.85, bf16[480,768]{1,0:T(8,128)(2,1)S(1)} %get-tuple-element.237, pred[1440]{0:T(1024)(128)(4,1)S(1)} %get-tuple-element.244, s32[480]{0:T(512)S(1)} %get-tuple-element.242, ...), kind=kOutput, calls=%fused_computation.92.clone.1 | convolution fusion | flops 181785120 | bytes 3281792 | tf_op jit(solution)/shard_map/while/body/eval_jaxpr/qd,kd->qk/dot_general | solution.py:141
  153.7 1.7 fusion.115
  156.6 2.1 %fusion.113 = (f32[480]{0:T(512)S(1)}, f32[480,1440]{1,0:T(8,128)S(1)}) fusion(bf16[1440,768]{1,0:T(8,128)(2,1)} %get-tuple-element.238, s32[]{:T(128)S(6)} %select_n.85, bf16[480,768]{1,0:T(8,128)(2,1)S(1)} %get-tuple-element.237, pred[1440]{0:T(1024)(128)(4,1)S(1)} %get-tuple-element.244, s32[480]{0:T(512)S(1)} %get-tuple-element.242, ...), kind=kOutput, calls=%fused_computation.92.clone.1 | convolution fusion | flops 181785120 | bytes 3281792 | tf_op jit(solution)/shard_map/while/body/eval_jaxpr/qd,kd->qk/dot_general | solution.py:141
  162.2 2.1 %fusion.113 = (f32[480]{0:T(512)S(1)}, f32[480,1440]{1,0:T(8,128)S(1)}) fusion(bf16[1440,768]{1,0:T(8,128)(2,1)} %get-tuple-element.238, s32[]{:T(128)S(6)} %select_n.85, bf16[480,768]{1,0:T(8,128)(2,1)S(1)} %get-tuple-element.237, pred[1440]{0:T(1024)(128)(4,1)S(1)} %get-tuple-element.244, s32[480]{0:T(512)S(1)} %get-tuple-element.242, ...), kind=kOutput, calls=%fused_computation.92.clone.1 | convolution fusion | flops 181785120 | bytes 3281792 | tf_op jit(solution)/shard_map/while/body/eval_jaxpr/qd,kd->qk/dot_general | solution.py:141
  164.9 1.7 fusion.115
  167.8 2.1 %fusion.113 = (f32[480]{0:T(512)S(1)}, f32[480,1440]{1,0:T(8,128)S(1)}) fusion(bf16[1440,768]{1,0:T(8,128)(2,1)} %get-tuple-element.238, s32[]{:T(128)S(6)} %select_n.85, bf16[480,768]{1,0:T(8,128)(2,1)S(1)} %get-tuple-element.237, pred[1440]{0:T(1024)(128)(4,1)S(1)} %get-tuple-element.244, s32[480]{0:T(512)S(1)} %get-tuple-element.242, ...), kind=kOutput, calls=%fused_computation.92.clone.1 | convolution fusion | flops 181785120 | bytes 3281792 | tf_op jit(solution)/shard_map/while/body/eval_jaxpr/qd,kd->qk/dot_general | solution.py:141
  173.4 2.1 %fusion.113 = (f32[480]{0:T(512)S(1)}, f32[480,1440]{1,0:T(8,128)S(1)}) fusion(bf16[1440,768]{1,0:T(8,128)(2,1)} %get-tuple-element.238, s32[]{:T(128)S(6)} %select_n.85, bf16[480,768]{1,0:T(8,128)(2,1)S(1)} %get-tuple-element.237, pred[1440]{0:T(1024)(128)(4,1)S(1)} %get-tuple-element.244, s32[480]{0:T(512)S(1)} %get-tuple-element.242, ...), kind=kOutput, calls=%fused_computation.92.clone.1 | convolution fusion | flops 181785120 | bytes 3281792 | tf_op jit(solution)/shard_map/while/body/eval_jaxpr/qd,kd->qk/dot_general | solution.py:141
  178.3 5.6 %all-to-all-start.4 = ((f32[8,1,6]{2,1,0:T(1,128)}), f32[8,1,6]{2,1,0:T(1,128)S(1)}, u32[]{:S(2)}, u32[]{:S(2)}) async-start(f32[8,1,6]{2,1,0:T(1,128)} %broadcast_in_dim.63), calls=%async_computation.4 | async-start | bytes 8192 | tf_op jit(solution)/shard_map/all_to_all | solution.py:55
  185.3 3.1 %all-to-all-done.4 = f32[8,1,6]{2,1,0:T(1,128)S(1)} async-done(((f32[8,1,6]{2,1,0:T(1,128)}), f32[8,1,6]{2,1,0:T(1,128)S(1)}, u32[]{:S(2)}, u32[]{:S(2)}) %all-to-all-start.4) | async-done | bytes 224 | tf_op jit(solution)/shard_map/all_to_all | solution.py:55
  188.8 2.1 %multiply_convert_fusion = (bf16[2,128,896]{2,1,0:T(8,128)(2,1)}, bf16[2,128,896]{2,1,0:T(8,128)(2,1)}) fusion(bf16[2,128,896]{2,1,0:T(8,128)(2,1)S(1)} %copy-done.17, f32[2]{0:T(128)S(1)} %compare_select_fusion.1, f32[2,128,128]{2,1,0:T(8,128)S(1)} %fusion.62, bf16[2,128,896]{2,1,0:T(8,128)(2,1)S(1)} %bitcast.79, f32[2]{0:T(128)S(1)} %copy-done.19), kind=kOutput, calls=%fused_computation.39 | convolution fusion | flops 354844672 | bytes 1966096 | tf_op jit(solution)/shard_map/dot_general | solution.py:83
  (133 shorter events, 44.3 us)
Async XLA Ops:
  0.6 8.9 %copy-start.2 = (bf16[480,768]{1,0:T(8,128)(2,1)S(1)}, bf16[480,768]{1,0:T(8,128)(2,1)}, u32[]{:S(2)}) copy-start(bf16[480,768]{1,0:T(8,128)(2,1)} %param.8) | copy-start | bytes 2211844
  0.6 11.2 %copy-start.9 = (bf16[2,16,7168]{2,1,0:T(8,128)(2,1)S(1)}, bf16[2,16,7168]{2,1,0:T(8,128)(2,1)}, u32[]{:S(2)}) copy-start(bf16[2,16,7168]{2,1,0:T(8,128)(2,1)} %param.12) | copy-start | bytes 1376260
  4.4 79.7 %collective-permute-start = (bf16[480,1664]{1,0:T(8,128)(2,1)}, bf16[480,1664]{1,0:T(8,128)(2,1)}, u32[]{:S(2)}, u32[]{:S(2)}) collective-permute-start(bf16[480,1664]{1,0:T(8,128)(2,1)} %pad_maximum_fusion.2), channel_id=1, source_target_pairs={{0,8},{8,16},{16,24},{24,32},{32,40},{40,48},{48,56},{56,64},{64,7... | collective-permute-start | bytes 4792328 | tf_op jit(solution)/shard_map/ppermute | solution.py:28
  10.5 72.1 %collective-permute-start.2 = (bf16[480,896]{1,0:T(8,128)(2,1)}, bf16[480,896]{1,0:T(8,128)(2,1)S(1)}, u32[]{:S(2)}, u32[]{:S(2)}) collective-permute-start(bf16[480,896]{1,0:T(8,128)(2,1)} %pad_maximum_fusion.3), channel_id=1, source_target_pairs={{8,0},{16,8},{24,16},{32,24},{40,32},{48,40},{56,48},{64,56},{72,6... | collective-permute-start | bytes 2580488 | tf_op jit(solution)/shard_map/ppermute | solution.py:28
  17.8 19.1 %copy-start = (bf16[480,768]{1,0:T(8,128)(2,1)S(1)}, bf16[480,768]{1,0:T(8,128)(2,1)}, u32[]{:S(2)}) copy-start(bf16[480,768]{1,0:T(8,128)(2,1)} %param.9) | copy-start | bytes 2211844
  23.9 14.2 %copy-start.11 = (s32[480]{0:T(512)S(1)}, s32[480]{0:T(512)}, u32[]{:S(2)}) copy-start(s32[480]{0:T(512)} %param.11) | copy-start | bytes 5764
  23.9 20.1 %all-to-all-start.1 = ((bf16[8,2,14336]{2,1,0:T(2,128)(2,1)}), bf16[8,2,14336]{2,1,0:T(2,128)(2,1)S(1)}, u32[]{:S(2)}, u32[]{:S(2)}) async-start(bf16[8,2,14336]{2,1,0:T(2,128)(2,1)} %reshape.430), calls=%async_computation.1 | async-start | bytes 917504 | tf_op jit(solution)/shard_map/all_to_all | solution.py:65
  35.7 3.1 %copy-start.13 = (pred[480]{0:T(512)(128)(4,1)}, pred[480]{0:T(512)(128)(4,1)S(1)}, u32[]{:S(2)}) copy-start(pred[480]{0:T(512)(128)(4,1)S(1)} %get-tuple-element.131) | copy-start | bytes 1444
  56.7 9.4 %all-to-all-start.2 = ((f32[8,2,16,128]{3,2,1,0:T(8,128)}), f32[8,2,16,128]{3,2,1,0:T(8,128)S(1)}, u32[]{:S(2)}, u32[]{:S(2)}) async-start(f32[8,2,16,128]{3,2,1,0:T(8,128)} %bitcast.71), calls=%async_computation.2 | async-start | bytes 262144 | tf_op jit(solution)/shard_map/all_to_all | solution.py:69
  66.8 9.4 %all-to-all-start.3 = ((f32[8,2,16,128]{3,2,1,0:T(8,128)}), f32[8,2,16,128]{3,2,1,0:T(8,128)S(1)}, u32[]{:S(2)}, u32[]{:S(2)}) async-start(f32[8,2,16,128]{3,2,1,0:T(8,128)} %broadcast_in_dim.57), calls=%async_computation.3 | async-start | bytes 262144 | tf_op jit(solution)/shard_map/all_to_all | solution.py:55
  80.5 10.2 %copy-start.14 = (pred[480]{0:T(512)(128)(4,1)S(1)}, pred[480]{0:T(512)(128)(4,1)}, u32[]{:S(2)}) copy-start(pred[480]{0:T(512)(128)(4,1)} %copy-done.13) | copy-start | bytes 1444
  84.1 52.1 %collective-permute-start.1 = (bf16[480,1664]{1,0:T(8,128)(2,1)}, bf16[480,1664]{1,0:T(8,128)(2,1)}, u32[]{:S(2)}, u32[]{:S(2)}) collective-permute-start(bf16[480,1664]{1,0:T(8,128)(2,1)} %collective-permute-done), channel_id=1, source_target_pairs={{0,8},{8,16},{16,24},{24,32},{32,40},{40,48},{48,56},{56,64},{64,7... | collective-permute-start | bytes 4792328 | tf_op jit(solution)/shard_map/ppermute | solution.py:28
  90.5 6.7 %copy-start.3 = (bf16[480,768]{0,1:T(8,128)(2,1)S(1)}, bf16[480,768]{0,1:T(8,128)(2,1)}, u32[]{:S(2)}) copy-start(bf16[480,768]{0,1:T(8,128)(2,1)} %copy.101) | copy-start | bytes 2211844
  97.2 2.6 %copy-start.4 = (bf16[480,768]{0,1:T(8,128)(2,1)S(1)}, bf16[480,768]{0,1:T(8,128)(2,1)}, u32[]{:S(2)}) copy-start(bf16[480,768]{0,1:T(8,128)(2,1)} %copy.111) | copy-start | bytes 2211844
  97.2 2.6 %copy-start.5 = (bf16[480,768]{0,1:T(8,128)(2,1)S(1)}, bf16[480,768]{0,1:T(8,128)(2,1)}, u32[]{:S(2)}) copy-start(bf16[480,768]{0,1:T(8,128)(2,1)} %copy.105) | copy-start | bytes 2211844
  97.2 2.6 %copy-start.10 = (pred[480,480]{1,0:T(8,128)(4,1)S(1)}, pred[480,480]{1,0:T(8,128)(4,1)}, u32[]{:S(2)}) copy-start(pred[480,480]{1,0:T(8,128)(4,1)} %copy.110) | copy-start | bytes 691204
  99.8 1.3 copy-start.16
  99.9 15.9 %copy-start.7 = (f32[2,128,128]{2,1,0:T(8,128)S(1)}, f32[2,128,128]{2,1,0:T(8,128)}, u32[]{:S(2)}) copy-start(f32[2,128,128]{2,1,0:T(8,128)} %fusion.61) | copy-start | bytes 393220
  99.9 15.9 %copy-start.8 = (f32[2,128,128]{2,1,0:T(8,128)S(1)}, f32[2,128,128]{2,1,0:T(8,128)}, u32[]{:S(2)}) copy-start(f32[2,128,128]{2,1,0:T(8,128)} %fusion.27) | copy-start | bytes 393220
  101.8 34.2 %all-to-all-start = ((f32[96,1,6]{2,1,0:T(1,128)}), f32[96,1,6]{2,1,0:T(1,128)S(1)}, u32[]{:S(2)}, u32[]{:S(2)}) async-start(f32[96,1,6]{2,1,0:T(1,128)} %broadcast_in_dim.56), calls=%async_computation | async-start | bytes 98304 | tf_op jit(solution)/shard_map/all_to_all | solution.py:55
  138.5 2.8 %copy-start.1 = (bf16[480,768]{1,0:T(8,128)(2,1)S(1)}, bf16[480,768]{1,0:T(8,128)(2,1)}, u32[]{:S(2)}) copy-start(bf16[480,768]{1,0:T(8,128)(2,1)} %param.10) | copy-start | bytes 2211844
  141.0 3.2 %copy-start.6 = (bf16[6,480,128]{2,1,0:T(8,128)(2,1)S(1)}, bf16[6,480,128]{2,1,0:T(8,128)(2,1)}, u32[]{:S(2)}) copy-start(bf16[6,480,128]{2,1,0:T(8,128)(2,1)} %custom-call) | copy-start | bytes 2211844
  141.0 3.2 %copy-start.12 = (s32[1440]{0:T(1024)S(1)}, s32[1440]{0:T(1024)}, u32[]{:S(2)}) copy-start(s32[1440]{0:T(1024)} %iota_add_fusion) | copy-start | bytes 17284
  141.0 3.2 %copy-start.15 = (pred[1440]{0:T(1024)(128)(4,1)S(1)}, pred[1440]{0:T(1024)(128)(4,1)}, u32[]{:S(2)}) copy-start(pred[1440]{0:T(1024)(128)(4,1)} %broadcast_compare_fusion) | copy-start | bytes 4324
  177.7 10.8 %copy-start.18 = (s32[2]{0:T(128)S(1)}, s32[2]{0:T(128)}, u32[]{:S(2)}) copy-start(s32[2]{0:T(128)} %and_select_fusion) | copy-start | bytes 28
  177.7 11.0 %copy-start.17 = (bf16[2,128,896]{2,1,0:T(8,128)(2,1)S(1)}, bf16[2,128,896]{2,1,0:T(8,128)(2,1)}, u32[]{:S(2)}) copy-start(bf16[2,128,896]{2,1,0:T(8,128)(2,1)} %param.13) | copy-start | bytes 1376260
  177.7 11.0 %copy-start.19 = (f32[2]{0:T(128)S(1)}, f32[2]{0:T(128)}, u32[]{:S(2)}) copy-start(f32[2]{0:T(128)} %get-tuple-element.125) | copy-start | bytes 28
  178.3 10.1 %all-to-all-start.4 = ((f32[8,1,6]{2,1,0:T(1,128)}), f32[8,1,6]{2,1,0:T(1,128)S(1)}, u32[]{:S(2)}, u32[]{:S(2)}) async-start(f32[8,1,6]{2,1,0:T(1,128)} %broadcast_in_dim.63), calls=%async_computation.4 | async-start | bytes 8192 | tf_op jit(solution)/shard_map/all_to_all | solution.py:55

commit v7 on v5

--- a/solution.py
+++ b/solution.py
@@ -135,8 +135,7 @@
         )
         return (mixed_rows.astype(jnp.bfloat16), jnp.max(row_max))
 
-    mixed_heads, _ = lax.map(one_head, jnp.arange(heads_here, dtype=jnp.int32))
-    attention_out = jnp.transpose(mixed_heads, (1, 0, 2)).reshape(tokens_here, heads_here * HD)
+    attention_out = jnp.concatenate([one_head(slot)[0] for slot in range(heads_here)], axis=1)
     heads_all = heads_here * head_count
     head_slots = jnp.arange(heads_all, dtype=jnp.int32)
     seq_max = jnp.max(gathered(head_max, "seq"), axis=0)

time: 163 us -> 169 us (1.037)
  matrix products: 45.1 us -> 52.5 us
  local copies, waits for them, and re-layouts: 15.4 us -> 20.5 us
  loops' own time: 4.05 us -> 0 us
  other arithmetic: 11.7 us -> 8.3 us
  waiting for transfers between devices: 31.8 us -> 33.5 us
    dot_general x6, matrix products: 13.1 us -> 20.2 us  [one_head(): jnp.einsum('qd,kd->qk', query_cols, key_cols, preferred_element_type=jnp....]
    unnamed x27 -> x36, local copies, waits for them, and re-layouts: 3.82 us -> 8.71 us
    another operation x1 -> x0, loops' own time: 4.05 us -> none  [shards(): mixed_heads, _ = lax.map(one_head, jnp.arange(heads_here, dtype=jnp.int32))]
    concatenate x1 -> x0, other arithmetic: 3.64 us -> none  [shards(): keys_all = jnp.concatenate([member[0] for member in ordered], axis=0)]
    dynamic_slice x6 -> x0, local copies, waits for them, and re-layouts: 3.52 us -> none  [shards(): mixed_heads, _ = lax.map(one_head, jnp.arange(heads_here, dtype=jnp.int32))]
    concatenate x0 -> x2, local copies, waits for them, and re-layouts: none -> 2.96 us  [the longest x1 2.04 us: shards(): values_all = jnp.concatenate([member[1] for member in ordered], axis=0)]
    ppermute x6, waiting for transfers between devices: 28.8 us -> 31.3 us  [shifted(): return lax.ppermute(shard, axis, pairs)]
    dot_general x3, matrix products: 8.32 us -> 6.13 us  [block_max(): jnp.einsum('qhd,khd->hqk', query_vectors.reshape(tokens_here, heads_here,...]
  transfers between devices with their start and end apart: 9 -> 9, of which waited for: 3 -> 3; matrix products, arithmetic and copies ran while one was open for 38% -> 24% of each run, Pallas kernels for 0% -> 0%
where the time goes in v7:
time: 169 us; the launch traced here: 168 us
  matrix products  52.5 us (31%)
  starting transfers between devices  51.8 us (31%)
  waiting for transfers between devices  33.5 us (20%)
  local copies, waits for them, and re-layouts  20.5 us (12%)
  other arithmetic  8.3 us (5%)
    all_to_all x3, starting transfers between devices, gathered(): return lax.all_to_all(spread, axis, 0, 0, tiled=True)  38.8 us
    ppermute x6, waiting for transfers between devices, shifted(): return lax.ppermute(shard, axis, pairs)  31.3 us
    dot_general x6, matrix products, one_head(): jnp.einsum('qd,kd->qk', query_cols, key_cols, preferred_element_type=jnp....  20.2 us
    ppermute x6, starting transfers between devices, shifted(): return lax.ppermute(shard, axis, pairs)  13 us
    dot_general x6, matrix products, one_head(): jnp.dot(exp_scores.astype(jnp.bfloat16), value_cols, preferred_element_ty...  11.4 us
    unnamed x36, local copies, waits for them, and re-layouts  8.71 us
    dot_general x1, matrix products, shards(): jnp.einsum('jmrd,kmsd->mjrks', pieces, pieces, preferred_element_type=jnp...  7.08 us
    dot_general x3, matrix products, block_max(): jnp.einsum('qhd,khd->hqk', query_vectors.reshape(tokens_here, heads_here,...  6.13 us
  transfers between devices with their start and end apart: 9, of which 3 were waited for; matrix products, arithmetic and copies ran while one was open for 24% of the time, Pallas kernels for 0%

profile of v7, /device:TPU:1, one launch (start us, length us, event | category | flops | bytes accessed | tf_op | source)
XLA Modules:
  0.0 167.7 jit_solution(7953220683734372070)
XLA Ops:
  0.6 3.3 %broadcast_in_dim.54 = bf16[8,2,16,7168]{3,2,1,0:T(8,128)(2,1)} broadcast(bf16[2,16,7168]{2,1,0:T(8,128)(2,1)} %param.10), dimensions={1,2,3} | broadcast | bytes 4128768 | tf_op jit(solution)/shard_map/broadcast_in_dim | solution.py:42
  3.9 15.0 %all-to-all-start = ((bf16[8,2,16,7168]{3,2,1,0:T(8,128)(2,1)}), bf16[8,2,16,7168]{3,2,1,0:T(8,128)(2,1)}, u32[]{:S(2)}, u32[]{:S(2)}) async-start(bf16[8,2,16,7168]{3,2,1,0:T(8,128)(2,1)} %broadcast_in_dim.54), calls=%async_computation | async-start | bytes 7340032 | tf_op jit(solution)/shard_map/all_to_all | solution.py:43
  20.3 2.2 %collective-permute-start.1 = (bf16[480,768]{1,0:T(8,128)(2,1)}, bf16[480,768]{1,0:T(8,128)(2,1)}, u32[]{:S(2)}, u32[]{:S(2)}) collective-permute-start(bf16[480,768]{1,0:T(8,128)(2,1)} %param.8), channel_id=1, source_target_pairs={{0,8},{8,16},{16,24},{24,32},{32,40},{40,48},{48,56},{56,64},{64,7... | collective-permute-start | bytes 2211848 | tf_op jit(solution)/shard_map/ppermute | solution.py:28
  25.8 2.4 %select_reduce_fusion = f32[6]{0:T(128)S(1)} fusion(pred[480,480]{1,0:T(8,128)(4,1)S(1)} %and_and_fusion.3, bf16[480,6,128]{0,2,1:T(8,128)(2,1)S(1)} %bitcast.91, bf16[480,6,128]{0,2,1:T(8,128)(2,1)} %bitcast.96), kind=kOutput, calls=%fused_computation.4 | convolution fusion | flops 358041600 | bytes 1704984 | tf_op jit(solution)/shard_map/qhd,khd->hqk/dot_general | solution.py:91
  28.2 23.9 %collective-permute-done.2 = s32[480]{0:T(512)S(1)} collective-permute-done((s32[480]{0:T(512)S(1)}, s32[480]{0:T(512)S(1)}, u32[]{:S(2)}, u32[]{:S(2)}) %collective-permute-start.2) | collective-permute-done | bytes 1952 | tf_op jit(solution)/shard_map/ppermute | solution.py:28
  52.1 4.2 %collective-permute-start.3 = (bf16[480,768]{1,0:T(8,128)(2,1)S(1)}, bf16[480,768]{1,0:T(8,128)(2,1)S(1)}, u32[]{:S(2)}, u32[]{:S(2)}) collective-permute-start(bf16[480,768]{1,0:T(8,128)(2,1)S(1)} %collective-permute-done), channel_id=1, source_target_pairs={{0,8},{8,16},{16,24},{24,32},{32,40},{40,48},{48,56},{56,64},{64,7... | collective-permute-start | bytes 2211848 | tf_op jit(solution)/shard_map/ppermute | solution.py:28
  57.4 2.8 %collective-permute-start.4 = (bf16[480,768]{1,0:T(8,128)(2,1)}, bf16[480,768]{1,0:T(8,128)(2,1)}, u32[]{:S(2)}, u32[]{:S(2)}) collective-permute-start(bf16[480,768]{1,0:T(8,128)(2,1)} %collective-permute-done.1), channel_id=1, source_target_pairs={{0,8},{8,16},{16,24},{24,32},{32,40},{40,48},{48,56},{56,64},{64,7... | collective-permute-start | bytes 2211848 | tf_op jit(solution)/shard_map/ppermute | solution.py:28
  61.8 2.4 %fusion.1 = f32[6]{0:T(128)S(1)} fusion(pred[480,480]{1,0:T(8,128)(4,1)S(1)} %and_and_fusion.2, bf16[480,6,128]{0,2,1:T(8,128)(2,1)} %bitcast.95, bf16[480,6,128]{0,2,1:T(8,128)(2,1)S(1)} %bitcast.92), kind=kOutput, calls=%fused_computation.3 | convolution fusion | flops 358041600 | bytes 1704984 | tf_op jit(solution)/shard_map/qhd,khd->hqk/dot_general | solution.py:91
  64.2 7.1 %select_reduce_fusion.1 = (f32[2]{0:T(128)S(1)}, f32[2,8,16,8,16]{4,2,3,1,0:T(8,128)S(1)}) fusion(pred[8,16,8,16]{3,1,2,0:T(8,128)(4,1)S(1)} %broadcast_compare_fusion, bf16[8,2,16,7168]{3,2,1,0:T(8,128)(2,1)} %all-to-all-done), kind=kOutput, calls=%fused_computation.88 | convolution fusion | flops 469827584 | bytes 3817480 | tf_op jit(solution)/shard_map/jmrd,kmsd->mjrks/dot_general | solution.py:56
  77.0 2.8 %fusion.48 = bf16[2,128,896]{2,1,0:T(8,128)(2,1)} fusion(f32[2,128,8,16]{1,3,2,0:T(8,128)S(1)} %bitcast.97, f32[2]{0:T(128)S(1)} %get-tuple-element.21, bf16[8,2,16,7168]{3,2,1,0:T(8,128)(2,1)} %all-to-all-done, s32[]{:T(128)S(6)} %select_n.61), kind=kOutput, calls=%fused_computation.59 | convolution fusion | flops 353239040 | bytes 1048588 | tf_op jit(solution)/shard_map/mijr,jmrd->mid/dot_general | solution.py:72
  79.8 7.4 %collective-permute-done.5 = s32[480]{0:T(512)S(1)} collective-permute-done((s32[480]{0:T(512)S(1)}, s32[480]{0:T(512)S(1)}, u32[]{:S(2)}, u32[]{:S(2)}) %collective-permute-start.5) | collective-permute-done | bytes 1952 | tf_op jit(solution)/shard_map/ppermute | solution.py:28
  90.2 3.5 %fusion.131 = (f32[480]{0:T(512)S(1)}, f32[480,1440]{0,1:T(8,128)}) fusion(bf16[480,768]{1,0:T(8,128)(2,1)S(1)} %copy-done.11, bf16[1440,768]{1,0:T(8,128)(2,1)} %constant_dynamic-update-slice_fusion, pred[1440]{0:T(1024)(128)(4,1)S(1)} %broadcast_compare_fusion.1, s32[480]{0:T(512)S(1)} %get-tuple-element.38, s32[1440]{0:T(1024)S(1)} %iota_add_fusion, ...), kind=kOutput, calls=%fused_computation.142 | convolution fusion | flops 181785120 | bytes 3280768 | tf_op jit(solution)/shard_map/qd,kd->qk/dot_general | solution.py:125
  93.7 3.5 %fusion.132 = (f32[480]{0:T(512)S(1)}, f32[480,1440]{0,1:T(8,128)}) fusion(bf16[480,768]{1,0:T(8,128)(2,1)S(1)} %copy-done.11, bf16[1440,768]{1,0:T(8,128)(2,1)} %constant_dynamic-update-slice_fusion, pred[1440]{0:T(1024)(128)(4,1)S(1)} %broadcast_compare_fusion.1, s32[480]{0:T(512)S(1)} %get-tuple-element.38, s32[1440]{0:T(1024)S(1)} %iota_add_fusion, ...), kind=kOutput, calls=%fused_computation.143 | convolution fusion | flops 181785120 | bytes 3280768 | tf_op jit(solution)/shard_map/qd,kd->qk/dot_general | solution.py:125
  97.2 3.6 %fusion.133 = (f32[480]{0:T(512)S(1)}, f32[480,1440]{0,1:T(8,128)}) fusion(bf16[480,768]{1,0:T(8,128)(2,1)S(1)} %copy-done.11, bf16[1440,768]{1,0:T(8,128)(2,1)} %constant_dynamic-update-slice_fusion, pred[1440]{0:T(1024)(128)(4,1)S(1)} %broadcast_compare_fusion.1, s32[480]{0:T(512)S(1)} %get-tuple-element.38, s32[1440]{0:T(1024)S(1)} %iota_add_fusion, ...), kind=kOutput, calls=%fused_computation.144 | convolution fusion | flops 181785120 | bytes 3280768 | tf_op jit(solution)/shard_map/qd,kd->qk/dot_general | solution.py:125
  100.7 3.5 %fusion.134 = (f32[480]{0:T(512)S(1)}, f32[480,1440]{0,1:T(8,128)}) fusion(bf16[480,768]{1,0:T(8,128)(2,1)S(1)} %copy-done.11, bf16[1440,768]{1,0:T(8,128)(2,1)} %constant_dynamic-update-slice_fusion, pred[1440]{0:T(1024)(128)(4,1)S(1)} %broadcast_compare_fusion.1, s32[480]{0:T(512)S(1)} %get-tuple-element.38, s32[1440]{0:T(1024)S(1)} %iota_add_fusion, ...), kind=kOutput, calls=%fused_computation.145 | convolution fusion | flops 181785120 | bytes 3280768 | tf_op jit(solution)/shard_map/qd,kd->qk/dot_general | solution.py:125
  104.2 3.5 %fusion.135 = (f32[480]{0:T(512)S(1)}, f32[480,1440]{0,1:T(8,128)}) fusion(bf16[480,768]{1,0:T(8,128)(2,1)S(1)} %copy-done.11, bf16[1440,768]{1,0:T(8,128)(2,1)} %constant_dynamic-update-slice_fusion, pred[1440]{0:T(1024)(128)(4,1)S(1)} %broadcast_compare_fusion.1, s32[480]{0:T(512)S(1)} %get-tuple-element.38, s32[1440]{0:T(1024)S(1)} %iota_add_fusion, ...), kind=kOutput, calls=%fused_computation.146 | convolution fusion | flops 181785120 | bytes 3280768 | tf_op jit(solution)/shard_map/qd,kd->qk/dot_general | solution.py:125
  107.7 2.7 %fusion.136 = (f32[480]{0:T(512)S(1)}, f32[480,1440]{0,1:T(8,128)S(1)}) fusion(bf16[480,768]{1,0:T(8,128)(2,1)} %param.6, bf16[1440,768]{1,0:T(8,128)(2,1)} %constant_dynamic-update-slice_fusion, pred[1440]{0:T(1024)(128)(4,1)S(1)} %broadcast_compare_fusion.1, s32[480]{0:T(512)S(1)} %get-tuple-element.38, s32[1440]{0:T(1024)S(1)} %iota_add_fusion, ...), kind=kOutput, calls=%fused_computation.147 | convolution fusion | flops 181785120 | bytes 3275040 | tf_op jit(solution)/shard_map/qd,kd->qk/dot_general | solution.py:125
  110.3 2.3 %copy.101 = bf16[480,768]{0,1:T(8,128)(2,1)} copy(bf16[480,768]{1,0:T(8,128)(2,1)} %copy-done.6) | data formatting | bytes 1474560 | tf_op jit(solution)/shard_map/optimization_barrier | solution.py:104
  112.7 2.2 %constant_dynamic-update-slice_fusion.5 = bf16[1440,768]{1,0:T(8,128)(2,1)} fusion(bf16[480,768]{1,0:T(8,128)(2,1)} %collective-permute-done.4), kind=kLoop, calls=%fused_computation.122 | loop fusion | bytes 1474560
  114.8 2.0 %constant_dynamic-update-slice_fusion.4 = bf16[1440,768]{1,0:T(8,128)(2,1)} fusion(bf16[1440,768]{1,0:T(8,128)(2,1)} %constant_dynamic-update-slice_fusion.5, bf16[480,768]{1,0:T(8,128)(2,1)} %collective-permute-done.1), kind=kLoop, calls=%fused_computation.121 | loop fusion | bytes 1474560
  116.9 2.0 %constant_dynamic-update-slice_fusion.3 = bf16[1440,768]{1,0:T(8,128)(2,1)} fusion(bf16[1440,768]{1,0:T(8,128)(2,1)} %constant_dynamic-update-slice_fusion.4, bf16[480,768]{1,0:T(8,128)(2,1)} %param.8), kind=kLoop, calls=%fused_computation.120 | loop fusion | bytes 1474560 | tf_op jit(solution)/shard_map/concatenate | solution.py:109
  121.2 17.5 %all-to-all-start.1 = ((f32[96,1,6]{2,1,0:T(1,128)}), f32[96,1,6]{2,1,0:T(1,128)S(1)}, u32[]{:S(2)}, u32[]{:S(2)}) async-start(f32[96,1,6]{2,1,0:T(1,128)} %broadcast_in_dim.59), calls=%async_computation.1 | async-start | bytes 98304 | tf_op jit(solution)/shard_map/all_to_all | solution.py:43
  138.7 2.5 %fusion.17 = f32[480]{0:T(512)S(1)} fusion(f32[480,1440]{0,1:T(8,128)} %get-tuple-element.26, f32[480]{0:T(512)S(1)} %get-tuple-element.25), kind=kLoop, calls=%fused_computation.33 | loop fusion | flops 1381920 | bytes 2768640 | tf_op jit(solution)/shard_map/reduce_sum | solution.py:131
  141.4 1.6 fusion.85
  143.5 1.9 %fusion.88 = bf16[480,768]{1,0:T(8,128)(2,1)S(1)} fusion(bf16[480,768]{1,0:T(8,128)(2,1)S(1)} %fusion.85, f32[480,1440]{0,1:T(8,128)S(1)} %copy-done.3, f32[480]{0:T(512)S(1)} %get-tuple-element.27, bf16[1440,768]{1,0:T(8,128)(2,1)} %constant_dynamic-update-slice_fusion.3, f32[480]{0:T(512)S(1)} %fusion.19), kind=kOutput, calls=%fused_computation.73 | convolution fusion | flops 178452480 | bytes 3444736 | tf_op jit(solution)/shard_map/dot_general | solution.py:133
  146.0 1.9 %fusion.91 = bf16[480,768]{1,0:T(8,128)(2,1)S(1)} fusion(bf16[480,768]{1,0:T(8,128)(2,1)S(1)} %fusion.88, f32[480,1440]{0,1:T(8,128)S(1)} %copy-done.2, f32[480]{0:T(512)S(1)} %get-tuple-element.29, bf16[1440,768]{1,0:T(8,128)(2,1)} %constant_dynamic-update-slice_fusion.3, f32[480]{0:T(512)S(1)} %fusion.21), kind=kOutput, calls=%fused_computation.74 | convolution fusion | flops 178452480 | bytes 3444736 | tf_op jit(solution)/shard_map/dot_general | solution.py:133
  148.4 1.9 %fusion.94 = bf16[480,768]{1,0:T(8,128)(2,1)S(1)} fusion(bf16[480,768]{1,0:T(8,128)(2,1)S(1)} %fusion.91, f32[480,1440]{0,1:T(8,128)S(1)} %copy-done.1, f32[480]{0:T(512)S(1)} %get-tuple-element.31, bf16[1440,768]{1,0:T(8,128)(2,1)} %constant_dynamic-update-slice_fusion.3, f32[480]{0:T(512)S(1)} %fusion.23), kind=kOutput, calls=%fused_computation.75 | convolution fusion | flops 178452480 | bytes 3444736 | tf_op jit(solution)/shard_map/dot_general | solution.py:133
  150.8 1.7 %fusion.97 = bf16[480,768]{1,0:T(8,128)(2,1)S(1)} fusion(bf16[480,768]{1,0:T(8,128)(2,1)S(1)} %fusion.94, f32[480,1440]{0,1:T(8,128)S(1)} %copy-done, f32[480]{0:T(512)S(1)} %get-tuple-element.33, bf16[1440,768]{1,0:T(8,128)(2,1)} %constant_dynamic-update-slice_fusion.3, f32[480]{0:T(512)S(1)} %fusion.25), kind=kOutput, calls=%fused_computation.76 | convolution fusion | flops 178452480 | bytes 3444736 | tf_op jit(solution)/shard_map/dot_general | solution.py:133
  154.6 6.3 %all-to-all-start.2 = ((f32[8,1,6]{2,1,0:T(1,128)}), f32[8,1,6]{2,1,0:T(1,128)S(1)}, u32[]{:S(2)}, u32[]{:S(2)}) async-start(f32[8,1,6]{2,1,0:T(1,128)} %broadcast_in_dim.60), calls=%async_computation.2 | async-start | bytes 8192 | tf_op jit(solution)/shard_map/all_to_all | solution.py:43
  160.9 2.3 %fusion.100 = bf16[480,768]{1,0:T(8,128)(2,1)} fusion(bf16[480,768]{1,0:T(8,128)(2,1)} %copy-done.14, f32[480,1440]{0,1:T(8,128)S(1)} %get-tuple-element.36, f32[480]{0:T(512)S(1)} %get-tuple-element.35, bf16[1440,768]{1,0:T(8,128)(2,1)} %constant_dynamic-update-slice_fusion.3, f32[480]{0:T(512)S(1)} %fusion.27), kind=kOutput, calls=%fused_computation.77 | convolution fusion | flops 178452480 | bytes 3260160 | tf_op jit(solution)/shard_map/dot_general | solution.py:133
  163.2 2.2 %all-to-all-done.2 = f32[8,1,6]{2,1,0:T(1,128)S(1)} async-done(((f32[8,1,6]{2,1,0:T(1,128)}), f32[8,1,6]{2,1,0:T(1,128)S(1)}, u32[]{:S(2)}, u32[]{:S(2)}) %all-to-all-start.2) | async-done | bytes 224 | tf_op jit(solution)/shard_map/all_to_all | solution.py:43
  165.7 2.0 %multiply_convert_fusion = bf16[2,128,896]{2,1,0:T(8,128)(2,1)} fusion(bf16[2,128,896]{2,1,0:T(8,128)(2,1)} %fusion.48, bf16[2,128,896]{2,1,0:T(8,128)(2,1)S(1)} %copy-done.12, f32[2]{0:T(128)S(1)} %compare_select_fusion.1), kind=kLoop, calls=%fused_computation.93 | loop fusion | flops 1605632 | bytes 1376264 | tf_op jit(solution)/shard_map/convert_element_type | solution.py:150
  (94 shorter events, 22.6 us)
Async XLA Ops:
  3.9 15.0 %copy-start.5 = (bf16[480,768]{1,0:T(8,128)(2,1)S(1)}, bf16[480,768]{1,0:T(8,128)(2,1)}, u32[]{:S(2)}) copy-start(bf16[480,768]{1,0:T(8,128)(2,1)} %param.7) | copy-start | bytes 2211844
  3.9 18.5 %copy-start.13 = (s32[480]{0:T(512)S(1)}, s32[480]{0:T(512)}, u32[]{:S(2)}) copy-start(s32[480]{0:T(512)} %param.9) | copy-start | bytes 5764
  3.9 21.3 %copy-start.10 = (bf16[480,768]{1,0:T(8,128)(2,1)S(1)}, bf16[480,768]{1,0:T(8,128)(2,1)}, u32[]{:S(2)}) copy-start(bf16[480,768]{1,0:T(8,128)(2,1)} %param.6) | copy-start | bytes 2211844
  3.9 60.3 %all-to-all-start = ((bf16[8,2,16,7168]{3,2,1,0:T(8,128)(2,1)}), bf16[8,2,16,7168]{3,2,1,0:T(8,128)(2,1)}, u32[]{:S(2)}, u32[]{:S(2)}) async-start(bf16[8,2,16,7168]{3,2,1,0:T(8,128)(2,1)} %broadcast_in_dim.54), calls=%async_computation | async-start | bytes 7340032 | tf_op jit(solution)/shard_map/all_to_all | solution.py:43
  18.9 33.1 %collective-permute-start = (bf16[480,768]{1,0:T(8,128)(2,1)S(1)}, bf16[480,768]{1,0:T(8,128)(2,1)S(1)}, u32[]{:S(2)}, u32[]{:S(2)}) collective-permute-start(bf16[480,768]{1,0:T(8,128)(2,1)S(1)} %copy-done.5), channel_id=1, source_target_pairs={{0,8},{8,16},{16,24},{24,32},{32,40},{40,48},{48,56},{56,64},{64,7... | collective-permute-start | bytes 2211848 | tf_op jit(solution)/shard_map/ppermute | solution.py:28
  20.3 31.8 %collective-permute-start.1 = (bf16[480,768]{1,0:T(8,128)(2,1)}, bf16[480,768]{1,0:T(8,128)(2,1)}, u32[]{:S(2)}, u32[]{:S(2)}) collective-permute-start(bf16[480,768]{1,0:T(8,128)(2,1)} %param.8), channel_id=1, source_target_pairs={{0,8},{8,16},{16,24},{24,32},{32,40},{40,48},{48,56},{56,64},{64,7... | collective-permute-start | bytes 2211848 | tf_op jit(solution)/shard_map/ppermute | solution.py:28
  22.4 29.7 %collective-permute-start.2 = (s32[480]{0:T(512)S(1)}, s32[480]{0:T(512)S(1)}, u32[]{:S(2)}, u32[]{:S(2)}) collective-permute-start(s32[480]{0:T(512)S(1)} %copy-done.13), channel_id=1, source_target_pairs={{0,8},{8,16},{16,24},{24,32},{32,40},{40,48},{48,56},{56,64},{64,7... | collective-permute-start | bytes 5768 | tf_op jit(solution)/shard_map/ppermute | solution.py:28
  25.4 36.3 %copy-start.7 = (bf16[480,768]{0,1:T(8,128)(2,1)}, bf16[480,768]{0,1:T(8,128)(2,1)S(1)}, u32[]{:S(2)}) copy-start(bf16[480,768]{0,1:T(8,128)(2,1)S(1)} %copy.87) | copy-start | bytes 2211844
  52.1 35.2 %collective-permute-start.3 = (bf16[480,768]{1,0:T(8,128)(2,1)S(1)}, bf16[480,768]{1,0:T(8,128)(2,1)S(1)}, u32[]{:S(2)}, u32[]{:S(2)}) collective-permute-start(bf16[480,768]{1,0:T(8,128)(2,1)S(1)} %collective-permute-done), channel_id=1, source_target_pairs={{0,8},{8,16},{16,24},{24,32},{32,40},{40,48},{48,56},{56,64},{64,7... | collective-permute-start | bytes 2211848 | tf_op jit(solution)/shard_map/ppermute | solution.py:28
  57.4 29.8 %collective-permute-start.4 = (bf16[480,768]{1,0:T(8,128)(2,1)}, bf16[480,768]{1,0:T(8,128)(2,1)}, u32[]{:S(2)}, u32[]{:S(2)}) collective-permute-start(bf16[480,768]{1,0:T(8,128)(2,1)} %collective-permute-done.1), channel_id=1, source_target_pairs={{0,8},{8,16},{16,24},{24,32},{32,40},{40,48},{48,56},{56,64},{64,7... | collective-permute-start | bytes 2211848 | tf_op jit(solution)/shard_map/ppermute | solution.py:28
  60.2 27.1 %collective-permute-start.5 = (s32[480]{0:T(512)S(1)}, s32[480]{0:T(512)S(1)}, u32[]{:S(2)}, u32[]{:S(2)}) collective-permute-start(s32[480]{0:T(512)S(1)} %collective-permute-done.2), channel_id=1, source_target_pairs={{0,8},{8,16},{16,24},{24,32},{32,40},{40,48},{48,56},{56,64},{64,7... | collective-permute-start | bytes 5768 | tf_op jit(solution)/shard_map/ppermute | solution.py:28
  79.8 10.4 %copy-start.11 = (bf16[480,768]{1,0:T(8,128)(2,1)S(1)}, bf16[480,768]{1,0:T(8,128)(2,1)}, u32[]{:S(2)}) copy-start(bf16[480,768]{1,0:T(8,128)(2,1)} %param.6) | copy-start | bytes 2211844
  87.2 13.5 %copy-start.6 = (bf16[480,768]{1,0:T(8,128)(2,1)}, bf16[480,768]{1,0:T(8,128)(2,1)S(1)}, u32[]{:S(2)}) copy-start(bf16[480,768]{1,0:T(8,128)(2,1)S(1)} %collective-permute-done.3) | copy-start | bytes 2211844
  112.7 6.5 %copy-start.8 = (bf16[480,768]{0,1:T(8,128)(2,1)S(1)}, bf16[480,768]{0,1:T(8,128)(2,1)}, u32[]{:S(2)}) copy-start(bf16[480,768]{0,1:T(8,128)(2,1)} %copy-done.7) | copy-start | bytes 2211844
  112.7 6.6 %copy-start.9 = (bf16[480,768]{0,1:T(8,128)(2,1)S(1)}, bf16[480,768]{0,1:T(8,128)(2,1)}, u32[]{:S(2)}) copy-start(bf16[480,768]{0,1:T(8,128)(2,1)} %copy.101) | copy-start | bytes 2211844
  121.2 32.7 %all-to-all-start.1 = ((f32[96,1,6]{2,1,0:T(1,128)}), f32[96,1,6]{2,1,0:T(1,128)S(1)}, u32[]{:S(2)}, u32[]{:S(2)}) async-start(f32[96,1,6]{2,1,0:T(1,128)} %broadcast_in_dim.59), calls=%async_computation.1 | async-start | bytes 98304 | tf_op jit(solution)/shard_map/all_to_all | solution.py:43
  138.7 2.7 %copy-start.4 = (f32[480,1440]{0,1:T(8,128)S(1)}, f32[480,1440]{0,1:T(8,128)}, u32[]{:S(2)}) copy-start(f32[480,1440]{0,1:T(8,128)} %get-tuple-element.26) | copy-start | bytes 8294404
  138.7 4.4 %copy-start.3 = (f32[480,1440]{0,1:T(8,128)S(1)}, f32[480,1440]{0,1:T(8,128)}, u32[]{:S(2)}) copy-start(f32[480,1440]{0,1:T(8,128)} %get-tuple-element.28) | copy-start | bytes 8294404
  143.0 2.4 %copy-start.2 = (f32[480,1440]{0,1:T(8,128)S(1)}, f32[480,1440]{0,1:T(8,128)}, u32[]{:S(2)}) copy-start(f32[480,1440]{0,1:T(8,128)} %get-tuple-element.30) | copy-start | bytes 8294404
  145.5 2.4 %copy-start.1 = (f32[480,1440]{0,1:T(8,128)S(1)}, f32[480,1440]{0,1:T(8,128)}, u32[]{:S(2)}) copy-start(f32[480,1440]{0,1:T(8,128)} %get-tuple-element.32) | copy-start | bytes 8294404
  147.9 2.4 %copy-start = (f32[480,1440]{0,1:T(8,128)S(1)}, f32[480,1440]{0,1:T(8,128)}, u32[]{:S(2)}) copy-start(f32[480,1440]{0,1:T(8,128)} %get-tuple-element.34) | copy-start | bytes 8294404
  152.5 0.9 copy-start.14
  153.4 12.4 %copy-start.12 = (bf16[2,128,896]{2,1,0:T(8,128)(2,1)S(1)}, bf16[2,128,896]{2,1,0:T(8,128)(2,1)}, u32[]{:S(2)}) copy-start(bf16[2,128,896]{2,1,0:T(8,128)(2,1)} %param.11) | copy-start | bytes 1376260
  154.6 10.8 %all-to-all-start.2 = ((f32[8,1,6]{2,1,0:T(1,128)}), f32[8,1,6]{2,1,0:T(1,128)S(1)}, u32[]{:S(2)}, u32[]{:S(2)}) async-start(f32[8,1,6]{2,1,0:T(1,128)} %broadcast_in_dim.60), calls=%async_computation.2 | async-start | bytes 8192 | tf_op jit(solution)/shard_map/all_to_all | solution.py:43

commit v8 on v7

--- a/solution.py
+++ b/solution.py
@@ -117,25 +117,33 @@
         & (key_place[None, :] >= 0)
     )
 
-    def one_head(head_slot):
-        col_start = head_slot * HD
-        query_cols = lax.dynamic_slice_in_dim(query_vectors, col_start, HD, 1)
-        key_cols = lax.dynamic_slice_in_dim(keys_all, col_start, HD, 1)
-        value_cols = lax.dynamic_slice_in_dim(values_all, col_start, HD, 1)
+    group = 2 if heads_here % 2 == 0 else 1
+
+    def head_group(group_index):
+        col_start = group_index * (group * HD)
+        query_cols = lax.dynamic_slice_in_dim(query_vectors, col_start, group * HD, 1)
+        key_cols = lax.dynamic_slice_in_dim(keys_all, col_start, group * HD, 1)
+        value_cols = lax.dynamic_slice_in_dim(values_all, col_start, group * HD, 1)
         scores = jnp.einsum(
-            "qd,kd->qk", query_cols, key_cols, preferred_element_type=jnp.float32
+            "qhd,khd->hqk",
+            query_cols.reshape(tokens_here, group, HD),
+            key_cols.reshape(-1, group, HD),
+            preferred_element_type=jnp.float32,
         ) / math.sqrt(HD)
-        masked = jnp.where(same_doc, scores, masked_fill)
-        row_max = jnp.max(masked, axis=1)
-        exp_scores = jnp.exp(masked - row_max[:, None])
-        row_total = jnp.sum(exp_scores, axis=1)
-        mixed_rows = (
-            jnp.dot(exp_scores.astype(jnp.bfloat16), value_cols, preferred_element_type=jnp.float32)
-            / row_total[:, None]
-        )
-        return (mixed_rows.astype(jnp.bfloat16), jnp.max(row_max))
+        masked = jnp.where(same_doc[None], scores, masked_fill)
+        row_max = jnp.max(masked, axis=2)
+        exp_scores = jnp.exp(masked - row_max[:, :, None])
+        row_total = jnp.sum(exp_scores, axis=2)
+        mixed_rows = jnp.einsum(
+            "hqk,khd->qhd",
+            exp_scores.astype(jnp.bfloat16),
+            value_cols.reshape(-1, group, HD),
+            preferred_element_type=jnp.float32,
+        ) / jnp.transpose(row_total)[:, :, None]
+        return mixed_rows.astype(jnp.bfloat16).reshape(tokens_here, group * HD)
 
-    attention_out = jnp.concatenate([one_head(slot)[0] for slot in range(heads_here)], axis=1)
+    mixed_groups = lax.map(head_group, jnp.arange(heads_here // group, dtype=jnp.int32))
+    attention_out = jnp.transpose(mixed_groups, (1, 0, 2)).reshape(tokens_here, heads_here * HD)
     heads_all = heads_here * head_count
     head_slots = jnp.arange(heads_all, dtype=jnp.int32)
     seq_max = jnp.max(gathered(head_max, "seq"), axis=0)

time: 169 us -> 158 us (0.935)
  matrix products: 52.5 us -> 33.8 us
  other arithmetic: 8.3 us -> 15.2 us
  waiting for transfers between devices: 33.5 us -> 31.2 us
  loops' own time: 0 us -> 2.17 us
    dot_general x12 -> x6, matrix products: 31.5 us -> 12 us  [the longest x3 7.46 us: head_group(): jnp.einsum('qhd,khd->hqk', query_cols.reshape(tokens_here, group, HD), ke...]
    unnamed x36 -> x17, local copies, waits for them, and re-layouts: 8.71 us -> 2.83 us
    while x0 -> x3, local copies, waits for them, and re-layouts: none -> 4.19 us
    concatenate x0 -> x1, other arithmetic: none -> 3.36 us  [shards(): values_all = jnp.concatenate([member[1] for member in ordered], axis=0)]
    concatenate x2 -> x0, local copies, waits for them, and re-layouts: 2.96 us -> none  [the longest x1 2.04 us: shards(): values_all = jnp.concatenate([member[1] for member in ordered], axis=0)]
    and x0 -> x3, other arithmetic: none -> 2.23 us  [shards(): (doc_ids[:, None] == docs_all[None, :]) & (key_place[None, :] <= query_pl...]
    another operation x0 -> x1, loops' own time: none -> 2.17 us  [shards(): lax.map(head_group, jnp.arange(heads_here // group, dtype=jnp.int32))]
    dynamic_update_slice x0 -> x3, local copies, waits for them, and re-layouts: none -> 2.15 us  [shards(): lax.map(head_group, jnp.arange(heads_here // group, dtype=jnp.int32))]
  transfers between devices with their start and end apart: 9 -> 9, of which waited for: 3 -> 3; matrix products, arithmetic and copies ran while one was open for 24% -> 39% of each run, Pallas kernels for 0% -> 0%
where the time goes in v8:
time: 158 us; the launch traced here: 157 us
  starting transfers between devices  52.8 us (33%)
  matrix products  33.8 us (21%)
  waiting for transfers between devices  31.2 us (20%)
  local copies, waits for them, and re-layouts  21.1 us (13%)
  other arithmetic  15.2 us (10%)
  loops' own time  2.17 us (1%)
    all_to_all x3, starting transfers between devices, gathered(): return lax.all_to_all(spread, axis, 0, 0, tiled=True)  39 us
    ppermute x6, waiting for transfers between devices, shifted(): return lax.ppermute(shard, axis, pairs)  29.3 us
    ppermute x6, starting transfers between devices, shifted(): return lax.ppermute(shard, axis, pairs)  13.7 us
    dot_general x3, matrix products, head_group(): jnp.einsum('qhd,khd->hqk', query_cols.reshape(tokens_here, group, HD), ke...  7.46 us
    dot_general x1, matrix products, shards(): jnp.einsum('jmrd,kmsd->mjrks', pieces, pieces, preferred_element_type=jnp...  7.18 us
    reduce_sum x3, other arithmetic, head_group(): row_total = jnp.sum(exp_scores, axis=2)  5.47 us
    dot_general x3, matrix products, block_max(): jnp.einsum('qhd,khd->hqk', query_vectors.reshape(tokens_here, heads_here,...  5 us
    broadcast_in_dim x3, local copies, waits for them, and re-layouts, gathered(): spread = jnp.broadcast_to(values[None], (size,) + values.shape)  4.53 us
  transfers between devices with their start and end apart: 9, of which 3 were waited for; matrix products, arithmetic and copies ran while one was open for 39% of the time, Pallas kernels for 0%

profile of v8, /device:TPU:1, one launch (start us, length us, event | category | flops | bytes accessed | tf_op | source)
XLA Modules:
  0.0 157.3 jit_solution(200039187052247088)
XLA Ops:
  0.6 3.3 %broadcast_in_dim.67 = bf16[8,2,16,7168]{3,2,1,0:T(8,128)(2,1)} broadcast(bf16[2,16,7168]{2,1,0:T(8,128)(2,1)} %param.12), dimensions={1,2,3} | broadcast | bytes 4128768 | tf_op jit(solution)/shard_map/broadcast_in_dim | solution.py:42
  3.9 15.0 %all-to-all-start = ((bf16[8,2,16,7168]{3,2,1,0:T(8,128)(2,1)}), bf16[8,2,16,7168]{3,2,1,0:T(8,128)(2,1)}, u32[]{:S(2)}, u32[]{:S(2)}) async-start(bf16[8,2,16,7168]{3,2,1,0:T(8,128)(2,1)} %broadcast_in_dim.67), calls=%async_computation | async-start | bytes 7340032 | tf_op jit(solution)/shard_map/all_to_all | solution.py:43
  20.3 2.2 %collective-permute-start.1 = (bf16[480,768]{1,0:T(8,128)(2,1)}, bf16[480,768]{1,0:T(8,128)(2,1)}, u32[]{:S(2)}, u32[]{:S(2)}) collective-permute-start(bf16[480,768]{1,0:T(8,128)(2,1)} %param.10), channel_id=1, source_target_pairs={{0,8},{8,16},{16,24},{24,32},{32,40},{40,48},{48,56},{56,64},{64,7... | collective-permute-start | bytes 2211848 | tf_op jit(solution)/shard_map/ppermute | solution.py:28
  25.0 1.4 copy.116
  28.1 24.0 %collective-permute-done.2 = s32[480]{0:T(512)S(1)} collective-permute-done((s32[480]{0:T(512)S(1)}, s32[480]{0:T(512)S(1)}, u32[]{:S(2)}, u32[]{:S(2)}) %collective-permute-start.2) | collective-permute-done | bytes 1952 | tf_op jit(solution)/shard_map/ppermute | solution.py:28
  53.3 4.2 %collective-permute-start.3 = (bf16[480,768]{1,0:T(8,128)(2,1)S(1)}, bf16[480,768]{1,0:T(8,128)(2,1)S(1)}, u32[]{:S(2)}, u32[]{:S(2)}) collective-permute-start(bf16[480,768]{1,0:T(8,128)(2,1)S(1)} %collective-permute-done), channel_id=1, source_target_pairs={{0,8},{8,16},{16,24},{24,32},{32,40},{40,48},{48,56},{56,64},{64,7... | collective-permute-start | bytes 2211848 | tf_op jit(solution)/shard_map/ppermute | solution.py:28
  57.5 1.9 %collective-permute-start.5 = (s32[480]{0:T(512)S(1)}, s32[480]{0:T(512)S(1)}, u32[]{:S(2)}, u32[]{:S(2)}) collective-permute-start(s32[480]{0:T(512)S(1)} %collective-permute-done.2), channel_id=1, source_target_pairs={{0,8},{8,16},{16,24},{24,32},{32,40},{40,48},{48,56},{56,64},{64,7... | collective-permute-start | bytes 5768 | tf_op jit(solution)/shard_map/ppermute | solution.py:28
  59.4 2.8 %collective-permute-start.4 = (bf16[480,768]{1,0:T(8,128)(2,1)}, bf16[480,768]{1,0:T(8,128)(2,1)}, u32[]{:S(2)}, u32[]{:S(2)}) collective-permute-start(bf16[480,768]{1,0:T(8,128)(2,1)} %collective-permute-done.1), channel_id=1, source_target_pairs={{0,8},{8,16},{16,24},{24,32},{32,40},{40,48},{48,56},{56,64},{64,7... | collective-permute-start | bytes 2211848 | tf_op jit(solution)/shard_map/ppermute | solution.py:28
  62.5 2.4 %fusion.27 = f32[6]{0:T(128)S(1)} fusion(pred[480,480]{1,0:T(8,128)(4,1)S(1)} %and_and_fusion.2, bf16[480,6,128]{0,2,1:T(8,128)(2,1)} %bitcast.118, bf16[480,6,128]{0,2,1:T(8,128)(2,1)S(1)} %bitcast.116), kind=kOutput, calls=%fused_computation.28 | convolution fusion | flops 358041600 | bytes 1704984 | tf_op jit(solution)/shard_map/qhd,khd->hqk/dot_general | solution.py:91
  65.0 7.2 %select_reduce_fusion.1 = (f32[2]{0:T(128)S(1)}, f32[2,8,16,8,16]{4,2,3,1,0:T(8,128)S(1)}) fusion(pred[8,16,8,16]{3,1,2,0:T(8,128)(4,1)} %broadcast_compare_fusion, bf16[8,2,16,7168]{3,2,1,0:T(8,128)(2,1)} %all-to-all-done), kind=kOutput, calls=%fused_computation.48 | convolution fusion | flops 469827584 | bytes 3817480 | tf_op jit(solution)/shard_map/jmrd,kmsd->mjrks/dot_general | solution.py:56
  73.5 1.4 fusion.37
  80.5 2.8 %fusion.32 = bf16[2,128,896]{2,1,0:T(8,128)(2,1)} fusion(f32[2,128,8,16]{1,3,2,0:T(8,128)S(1)} %bitcast.122, f32[2]{0:T(128)S(1)} %get-tuple-element.129, bf16[8,2,16,7168]{3,2,1,0:T(8,128)(2,1)} %all-to-all-done, s32[]{:T(128)S(6)} %select_n.51), kind=kOutput, calls=%fused_computation.37 | convolution fusion | flops 353239040 | bytes 1048588 | tf_op jit(solution)/shard_map/mijr,jmrd->mid/dot_general | solution.py:72
  83.3 5.2 %collective-permute-done.4 = bf16[480,768]{1,0:T(8,128)(2,1)} collective-permute-done((bf16[480,768]{1,0:T(8,128)(2,1)}, bf16[480,768]{1,0:T(8,128)(2,1)}, u32[]{:S(2)}, u32[]{:S(2)}) %collective-permute-start.4) | collective-permute-done | bytes 737312 | tf_op jit(solution)/shard_map/ppermute | solution.py:28
  91.1 17.7 %all-to-all-start.1 = ((f32[96,1,6]{2,1,0:T(1,128)}), f32[96,1,6]{2,1,0:T(1,128)S(1)}, u32[]{:S(2)}, u32[]{:S(2)}) async-start(f32[96,1,6]{2,1,0:T(1,128)} %broadcast_in_dim.71), calls=%async_computation.1 | async-start | bytes 98304 | tf_op jit(solution)/shard_map/all_to_all | solution.py:43
  108.8 3.4 %pad_maximum_fusion = (bf16[1440,768]{1,0:T(8,128)(2,1)S(1)}, bf16[1440,768]{1,0:T(8,128)(2,1)}) fusion(bf16[480,768]{1,0:T(8,128)(2,1)} %param.10, bf16[480,768]{1,0:T(8,128)(2,1)} %collective-permute-done.1, bf16[480,768]{1,0:T(8,128)(2,1)} %collective-permute-done.4, bf16[480,768]{1,0:T(8,128)(2,1)S(1)} %copy-done, bf16[480,768]{1,0:T(8,128)(2,1)} %copy-done.1, ...), kind=kLoop, calls=%fused_computation.33 | loop fusion | flops 13271040 | bytes 8847360 | tf_op jit(solution)/shard_map/concatenate | solution.py:109
  112.2 31.2 %while.11 = (s32[]{:T(128)}, bf16[3,480,256]{2,1,0:T(8,128)(2,1)}, s32[3]{0:T(128)S(1)}, bf16[1440,768]{1,0:T(8,128)(2,1)S(1)}, bf16[480,768]{1,0:T(8,128)(2,1)}...) while((s32[]{:T(128)}, bf16[3,480,256]{2,1,0:T(8,128)(2,1)}, ...), condition=%wide.region_6.7_spmd.clone, body=%wide.region_3.6_spmd.clone.sunk | while | flops 726003840 | bytes 25780080 | solution.py:145
  113.5 1.4 dynamic-slice_bitcast_fusion.8
  115.7 2.5 %fusion.101 = (f32[2,480]{1,0:T(2,128)S(1)}, f32[2,480,1440]{2,1,0:T(8,128)S(1)}) fusion(pred[480,1440]{1,0:T(8,128)(4,1)S(1)} %and_and_fusion.5, bf16[180,2,8,128]{3,2,1,0:T(8,128)(2,1)S(1)} %get-tuple-element.206, bf16[480,768]{1,0:T(8,128)(2,1)} %get-tuple-element.244, s32[]{:T(128)S(6)} %select_n.90), kind=kOutput, calls=%fused_computation.3.clone.1 | convolution fusion | flops 358040640 | bytes 7207684 | tf_op jit(solution)/shard_map/while/body/eval_jaxpr/qhd,khd->hqk/dot_general | solution.py:127
  118.1 1.8 %fusion.102 = f32[2,480]{1,0:T(2,128)S(1)} fusion(f32[2,480,1440]{2,1,0:T(8,128)S(1)} %get-tuple-element.207, f32[2,480]{1,0:T(2,128)S(1)} %get-tuple-element.208, pred[480,1440]{1,0:T(8,128)(4,1)S(1)} %and_and_fusion.5), kind=kLoop, calls=%fused_computation.4.clone.1 | loop fusion | flops 5528640 | bytes 6228480 | tf_op jit(solution)/shard_map/while/body/eval_jaxpr/reduce_sum | solution.py:136
  120.0 1.5 fusion.103
  123.9 1.4 dynamic-slice_bitcast_fusion.8
  126.1 2.5 %fusion.101 = (f32[2,480]{1,0:T(2,128)S(1)}, f32[2,480,1440]{2,1,0:T(8,128)S(1)}) fusion(pred[480,1440]{1,0:T(8,128)(4,1)S(1)} %and_and_fusion.5, bf16[180,2,8,128]{3,2,1,0:T(8,128)(2,1)S(1)} %get-tuple-element.206, bf16[480,768]{1,0:T(8,128)(2,1)} %get-tuple-element.244, s32[]{:T(128)S(6)} %select_n.90), kind=kOutput, calls=%fused_computation.3.clone.1 | convolution fusion | flops 358040640 | bytes 7207684 | tf_op jit(solution)/shard_map/while/body/eval_jaxpr/qhd,khd->hqk/dot_general | solution.py:127
  128.5 1.8 %fusion.102 = f32[2,480]{1,0:T(2,128)S(1)} fusion(f32[2,480,1440]{2,1,0:T(8,128)S(1)} %get-tuple-element.207, f32[2,480]{1,0:T(2,128)S(1)} %get-tuple-element.208, pred[480,1440]{1,0:T(8,128)(4,1)S(1)} %and_and_fusion.5), kind=kLoop, calls=%fused_computation.4.clone.1 | loop fusion | flops 5528640 | bytes 6228480 | tf_op jit(solution)/shard_map/while/body/eval_jaxpr/reduce_sum | solution.py:136
  130.4 1.5 fusion.103
  134.3 1.4 dynamic-slice_bitcast_fusion.8
  136.5 2.5 %fusion.101 = (f32[2,480]{1,0:T(2,128)S(1)}, f32[2,480,1440]{2,1,0:T(8,128)S(1)}) fusion(pred[480,1440]{1,0:T(8,128)(4,1)S(1)} %and_and_fusion.5, bf16[180,2,8,128]{3,2,1,0:T(8,128)(2,1)S(1)} %get-tuple-element.206, bf16[480,768]{1,0:T(8,128)(2,1)} %get-tuple-element.244, s32[]{:T(128)S(6)} %select_n.90), kind=kOutput, calls=%fused_computation.3.clone.1 | convolution fusion | flops 358040640 | bytes 7207684 | tf_op jit(solution)/shard_map/while/body/eval_jaxpr/qhd,khd->hqk/dot_general | solution.py:127
  138.9 1.8 %fusion.102 = f32[2,480]{1,0:T(2,128)S(1)} fusion(f32[2,480,1440]{2,1,0:T(8,128)S(1)} %get-tuple-element.207, f32[2,480]{1,0:T(2,128)S(1)} %get-tuple-element.208, pred[480,1440]{1,0:T(8,128)(4,1)S(1)} %and_and_fusion.5), kind=kLoop, calls=%fused_computation.4.clone.1 | loop fusion | flops 5528640 | bytes 6228480 | tf_op jit(solution)/shard_map/while/body/eval_jaxpr/reduce_sum | solution.py:136
  140.8 1.5 fusion.103
  144.1 6.4 %all-to-all-start.2 = ((f32[8,1,6]{2,1,0:T(1,128)}), f32[8,1,6]{2,1,0:T(1,128)S(1)}, u32[]{:S(2)}, u32[]{:S(2)}) async-start(f32[8,1,6]{2,1,0:T(1,128)} %broadcast_in_dim.72), calls=%async_computation.2 | async-start | bytes 8192 | tf_op jit(solution)/shard_map/all_to_all | solution.py:43
  150.5 1.4 copy.130
  153.0 2.0 %all-to-all-done.2 = f32[8,1,6]{2,1,0:T(1,128)S(1)} async-done(((f32[8,1,6]{2,1,0:T(1,128)}), f32[8,1,6]{2,1,0:T(1,128)S(1)}, u32[]{:S(2)}, u32[]{:S(2)}) %all-to-all-start.2) | async-done | bytes 224 | tf_op jit(solution)/shard_map/all_to_all | solution.py:43
  155.3 2.0 %multiply_convert_fusion = bf16[2,128,896]{2,1,0:T(8,128)(2,1)} fusion(bf16[2,128,896]{2,1,0:T(8,128)(2,1)} %fusion.32, bf16[2,128,896]{2,1,0:T(8,128)(2,1)S(1)} %copy-done.5, f32[2]{0:T(128)S(1)} %compare_select_fusion.1), kind=kLoop, calls=%fused_computation.53 | loop fusion | flops 1605632 | bytes 1376264 | tf_op jit(solution)/shard_map/convert_element_type | solution.py:158
  (88 shorter events, 25.8 us)
Async XLA Ops:
  3.9 15.0 %copy-start = (bf16[480,768]{1,0:T(8,128)(2,1)S(1)}, bf16[480,768]{1,0:T(8,128)(2,1)}, u32[]{:S(2)}) copy-start(bf16[480,768]{1,0:T(8,128)(2,1)} %param.9) | copy-start | bytes 2211844
  3.9 18.6 %copy-start.6 = (s32[480]{0:T(512)S(1)}, s32[480]{0:T(512)}, u32[]{:S(2)}) copy-start(s32[480]{0:T(512)} %param.11) | copy-start | bytes 5764
  3.9 61.0 %all-to-all-start = ((bf16[8,2,16,7168]{3,2,1,0:T(8,128)(2,1)}), bf16[8,2,16,7168]{3,2,1,0:T(8,128)(2,1)}, u32[]{:S(2)}, u32[]{:S(2)}) async-start(bf16[8,2,16,7168]{3,2,1,0:T(8,128)(2,1)} %broadcast_in_dim.67), calls=%async_computation | async-start | bytes 7340032 | tf_op jit(solution)/shard_map/all_to_all | solution.py:43
  18.9 33.1 %collective-permute-start = (bf16[480,768]{1,0:T(8,128)(2,1)S(1)}, bf16[480,768]{1,0:T(8,128)(2,1)S(1)}, u32[]{:S(2)}, u32[]{:S(2)}) collective-permute-start(bf16[480,768]{1,0:T(8,128)(2,1)S(1)} %copy-done), channel_id=1, source_target_pairs={{0,8},{8,16},{16,24},{24,32},{32,40},{40,48},{48,56},{56,64},{64,7... | collective-permute-start | bytes 2211848 | tf_op jit(solution)/shard_map/ppermute | solution.py:28
  20.3 31.8 %collective-permute-start.1 = (bf16[480,768]{1,0:T(8,128)(2,1)}, bf16[480,768]{1,0:T(8,128)(2,1)}, u32[]{:S(2)}, u32[]{:S(2)}) collective-permute-start(bf16[480,768]{1,0:T(8,128)(2,1)} %param.10), channel_id=1, source_target_pairs={{0,8},{8,16},{16,24},{24,32},{32,40},{40,48},{48,56},{56,64},{64,7... | collective-permute-start | bytes 2211848 | tf_op jit(solution)/shard_map/ppermute | solution.py:28
  22.5 29.6 %collective-permute-start.2 = (s32[480]{0:T(512)S(1)}, s32[480]{0:T(512)S(1)}, u32[]{:S(2)}, u32[]{:S(2)}) collective-permute-start(s32[480]{0:T(512)S(1)} %copy-done.6), channel_id=1, source_target_pairs={{0,8},{8,16},{16,24},{24,32},{32,40},{40,48},{48,56},{56,64},{64,7... | collective-permute-start | bytes 5768 | tf_op jit(solution)/shard_map/ppermute | solution.py:28
  26.4 36.1 %copy-start.3 = (bf16[480,768]{0,1:T(8,128)(2,1)}, bf16[480,768]{0,1:T(8,128)(2,1)S(1)}, u32[]{:S(2)}) copy-start(bf16[480,768]{0,1:T(8,128)(2,1)S(1)} %copy.116) | copy-start | bytes 2211844
  52.1 12.9 %copy-start.1 = (bf16[480,768]{1,0:T(8,128)(2,1)}, bf16[480,768]{1,0:T(8,128)(2,1)S(1)}, u32[]{:S(2)}) copy-start(bf16[480,768]{1,0:T(8,128)(2,1)S(1)} %collective-permute-done) | copy-start | bytes 2211844
  53.3 30.0 %collective-permute-start.3 = (bf16[480,768]{1,0:T(8,128)(2,1)S(1)}, bf16[480,768]{1,0:T(8,128)(2,1)S(1)}, u32[]{:S(2)}, u32[]{:S(2)}) collective-permute-start(bf16[480,768]{1,0:T(8,128)(2,1)S(1)} %collective-permute-done), channel_id=1, source_target_pairs={{0,8},{8,16},{16,24},{24,32},{32,40},{40,48},{48,56},{56,64},{64,7... | collective-permute-start | bytes 2211848 | tf_op jit(solution)/shard_map/ppermute | solution.py:28
  57.5 25.8 %collective-permute-start.5 = (s32[480]{0:T(512)S(1)}, s32[480]{0:T(512)S(1)}, u32[]{:S(2)}, u32[]{:S(2)}) collective-permute-start(s32[480]{0:T(512)S(1)} %collective-permute-done.2), channel_id=1, source_target_pairs={{0,8},{8,16},{16,24},{24,32},{32,40},{40,48},{48,56},{56,64},{64,7... | collective-permute-start | bytes 5768 | tf_op jit(solution)/shard_map/ppermute | solution.py:28
  59.4 29.1 %collective-permute-start.4 = (bf16[480,768]{1,0:T(8,128)(2,1)}, bf16[480,768]{1,0:T(8,128)(2,1)}, u32[]{:S(2)}, u32[]{:S(2)}) collective-permute-start(bf16[480,768]{1,0:T(8,128)(2,1)} %collective-permute-done.1), channel_id=1, source_target_pairs={{0,8},{8,16},{16,24},{24,32},{32,40},{40,48},{48,56},{56,64},{64,7... | collective-permute-start | bytes 2211848 | tf_op jit(solution)/shard_map/ppermute | solution.py:28
  78.0 11.2 %copy-start.4 = (bf16[480,768]{0,1:T(8,128)(2,1)S(1)}, bf16[480,768]{0,1:T(8,128)(2,1)}, u32[]{:S(2)}) copy-start(bf16[480,768]{0,1:T(8,128)(2,1)} %copy-done.3) | copy-start | bytes 2211844
  83.3 7.2 %copy-start.2 = (bf16[480,768]{1,0:T(8,128)(2,1)}, bf16[480,768]{1,0:T(8,128)(2,1)S(1)}, u32[]{:S(2)}) copy-start(bf16[480,768]{1,0:T(8,128)(2,1)S(1)} %collective-permute-done.3) | copy-start | bytes 2211844
  91.1 52.2 %all-to-all-start.1 = ((f32[96,1,6]{2,1,0:T(1,128)}), f32[96,1,6]{2,1,0:T(1,128)S(1)}, u32[]{:S(2)}, u32[]{:S(2)}) async-start(f32[96,1,6]{2,1,0:T(1,128)} %broadcast_in_dim.71), calls=%async_computation.1 | async-start | bytes 98304 | tf_op jit(solution)/shard_map/all_to_all | solution.py:43
  112.2 43.1 %copy-start.5 = (bf16[2,128,896]{2,1,0:T(8,128)(2,1)S(1)}, bf16[2,128,896]{2,1,0:T(8,128)(2,1)}, u32[]{:S(2)}) copy-start(bf16[2,128,896]{2,1,0:T(8,128)(2,1)} %param.13) | copy-start | bytes 1376260
  144.1 10.9 %all-to-all-start.2 = ((f32[8,1,6]{2,1,0:T(1,128)}), f32[8,1,6]{2,1,0:T(1,128)S(1)}, u32[]{:S(2)}, u32[]{:S(2)}) async-start(f32[8,1,6]{2,1,0:T(1,128)} %broadcast_in_dim.72), calls=%async_computation.2 | async-start | bytes 8192 | tf_op jit(solution)/shard_map/all_to_all | solution.py:43

commit v9 on v8

--- a/solution.py
+++ b/solution.py
@@ -117,7 +117,7 @@
         & (key_place[None, :] >= 0)
     )
 
-    group = 2 if heads_here % 2 == 0 else 1
+    group = 3 if heads_here % 3 == 0 else 1
 
     def head_group(group_index):
         col_start = group_index * (group * HD)

time: 158 us -> 168 us (1.063)
  matrix products: 33.8 us -> 38.9 us
  local copies, waits for them, and re-layouts: 21.1 us -> 25.3 us
    dynamic_slice x0 -> x8, local copies, waits for them, and re-layouts: none -> 10.4 us  [the longest x4 6 us: head_group(): key_cols = lax.dynamic_slice_in_dim(keys_all, col_start, group * HD, 1)]
    dot_general x3 -> x2, matrix products: 4.51 us -> 11.6 us  [head_group(): jnp.einsum('hqk,khd->qhd', exp_scores.astype(jnp.bfloat16), value_cols.re...]
    dot_general x3, matrix products: 5 us -> 8.39 us  [block_max(): jnp.einsum('qhd,khd->hqk', query_vectors.reshape(tokens_here, heads_here,...]
    dot_general x3 -> x2, matrix products: 7.46 us -> 4.27 us  [head_group(): jnp.einsum('qhd,khd->hqk', query_cols.reshape(tokens_here, group, HD), ke...]
    while x3 -> x4, local copies, waits for them, and re-layouts: 4.19 us -> 1.45 us
    reshape x0 -> x1, local copies, waits for them, and re-layouts: none -> 2.26 us  [shards(): jnp.transpose(mixed_groups, (1, 0, 2)).reshape(tokens_here, heads_here * HD)]
    reduce_sum x3 -> x2, other arithmetic: 5.47 us -> 5.38 us  [head_group(): row_total = jnp.sum(exp_scores, axis=2)]
  transfers between devices with their start and end apart: 9 -> 9, of which waited for: 3 -> 3; matrix products, arithmetic and copies ran while one was open for 39% -> 40% of each run, Pallas kernels for 0% -> 0%
where the time goes in v9:
time: 168 us; the launch traced here: 167 us
  starting transfers between devices  52.8 us (31%)
  matrix products  38.9 us (23%)
  waiting for transfers between devices  31.3 us (19%)
  local copies, waits for them, and re-layouts  25.3 us (15%)
  other arithmetic  16.4 us (10%)
    all_to_all x3, starting transfers between devices, gathered(): return lax.all_to_all(spread, axis, 0, 0, tiled=True)  39 us
    ppermute x6, waiting for transfers between devices, shifted(): return lax.ppermute(shard, axis, pairs)  29.1 us
    ppermute x6, starting transfers between devices, shifted(): return lax.ppermute(shard, axis, pairs)  13.7 us
    dot_general x2, matrix products, head_group(): jnp.einsum('hqk,khd->qhd', exp_scores.astype(jnp.bfloat16), value_cols.re...  11.6 us
    dot_general x3, matrix products, block_max(): jnp.einsum('qhd,khd->hqk', query_vectors.reshape(tokens_here, heads_here,...  8.39 us
    dot_general x1, matrix products, shards(): jnp.einsum('jmrd,kmsd->mjrks', pieces, pieces, preferred_element_type=jnp...  6.9 us
    dynamic_slice x4, local copies, waits for them, and re-layouts, head_group(): key_cols = lax.dynamic_slice_in_dim(keys_all, col_start, group * HD, 1)  6 us
    reduce_sum x2, other arithmetic, head_group(): row_total = jnp.sum(exp_scores, axis=2)  5.38 us
  transfers between devices with their start and end apart: 9, of which 3 were waited for; matrix products, arithmetic and copies ran while one was open for 40% of the time, Pallas kernels for 0%

profile of v9, /device:TPU:1, one launch (start us, length us, event | category | flops | bytes accessed | tf_op | source)
XLA Modules:
  0.0 167.1 jit_solution(2433617921997093157)
XLA Ops:
  0.6 3.3 %broadcast_in_dim.67 = bf16[8,2,16,7168]{3,2,1,0:T(8,128)(2,1)} broadcast(bf16[2,16,7168]{2,1,0:T(8,128)(2,1)} %param.12), dimensions={1,2,3} | broadcast | bytes 4128768 | tf_op jit(solution)/shard_map/broadcast_in_dim | solution.py:42
  3.9 15.0 %all-to-all-start = ((bf16[8,2,16,7168]{3,2,1,0:T(8,128)(2,1)}), bf16[8,2,16,7168]{3,2,1,0:T(8,128)(2,1)}, u32[]{:S(2)}, u32[]{:S(2)}) async-start(bf16[8,2,16,7168]{3,2,1,0:T(8,128)(2,1)} %broadcast_in_dim.67), calls=%async_computation | async-start | bytes 7340032 | tf_op jit(solution)/shard_map/all_to_all | solution.py:43
  18.9 1.3 collective-permute-start
  20.3 2.2 %collective-permute-start.1 = (bf16[480,768]{1,0:T(8,128)(2,1)}, bf16[480,768]{1,0:T(8,128)(2,1)}, u32[]{:S(2)}, u32[]{:S(2)}) collective-permute-start(bf16[480,768]{1,0:T(8,128)(2,1)} %param.10), channel_id=1, source_target_pairs={{0,8},{8,16},{16,24},{24,32},{32,40},{40,48},{48,56},{56,64},{64,7... | collective-permute-start | bytes 2211848 | tf_op jit(solution)/shard_map/ppermute | solution.py:28
  22.4 1.3 collective-permute-start.2
  26.9 3.0 %select_reduce_fusion = f32[6]{0:T(128)} fusion(pred[480,480]{1,0:T(8,128)(4,1)S(1)} %and_and_fusion.3, bf16[480,6,128]{0,2,1:T(8,128)(2,1)} %bitcast, bf16[480,6,128]{0,2,1:T(8,128)(2,1)S(1)} %bitcast.111), kind=kOutput, calls=%fused_computation.22 | convolution fusion | flops 358041600 | bytes 1704984 | tf_op jit(solution)/shard_map/qhd,khd->hqk/dot_general | solution.py:91
  30.5 21.6 %collective-permute-done.2 = s32[480]{0:T(512)S(1)} collective-permute-done((s32[480]{0:T(512)S(1)}, s32[480]{0:T(512)S(1)}, u32[]{:S(2)}, u32[]{:S(2)}) %collective-permute-start.2) | collective-permute-done | bytes 1952 | tf_op jit(solution)/shard_map/ppermute | solution.py:28
  52.4 4.2 %collective-permute-start.3 = (bf16[480,768]{1,0:T(8,128)(2,1)S(1)}, bf16[480,768]{1,0:T(8,128)(2,1)S(1)}, u32[]{:S(2)}, u32[]{:S(2)}) collective-permute-start(bf16[480,768]{1,0:T(8,128)(2,1)S(1)} %collective-permute-done), channel_id=1, source_target_pairs={{0,8},{8,16},{16,24},{24,32},{32,40},{40,48},{48,56},{56,64},{64,7... | collective-permute-start | bytes 2211848 | tf_op jit(solution)/shard_map/ppermute | solution.py:28
  56.6 1.9 %collective-permute-start.5 = (s32[480]{0:T(512)S(1)}, s32[480]{0:T(512)S(1)}, u32[]{:S(2)}, u32[]{:S(2)}) collective-permute-start(s32[480]{0:T(512)S(1)} %collective-permute-done.2), channel_id=1, source_target_pairs={{0,8},{8,16},{16,24},{24,32},{32,40},{40,48},{48,56},{56,64},{64,7... | collective-permute-start | bytes 5768 | tf_op jit(solution)/shard_map/ppermute | solution.py:28
  58.5 2.9 %collective-permute-start.4 = (bf16[480,768]{1,0:T(8,128)(2,1)}, bf16[480,768]{1,0:T(8,128)(2,1)}, u32[]{:S(2)}, u32[]{:S(2)}) collective-permute-start(bf16[480,768]{1,0:T(8,128)(2,1)} %collective-permute-done.1), channel_id=1, source_target_pairs={{0,8},{8,16},{16,24},{24,32},{32,40},{40,48},{48,56},{56,64},{64,7... | collective-permute-start | bytes 2211848 | tf_op jit(solution)/shard_map/ppermute | solution.py:28
  61.6 3.0 %fusion.20 = f32[6]{0:T(128)} fusion(pred[480,480]{1,0:T(8,128)(4,1)S(1)} %and_and_fusion.2, bf16[480,6,128]{0,2,1:T(8,128)(2,1)S(1)} %bitcast.110, bf16[480,6,128]{0,2,1:T(8,128)(2,1)} %bitcast), kind=kOutput, calls=%fused_computation.21 | convolution fusion | flops 358041600 | bytes 1704984 | tf_op jit(solution)/shard_map/qhd,khd->hqk/dot_general | solution.py:91
  64.6 6.9 %select_reduce_fusion.1 = (f32[2]{0:T(128)S(1)}, f32[2,8,16,8,16]{4,2,3,1,0:T(8,128)S(1)}) fusion(pred[8,16,8,16]{3,1,2,0:T(8,128)(4,1)S(1)} %broadcast_compare_fusion, bf16[8,2,16,7168]{3,2,1,0:T(8,128)(2,1)} %all-to-all-done), kind=kOutput, calls=%fused_computation.41 | convolution fusion | flops 469827584 | bytes 3817480 | tf_op jit(solution)/shard_map/jmrd,kmsd->mjrks/dot_general | solution.py:56
  77.3 2.8 %fusion.25 = bf16[2,128,896]{2,1,0:T(8,128)(2,1)} fusion(f32[2,128,8,16]{1,3,2,0:T(8,128)S(1)} %bitcast.114, f32[2]{0:T(128)S(1)} %get-tuple-element.169, bf16[8,2,16,7168]{3,2,1,0:T(8,128)(2,1)} %all-to-all-done, s32[]{:T(128)S(6)} %select_n.51), kind=kOutput, calls=%fused_computation.30 | convolution fusion | flops 353239040 | bytes 1048588 | tf_op jit(solution)/shard_map/mijr,jmrd->mid/dot_general | solution.py:72
  80.1 7.5 %collective-permute-done.4 = bf16[480,768]{1,0:T(8,128)(2,1)} collective-permute-done((bf16[480,768]{1,0:T(8,128)(2,1)}, bf16[480,768]{1,0:T(8,128)(2,1)}, u32[]{:S(2)}, u32[]{:S(2)}) %collective-permute-start.4) | collective-permute-done | bytes 737312 | tf_op jit(solution)/shard_map/ppermute | solution.py:28
  89.6 2.4 %fusion.19 = f32[6]{0:T(128)S(1)} fusion(pred[480,480]{1,0:T(8,128)(4,1)S(1)} %and_and_fusion.1, bf16[480,6,128]{0,2,1:T(8,128)(2,1)S(1)} %bitcast.112, bf16[480,6,128]{0,2,1:T(8,128)(2,1)} %bitcast), kind=kOutput, calls=%fused_computation.19 | convolution fusion | flops 358041600 | bytes 1704984 | tf_op jit(solution)/shard_map/qhd,khd->hqk/dot_general | solution.py:91
  92.7 17.7 %all-to-all-start.1 = ((f32[96,1,6]{2,1,0:T(1,128)}), f32[96,1,6]{2,1,0:T(1,128)S(1)}, u32[]{:S(2)}, u32[]{:S(2)}) async-start(f32[96,1,6]{2,1,0:T(1,128)} %broadcast_in_dim.71), calls=%async_computation.1 | async-start | bytes 98304 | tf_op jit(solution)/shard_map/all_to_all | solution.py:43
  110.4 3.6 %pad_maximum_fusion = (bf16[1440,768]{1,0:T(8,128)(2,1)}, bf16[1440,768]{1,0:T(8,128)(2,1)}) fusion(bf16[480,768]{1,0:T(8,128)(2,1)} %param.10, bf16[480,768]{1,0:T(8,128)(2,1)} %collective-permute-done.1, bf16[480,768]{1,0:T(8,128)(2,1)} %collective-permute-done.4, bf16[480,768]{1,0:T(8,128)(2,1)S(1)} %copy-done.1, ...), kind=kLoop, calls=%fused_computation.26 | loop fusion | flops 13271040 | bytes 8847360 | tf_op jit(solution)/shard_map/concatenate | solution.py:109
  113.9 39.1 %while.11 = (s32[]{:T(128)}, bf16[2,480,384]{1,2,0:T(8,128)(2,1)}, s32[2]{0:T(128)S(1)}, bf16[1440,768]{1,0:T(8,128)(2,1)}, bf16[480,768]{0,1:T(8,128)(2,1)}, /*...) while((s32[]{:T(128)}, bf16[2,480,384]{1,2,0:T(8,128)(2,1)}, ...), condition=%wide.region_6.7_spmd.clone, body=%wide.region_3.6_spmd.clone.sunk | while | flops 1087623424 | bytes 74904840 | solution.py:145
  115.2 1.8 %constant_dynamic-slice_fusion.5 = (bf16[1440,384]{1,0:T(8,128)(2,1)S(1)}, bf16[1440,384]{1,0:T(8,128)(2,1)S(1)}) fusion(bf16[1440,768]{1,0:T(8,128)(2,1)} %get-tuple-element.285, s32[]{:T(128)S(6)} %select_n.90, bf16[1440,768]{1,0:T(8,128)(2,1)} %get-tuple-element.283), kind=kLoop, calls=%fused_computation.13.clone.1 | loop fusion | bytes 4423684 | tf_op jit(solution)/shard_map/while/body/eval_jaxpr/dynamic_slice | solution.py:125
  117.0 1.2 copy.184
  120.0 2.1 %fusion.101 = (f32[3,480]{1,0:T(4,128)S(1)}, f32[3,480,1440]{2,1,0:T(8,128)S(1)}) fusion(pred[480,1440]{1,0:T(8,128)(4,1)S(1)} %and_and_fusion.5, bf16[480,3,128]{0,2,1:T(8,128)(2,1)S(1)} %bitcast.106, bf16[1440,3,128]{0,2,1:T(8,128)(2,1)S(1)} %bitcast.105), kind=kOutput, calls=%fused_computation.3.clone.1 | convolution fusion | flops 537060992 | bytes 10465920 | tf_op jit(solution)/shard_map/while/body/eval_jaxpr/qhd,khd->hqk/dot_general | solution.py:127
  122.1 2.7 %fusion.102 = f32[3,480]{1,0:T(4,128)S(1)} fusion(f32[3,480,1440]{2,1,0:T(8,128)S(1)} %get-tuple-element.248, f32[3,480]{1,0:T(4,128)S(1)} %get-tuple-element.249, pred[480,1440]{1,0:T(8,128)(4,1)S(1)} %and_and_fusion.5), kind=kLoop, calls=%fused_computation.4.clone.1 | loop fusion | flops 8292960 | bytes 8997120 | tf_op jit(solution)/shard_map/while/body/eval_jaxpr/reduce_sum | solution.py:136
  126.7 5.8 %fusion.103 = bf16[480,3,128]{2,0,1:T(8,128)(2,1)S(1)} fusion(bf16[1440,3,128]{0,2,1:T(8,128)(2,1)S(1)} %bitcast.108, f32[3,480,1440]{2,1,0:T(8,128)} %copy-done, f32[3,480]{1,0:T(4,128)S(1)} %get-tuple-element.249, pred[480,1440]{1,0:T(8,128)(4,1)S(1)} %and_and_fusion.5, f32[480,3]{0,1:T(4,128)S(1)} %bitcast.113), kind=kOutput, calls=%fused_computation.11.clone.1 | convolution fusion | flops 539504640 | bytes 10471680 | tf_op jit(solution)/shard_map/while/body/eval_jaxpr/hqk,khd->qhd/dot_general | solution.py:137
  134.8 1.8 %constant_dynamic-slice_fusion.5 = (bf16[1440,384]{1,0:T(8,128)(2,1)S(1)}, bf16[1440,384]{1,0:T(8,128)(2,1)S(1)}) fusion(bf16[1440,768]{1,0:T(8,128)(2,1)} %get-tuple-element.285, s32[]{:T(128)S(6)} %select_n.90, bf16[1440,768]{1,0:T(8,128)(2,1)} %get-tuple-element.283), kind=kLoop, calls=%fused_computation.13.clone.1 | loop fusion | bytes 4423684 | tf_op jit(solution)/shard_map/while/body/eval_jaxpr/dynamic_slice | solution.py:125
  136.6 1.2 copy.184
  139.6 2.1 %fusion.101 = (f32[3,480]{1,0:T(4,128)S(1)}, f32[3,480,1440]{2,1,0:T(8,128)S(1)}) fusion(pred[480,1440]{1,0:T(8,128)(4,1)S(1)} %and_and_fusion.5, bf16[480,3,128]{0,2,1:T(8,128)(2,1)S(1)} %bitcast.106, bf16[1440,3,128]{0,2,1:T(8,128)(2,1)S(1)} %bitcast.105), kind=kOutput, calls=%fused_computation.3.clone.1 | convolution fusion | flops 537060992 | bytes 10465920 | tf_op jit(solution)/shard_map/while/body/eval_jaxpr/qhd,khd->hqk/dot_general | solution.py:127
  141.7 2.7 %fusion.102 = f32[3,480]{1,0:T(4,128)S(1)} fusion(f32[3,480,1440]{2,1,0:T(8,128)S(1)} %get-tuple-element.248, f32[3,480]{1,0:T(4,128)S(1)} %get-tuple-element.249, pred[480,1440]{1,0:T(8,128)(4,1)S(1)} %and_and_fusion.5), kind=kLoop, calls=%fused_computation.4.clone.1 | loop fusion | flops 8292960 | bytes 8997120 | tf_op jit(solution)/shard_map/while/body/eval_jaxpr/reduce_sum | solution.py:136
  146.3 5.8 %fusion.103 = bf16[480,3,128]{2,0,1:T(8,128)(2,1)S(1)} fusion(bf16[1440,3,128]{0,2,1:T(8,128)(2,1)S(1)} %bitcast.108, f32[3,480,1440]{2,1,0:T(8,128)} %copy-done, f32[3,480]{1,0:T(4,128)S(1)} %get-tuple-element.249, pred[480,1440]{1,0:T(8,128)(4,1)S(1)} %and_and_fusion.5, f32[480,3]{0,1:T(4,128)S(1)} %bitcast.113), kind=kOutput, calls=%fused_computation.11.clone.1 | convolution fusion | flops 539504640 | bytes 10471680 | tf_op jit(solution)/shard_map/while/body/eval_jaxpr/hqk,khd->qhd/dot_general | solution.py:137
  153.8 6.4 %all-to-all-start.2 = ((f32[8,1,6]{2,1,0:T(1,128)}), f32[8,1,6]{2,1,0:T(1,128)S(1)}, u32[]{:S(2)}, u32[]{:S(2)}) async-start(f32[8,1,6]{2,1,0:T(1,128)} %broadcast_in_dim.72), calls=%async_computation.2 | async-start | bytes 8192 | tf_op jit(solution)/shard_map/all_to_all | solution.py:43
  160.2 2.3 %copy.166 = bf16[480,768]{1,0:T(8,128)(2,1)} copy(bf16[480,768]{0,1:T(8,128)(2,1)} %bitcast.109) | data formatting | bytes 1474560 | tf_op jit(solution)/shard_map/reshape | solution.py:146
  162.4 2.2 %all-to-all-done.2 = f32[8,1,6]{2,1,0:T(1,128)S(1)} async-done(((f32[8,1,6]{2,1,0:T(1,128)}), f32[8,1,6]{2,1,0:T(1,128)S(1)}, u32[]{:S(2)}, u32[]{:S(2)}) %all-to-all-start.2) | async-done | bytes 224 | tf_op jit(solution)/shard_map/all_to_all | solution.py:43
  165.0 2.1 %multiply_convert_fusion = bf16[2,128,896]{2,1,0:T(8,128)(2,1)} fusion(bf16[2,128,896]{2,1,0:T(8,128)(2,1)} %fusion.25, bf16[2,128,896]{2,1,0:T(8,128)(2,1)} %param.13, f32[2]{0:T(128)S(1)} %compare_select_fusion.1), kind=kLoop, calls=%fused_computation.46 | loop fusion | flops 1605632 | bytes 1376264 | tf_op jit(solution)/shard_map/convert_element_type | solution.py:158
  (90 shorter events, 24.0 us)
Async XLA Ops:
  3.9 15.0 %copy-start.1 = (bf16[480,768]{1,0:T(8,128)(2,1)S(1)}, bf16[480,768]{1,0:T(8,128)(2,1)}, u32[]{:S(2)}) copy-start(bf16[480,768]{1,0:T(8,128)(2,1)} %param.9) | copy-start | bytes 2211844
  3.9 18.5 %copy-start.3 = (s32[480]{0:T(512)S(1)}, s32[480]{0:T(512)}, u32[]{:S(2)}) copy-start(s32[480]{0:T(512)} %param.11) | copy-start | bytes 5764
  3.9 21.5 %copy-start.2 = (bf16[480,768]{1,0:T(8,128)(2,1)S(1)}, bf16[480,768]{1,0:T(8,128)(2,1)}, u32[]{:S(2)}) copy-start(bf16[480,768]{1,0:T(8,128)(2,1)} %param.8) | copy-start | bytes 2211844
  3.9 60.7 %all-to-all-start = ((bf16[8,2,16,7168]{3,2,1,0:T(8,128)(2,1)}), bf16[8,2,16,7168]{3,2,1,0:T(8,128)(2,1)}, u32[]{:S(2)}, u32[]{:S(2)}) async-start(bf16[8,2,16,7168]{3,2,1,0:T(8,128)(2,1)} %broadcast_in_dim.67), calls=%async_computation | async-start | bytes 7340032 | tf_op jit(solution)/shard_map/all_to_all | solution.py:43
  18.9 33.1 %collective-permute-start = (bf16[480,768]{1,0:T(8,128)(2,1)S(1)}, bf16[480,768]{1,0:T(8,128)(2,1)S(1)}, u32[]{:S(2)}, u32[]{:S(2)}) collective-permute-start(bf16[480,768]{1,0:T(8,128)(2,1)S(1)} %copy-done.1), channel_id=1, source_target_pairs={{0,8},{8,16},{16,24},{24,32},{32,40},{40,48},{48,56},{56,64},{64,7... | collective-permute-start | bytes 2211848 | tf_op jit(solution)/shard_map/ppermute | solution.py:28
  20.3 31.8 %collective-permute-start.1 = (bf16[480,768]{1,0:T(8,128)(2,1)}, bf16[480,768]{1,0:T(8,128)(2,1)}, u32[]{:S(2)}, u32[]{:S(2)}) collective-permute-start(bf16[480,768]{1,0:T(8,128)(2,1)} %param.10), channel_id=1, source_target_pairs={{0,8},{8,16},{16,24},{24,32},{32,40},{40,48},{48,56},{56,64},{64,7... | collective-permute-start | bytes 2211848 | tf_op jit(solution)/shard_map/ppermute | solution.py:28
  22.4 29.6 %collective-permute-start.2 = (s32[480]{0:T(512)S(1)}, s32[480]{0:T(512)S(1)}, u32[]{:S(2)}, u32[]{:S(2)}) collective-permute-start(s32[480]{0:T(512)S(1)} %copy-done.3), channel_id=1, source_target_pairs={{0,8},{8,16},{16,24},{24,32},{32,40},{40,48},{48,56},{56,64},{64,7... | collective-permute-start | bytes 5768 | tf_op jit(solution)/shard_map/ppermute | solution.py:28
  52.4 27.7 %collective-permute-start.3 = (bf16[480,768]{1,0:T(8,128)(2,1)S(1)}, bf16[480,768]{1,0:T(8,128)(2,1)S(1)}, u32[]{:S(2)}, u32[]{:S(2)}) collective-permute-start(bf16[480,768]{1,0:T(8,128)(2,1)S(1)} %collective-permute-done), channel_id=1, source_target_pairs={{0,8},{8,16},{16,24},{24,32},{32,40},{40,48},{48,56},{56,64},{64,7... | collective-permute-start | bytes 2211848 | tf_op jit(solution)/shard_map/ppermute | solution.py:28
  56.6 23.5 %collective-permute-start.5 = (s32[480]{0:T(512)S(1)}, s32[480]{0:T(512)S(1)}, u32[]{:S(2)}, u32[]{:S(2)}) collective-permute-start(s32[480]{0:T(512)S(1)} %collective-permute-done.2), channel_id=1, source_target_pairs={{0,8},{8,16},{16,24},{24,32},{32,40},{40,48},{48,56},{56,64},{64,7... | collective-permute-start | bytes 5768 | tf_op jit(solution)/shard_map/ppermute | solution.py:28
  58.5 29.1 %collective-permute-start.4 = (bf16[480,768]{1,0:T(8,128)(2,1)}, bf16[480,768]{1,0:T(8,128)(2,1)}, u32[]{:S(2)}, u32[]{:S(2)}) collective-permute-start(bf16[480,768]{1,0:T(8,128)(2,1)} %collective-permute-done.1), channel_id=1, source_target_pairs={{0,8},{8,16},{16,24},{24,32},{32,40},{40,48},{48,56},{56,64},{64,7... | collective-permute-start | bytes 2211848 | tf_op jit(solution)/shard_map/ppermute | solution.py:28
  74.6 14.1 %copy-start.5 = (s32[480]{0:T(512)S(1)}, s32[480]{0:T(512)}, u32[]{:S(2)}) copy-start(s32[480]{0:T(512)} %iota_add_fusion.1) | copy-start | bytes 5764
  74.6 14.1 %copy-start.6 = (pred[480]{0:T(512)(128)(4,1)S(1)}, pred[480]{0:T(512)(128)(4,1)}, u32[]{:S(2)}) copy-start(pred[480]{0:T(512)(128)(4,1)} %broadcast_compare_fusion.2) | copy-start | bytes 1444
  80.1 11.9 %copy-start.7 = (f32[6]{0:T(128)S(1)}, f32[6]{0:T(128)}, u32[]{:S(2)}) copy-start(f32[6]{0:T(128)} %select_reduce_fusion) | copy-start | bytes 76
  80.1 11.9 %copy-start.8 = (f32[6]{0:T(128)S(1)}, f32[6]{0:T(128)}, u32[]{:S(2)}) copy-start(f32[6]{0:T(128)} %fusion.20) | copy-start | bytes 76
  80.1 7.5 %copy-start.4 = (s32[480]{0:T(512)}, s32[480]{0:T(512)S(1)}, u32[]{:S(2)}) copy-start(s32[480]{0:T(512)S(1)} %collective-permute-done.5) | copy-start | bytes 5764
  92.7 60.4 %all-to-all-start.1 = ((f32[96,1,6]{2,1,0:T(1,128)}), f32[96,1,6]{2,1,0:T(1,128)S(1)}, u32[]{:S(2)}, u32[]{:S(2)}) async-start(f32[96,1,6]{2,1,0:T(1,128)} %broadcast_in_dim.71), calls=%async_computation.1 | async-start | bytes 98304 | tf_op jit(solution)/shard_map/all_to_all | solution.py:43
  113.9 50.8 %copy-start.9 = (s32[2]{0:T(128)S(1)}, s32[2]{0:T(128)}, u32[]{:S(2)}) copy-start(s32[2]{0:T(128)} %and_select_fusion) | copy-start | bytes 28
  122.1 3.4 %copy-start = (f32[3,480,1440]{2,1,0:T(8,128)}, f32[3,480,1440]{2,1,0:T(8,128)S(1)}, u32[]{:S(2)}) copy-start(f32[3,480,1440]{2,1,0:T(8,128)S(1)} %get-tuple-element.248) | copy-start | bytes 24883204 | tf_op jit(solution)/shard_map/while
  141.7 3.4 %copy-start = (f32[3,480,1440]{2,1,0:T(8,128)}, f32[3,480,1440]{2,1,0:T(8,128)S(1)}, u32[]{:S(2)}) copy-start(f32[3,480,1440]{2,1,0:T(8,128)S(1)} %get-tuple-element.248) | copy-start | bytes 24883204 | tf_op jit(solution)/shard_map/while
  153.8 10.9 %all-to-all-start.2 = ((f32[8,1,6]{2,1,0:T(1,128)}), f32[8,1,6]{2,1,0:T(1,128)S(1)}, u32[]{:S(2)}, u32[]{:S(2)}) async-start(f32[8,1,6]{2,1,0:T(1,128)} %broadcast_in_dim.72), calls=%async_computation.2 | async-start | bytes 8192 | tf_op jit(solution)/shard_map/all_to_all | solution.py:43

commit v10 on v8

--- a/solution.py
+++ b/solution.py
@@ -101,12 +101,16 @@
     first, local_max = lax.optimization_barrier((first, local_max))
     second = shifted(first, "seq", 1)
     first_max = block_max(first, REACH - 1)
-    second, first_max, update = lax.optimization_barrier((second, first_max, update))
+    key_window = jnp.concatenate([jnp.zeros_like(key_vectors), first[0], key_vectors], axis=0)
+    value_window = jnp.concatenate([jnp.zeros_like(value_vectors), first[1], value_vectors], axis=0)
+    second, first_max, update, key_window, value_window = lax.optimization_barrier(
+        (second, first_max, update, key_window, value_window)
+    )
     head_max = jnp.maximum(jnp.maximum(local_max, first_max), block_max(second, REACH - 2))
     earlier = [first, second]
     ordered = [earlier[REACH - 1 - position] for position in range(REACH)] + [local_block]
-    keys_all = jnp.concatenate([member[0] for member in ordered], axis=0)
-    values_all = jnp.concatenate([member[1] for member in ordered], axis=0)
+    keys_all = lax.dynamic_update_slice_in_dim(key_window, second[0], 0, 0)
+    values_all = lax.dynamic_update_slice_in_dim(value_window, second[1], 0, 0)
     docs_all = jnp.concatenate([member[2] for member in ordered], axis=0)
     key_place = (seq_index - REACH) * tokens_here + jnp.arange(
         (REACH + 1) * tokens_here, dtype=jnp.int32

time: 158 us -> 162 us (1.025)
  local copies, waits for them, and re-layouts: 21.1 us -> 25.8 us
  matrix products: 33.8 us -> 31.6 us
    dynamic_update_slice x0 -> x2, local copies, waits for them, and re-layouts: none -> 3.19 us  [the longest x1 2.02 us: shards(): keys_all = lax.dynamic_update_slice_in_dim(key_window, second[0], 0, 0)]
    optimization_barrier x1, local copies, waits for them, and re-layouts: 0.28 us -> 2.27 us  [shards(): lax.optimization_barrier((second, first_max, update, key_window, value_wi...]
  transfers between devices with their start and end apart: 9 -> 9, of which waited for: 3 -> 3; matrix products, arithmetic and copies ran while one was open for 39% -> 37% of each run, Pallas kernels for 0% -> 0%
where the time goes in v10:
time: 162 us; the launch traced here: 160 us
  starting transfers between devices  53.4 us (33%)
  waiting for transfers between devices  32.2 us (20%)
  matrix products  31.6 us (20%)
  local copies, waits for them, and re-layouts  25.8 us (16%)
  other arithmetic  14.3 us (9%)
  loops' own time  2.2 us (1%)
    all_to_all x3, starting transfers between devices, gathered(): return lax.all_to_all(spread, axis, 0, 0, tiled=True)  38.8 us
    ppermute x6, waiting for transfers between devices, shifted(): return lax.ppermute(shard, axis, pairs)  30.2 us
    ppermute x6, starting transfers between devices, shifted(): return lax.ppermute(shard, axis, pairs)  14.5 us
    dot_general x3, matrix products, head_group(): jnp.einsum('qhd,khd->hqk', query_cols.reshape(tokens_here, group, HD), ke...  7.46 us
    dot_general x1, matrix products, shards(): jnp.einsum('jmrd,kmsd->mjrks', pieces, pieces, preferred_element_type=jnp...  6.9 us
    reduce_sum x3, other arithmetic, head_group(): row_total = jnp.sum(exp_scores, axis=2)  5.47 us
    dot_general x3, matrix products, block_max(): jnp.einsum('qhd,khd->hqk', query_vectors.reshape(tokens_here, heads_here,...  5 us
    broadcast_in_dim x3, local copies, waits for them, and re-layouts, gathered(): spread = jnp.broadcast_to(values[None], (size,) + values.shape)  4.53 us
  transfers between devices with their start and end apart: 9, of which 3 were waited for; matrix products, arithmetic and copies ran while one was open for 37% of the time, Pallas kernels for 0%

profile of v10, /device:TPU:1, one launch (start us, length us, event | category | flops | bytes accessed | tf_op | source)
XLA Modules:
  0.0 160.4 jit_solution(12398161643178555334)
XLA Ops:
  0.6 3.3 %broadcast_in_dim.67 = bf16[8,2,16,7168]{3,2,1,0:T(8,128)(2,1)} broadcast(bf16[2,16,7168]{2,1,0:T(8,128)(2,1)} %param.12), dimensions={1,2,3} | broadcast | bytes 4128768 | tf_op jit(solution)/shard_map/broadcast_in_dim | solution.py:42
  3.9 15.0 %all-to-all-start = ((bf16[8,2,16,7168]{3,2,1,0:T(8,128)(2,1)}), bf16[8,2,16,7168]{3,2,1,0:T(8,128)(2,1)}, u32[]{:S(2)}, u32[]{:S(2)}) async-start(bf16[8,2,16,7168]{3,2,1,0:T(8,128)(2,1)} %broadcast_in_dim.67), calls=%async_computation | async-start | bytes 7340032 | tf_op jit(solution)/shard_map/all_to_all | solution.py:43
  18.9 2.2 %collective-permute-start = (bf16[480,768]{1,0:T(8,128)(2,1)S(1)}, bf16[480,768]{1,0:T(8,128)(2,1)}, u32[]{:S(2)}, u32[]{:S(2)}) collective-permute-start(bf16[480,768]{1,0:T(8,128)(2,1)S(1)} %copy-done), channel_id=1, source_target_pairs={{0,8},{8,16},{16,24},{24,32},{32,40},{40,48},{48,56},{56,64},{64,7... | collective-permute-start | bytes 2211848 | tf_op jit(solution)/shard_map/ppermute | solution.py:28
  21.1 2.2 %collective-permute-start.1 = (bf16[480,768]{1,0:T(8,128)(2,1)}, bf16[480,768]{1,0:T(8,128)(2,1)}, u32[]{:S(2)}, u32[]{:S(2)}) collective-permute-start(bf16[480,768]{1,0:T(8,128)(2,1)} %param.10), channel_id=1, source_target_pairs={{0,8},{8,16},{16,24},{24,32},{32,40},{40,48},{48,56},{56,64},{64,7... | collective-permute-start | bytes 2211848 | tf_op jit(solution)/shard_map/ppermute | solution.py:28
  25.1 1.4 copy.116
  28.2 23.9 %collective-permute-done.2 = s32[480]{0:T(512)S(1)} collective-permute-done((s32[480]{0:T(512)S(1)}, s32[480]{0:T(512)S(1)}, u32[]{:S(2)}, u32[]{:S(2)}) %collective-permute-start.2) | collective-permute-done | bytes 1952 | tf_op jit(solution)/shard_map/ppermute | solution.py:28
  52.1 1.4 copy.121
  53.5 5.0 %collective-permute-start.3 = (bf16[480,768]{1,0:T(8,128)(2,1)}, bf16[480,768]{1,0:T(8,128)(2,1)}, u32[]{:S(2)}, u32[]{:S(2)}) collective-permute-start(bf16[480,768]{1,0:T(8,128)(2,1)} %collective-permute-done), channel_id=1, source_target_pairs={{0,8},{8,16},{16,24},{24,32},{32,40},{40,48},{48,56},{56,64},{64,7... | collective-permute-start | bytes 2211848 | tf_op jit(solution)/shard_map/ppermute | solution.py:28
  59.8 2.6 %collective-permute-start.4 = (bf16[480,768]{1,0:T(8,128)(2,1)}, bf16[480,768]{1,0:T(8,128)(2,1)}, u32[]{:S(2)}, u32[]{:S(2)}) collective-permute-start(bf16[480,768]{1,0:T(8,128)(2,1)} %collective-permute-done.1), channel_id=1, source_target_pairs={{0,8},{8,16},{16,24},{24,32},{32,40},{40,48},{48,56},{56,64},{64,7... | collective-permute-start | bytes 2211848 | tf_op jit(solution)/shard_map/ppermute | solution.py:28
  64.0 3.2 %pad_maximum_fusion.1 = (bf16[1440,768]{1,0:T(8,128)(2,1)S(1)}, bf16[1440,768]{1,0:T(8,128)(2,1)}) fusion(bf16[480,768]{1,0:T(8,128)(2,1)} %param.10, bf16[480,768]{1,0:T(8,128)(2,1)} %collective-permute-done.1, bf16[1440]{0:T(1024)(128)(2,1)S(1)} %pad.3.clone, bf16[480,768]{1,0:T(8,128)(2,1)S(1)} %copy-done, bf16[480,768]{1,0:T(8,128)(2,1)} %collective-permute-done), kind=kLoop, calls=%fused_computation.34 | loop fusion | flops 12165120 | bytes 7375680 | tf_op jit(solution)/shard_map/concatenate | solution.py:105
  67.1 6.9 %select_reduce_fusion.1 = (f32[2]{0:T(128)S(1)}, f32[2,8,16,8,16]{4,2,3,1,0:T(8,128)S(1)}) fusion(pred[8,16,8,16]{3,1,2,0:T(8,128)(4,1)S(1)} %broadcast_compare_fusion, bf16[8,2,16,7168]{3,2,1,0:T(8,128)(2,1)} %all-to-all-done), kind=kOutput, calls=%fused_computation.48 | convolution fusion | flops 469827584 | bytes 3817480 | tf_op jit(solution)/shard_map/jmrd,kmsd->mjrks/dot_general | solution.py:56
  79.8 2.8 %fusion.32 = bf16[2,128,896]{2,1,0:T(8,128)(2,1)} fusion(f32[2,128,8,16]{1,3,2,0:T(8,128)S(1)} %bitcast.122, f32[2]{0:T(128)S(1)} %get-tuple-element.135, bf16[8,2,16,7168]{3,2,1,0:T(8,128)(2,1)} %all-to-all-done, s32[]{:T(128)S(6)} %select_n.51), kind=kOutput, calls=%fused_computation.37 | convolution fusion | flops 353239040 | bytes 1048588 | tf_op jit(solution)/shard_map/mijr,jmrd->mid/dot_general | solution.py:72
  82.6 6.3 %collective-permute-done.4 = bf16[480,768]{1,0:T(8,128)(2,1)} collective-permute-done((bf16[480,768]{1,0:T(8,128)(2,1)}, bf16[480,768]{1,0:T(8,128)(2,1)}, u32[]{:S(2)}, u32[]{:S(2)}) %collective-permute-start.4) | collective-permute-done | bytes 737312 | tf_op jit(solution)/shard_map/ppermute | solution.py:28
  88.9 2.3 %copy.131 = bf16[480,768]{0,1:T(8,128)(2,1)} copy(bf16[480,768]{1,0:T(8,128)(2,1)} %collective-permute-done.3) | data formatting | bytes 1474560 | tf_op jit(solution)/shard_map/optimization_barrier | solution.py:106
  91.6 2.4 %fusion.26 = f32[6]{0:T(128)S(1)} fusion(pred[480,480]{1,0:T(8,128)(4,1)S(1)} %and_and_fusion.1, bf16[480,6,128]{0,2,1:T(8,128)(2,1)} %bitcast.119, bf16[480,6,128]{0,2,1:T(8,128)(2,1)S(1)} %bitcast.117), kind=kOutput, calls=%fused_computation.26 | convolution fusion | flops 358041600 | bytes 1704984 | tf_op jit(solution)/shard_map/qhd,khd->hqk/dot_general | solution.py:91
  94.6 17.4 %all-to-all-start.1 = ((f32[96,1,6]{2,1,0:T(1,128)}), f32[96,1,6]{2,1,0:T(1,128)S(1)}, u32[]{:S(2)}, u32[]{:S(2)}) async-start(f32[96,1,6]{2,1,0:T(1,128)} %broadcast_in_dim.71), calls=%async_computation.1 | async-start | bytes 98304 | tf_op jit(solution)/shard_map/all_to_all | solution.py:43
  112.1 2.0 %constant_dynamic-update-slice_fusion.1 = bf16[1440,768]{1,0:T(8,128)(2,1)} fusion(bf16[1440,768]{1,0:T(8,128)(2,1)} %get-tuple-element.57, bf16[480,768]{1,0:T(8,128)(2,1)} %collective-permute-done.3), kind=kLoop, calls=%fused_computation.74 | loop fusion | bytes 1474560 | tf_op jit(solution)/shard_map/dynamic_update_slice | solution.py:112
  115.3 31.2 %while.11 = (s32[]{:T(128)}, bf16[3,480,256]{2,1,0:T(8,128)(2,1)}, s32[3]{0:T(128)S(1)}, bf16[1440,768]{1,0:T(8,128)(2,1)S(1)}, bf16[480,768]{1,0:T(8,128)(2,1)}...) while((s32[]{:T(128)}, bf16[3,480,256]{2,1,0:T(8,128)(2,1)}, ...), condition=%wide.region_6.7_spmd.clone, body=%wide.region_3.6_spmd.clone.sunk | while | flops 726003840 | bytes 25780080 | solution.py:149
  118.8 2.5 %fusion.101 = (f32[2,480]{1,0:T(2,128)S(1)}, f32[2,480,1440]{2,1,0:T(8,128)S(1)}) fusion(pred[480,1440]{1,0:T(8,128)(4,1)S(1)} %and_and_fusion.5, bf16[180,2,8,128]{3,2,1,0:T(8,128)(2,1)S(1)} %get-tuple-element.212, bf16[480,768]{1,0:T(8,128)(2,1)} %get-tuple-element.250, s32[]{:T(128)S(6)} %select_n.90), kind=kOutput, calls=%fused_computation.3.clone.1 | convolution fusion | flops 358040640 | bytes 7207684 | tf_op jit(solution)/shard_map/while/body/eval_jaxpr/qhd,khd->hqk/dot_general | solution.py:131
  121.3 1.8 %fusion.102 = f32[2,480]{1,0:T(2,128)S(1)} fusion(f32[2,480,1440]{2,1,0:T(8,128)S(1)} %get-tuple-element.213, f32[2,480]{1,0:T(2,128)S(1)} %get-tuple-element.214, pred[480,1440]{1,0:T(8,128)(4,1)S(1)} %and_and_fusion.5), kind=kLoop, calls=%fused_computation.4.clone.1 | loop fusion | flops 5528640 | bytes 6228480 | tf_op jit(solution)/shard_map/while/body/eval_jaxpr/reduce_sum | solution.py:140
  123.1 1.5 fusion.103
  127.0 1.4 dynamic-slice_bitcast_fusion.8
  129.2 2.5 %fusion.101 = (f32[2,480]{1,0:T(2,128)S(1)}, f32[2,480,1440]{2,1,0:T(8,128)S(1)}) fusion(pred[480,1440]{1,0:T(8,128)(4,1)S(1)} %and_and_fusion.5, bf16[180,2,8,128]{3,2,1,0:T(8,128)(2,1)S(1)} %get-tuple-element.212, bf16[480,768]{1,0:T(8,128)(2,1)} %get-tuple-element.250, s32[]{:T(128)S(6)} %select_n.90), kind=kOutput, calls=%fused_computation.3.clone.1 | convolution fusion | flops 358040640 | bytes 7207684 | tf_op jit(solution)/shard_map/while/body/eval_jaxpr/qhd,khd->hqk/dot_general | solution.py:131
  131.7 1.8 %fusion.102 = f32[2,480]{1,0:T(2,128)S(1)} fusion(f32[2,480,1440]{2,1,0:T(8,128)S(1)} %get-tuple-element.213, f32[2,480]{1,0:T(2,128)S(1)} %get-tuple-element.214, pred[480,1440]{1,0:T(8,128)(4,1)S(1)} %and_and_fusion.5), kind=kLoop, calls=%fused_computation.4.clone.1 | loop fusion | flops 5528640 | bytes 6228480 | tf_op jit(solution)/shard_map/while/body/eval_jaxpr/reduce_sum | solution.py:140
  133.5 1.5 fusion.103
  137.4 1.4 dynamic-slice_bitcast_fusion.8
  139.6 2.5 %fusion.101 = (f32[2,480]{1,0:T(2,128)S(1)}, f32[2,480,1440]{2,1,0:T(8,128)S(1)}) fusion(pred[480,1440]{1,0:T(8,128)(4,1)S(1)} %and_and_fusion.5, bf16[180,2,8,128]{3,2,1,0:T(8,128)(2,1)S(1)} %get-tuple-element.212, bf16[480,768]{1,0:T(8,128)(2,1)} %get-tuple-element.250, s32[]{:T(128)S(6)} %select_n.90), kind=kOutput, calls=%fused_computation.3.clone.1 | convolution fusion | flops 358040640 | bytes 7207684 | tf_op jit(solution)/shard_map/while/body/eval_jaxpr/qhd,khd->hqk/dot_general | solution.py:131
  142.1 1.8 %fusion.102 = f32[2,480]{1,0:T(2,128)S(1)} fusion(f32[2,480,1440]{2,1,0:T(8,128)S(1)} %get-tuple-element.213, f32[2,480]{1,0:T(2,128)S(1)} %get-tuple-element.214, pred[480,1440]{1,0:T(8,128)(4,1)S(1)} %and_and_fusion.5), kind=kLoop, calls=%fused_computation.4.clone.1 | loop fusion | flops 5528640 | bytes 6228480 | tf_op jit(solution)/shard_map/while/body/eval_jaxpr/reduce_sum | solution.py:140
  143.9 1.5 fusion.103
  147.2 6.4 %all-to-all-start.2 = ((f32[8,1,6]{2,1,0:T(1,128)}), f32[8,1,6]{2,1,0:T(1,128)S(1)}, u32[]{:S(2)}, u32[]{:S(2)}) async-start(f32[8,1,6]{2,1,0:T(1,128)} %broadcast_in_dim.72), calls=%async_computation.2 | async-start | bytes 8192 | tf_op jit(solution)/shard_map/all_to_all | solution.py:43
  156.1 2.0 %all-to-all-done.2 = f32[8,1,6]{2,1,0:T(1,128)S(1)} async-done(((f32[8,1,6]{2,1,0:T(1,128)}), f32[8,1,6]{2,1,0:T(1,128)S(1)}, u32[]{:S(2)}, u32[]{:S(2)}) %all-to-all-start.2) | async-done | bytes 224 | tf_op jit(solution)/shard_map/all_to_all | solution.py:43
  158.4 2.0 %multiply_convert_fusion = bf16[2,128,896]{2,1,0:T(8,128)(2,1)} fusion(bf16[2,128,896]{2,1,0:T(8,128)(2,1)} %fusion.32, bf16[2,128,896]{2,1,0:T(8,128)(2,1)S(1)} %copy-done.3, f32[2]{0:T(128)S(1)} %compare_select_fusion.1), kind=kLoop, calls=%fused_computation.53 | loop fusion | flops 1605632 | bytes 1376264 | tf_op jit(solution)/shard_map/convert_element_type | solution.py:162
  (87 shorter events, 26.4 us)
Async XLA Ops:
  3.9 15.0 %copy-start = (bf16[480,768]{1,0:T(8,128)(2,1)S(1)}, bf16[480,768]{1,0:T(8,128)(2,1)}, u32[]{:S(2)}) copy-start(bf16[480,768]{1,0:T(8,128)(2,1)} %param.9) | copy-start | bytes 2211844
  3.9 19.4 %copy-start.4 = (s32[480]{0:T(512)S(1)}, s32[480]{0:T(512)}, u32[]{:S(2)}) copy-start(s32[480]{0:T(512)} %param.11) | copy-start | bytes 5764
  3.9 63.2 %all-to-all-start = ((bf16[8,2,16,7168]{3,2,1,0:T(8,128)(2,1)}), bf16[8,2,16,7168]{3,2,1,0:T(8,128)(2,1)}, u32[]{:S(2)}, u32[]{:S(2)}) async-start(bf16[8,2,16,7168]{3,2,1,0:T(8,128)(2,1)} %broadcast_in_dim.67), calls=%async_computation | async-start | bytes 7340032 | tf_op jit(solution)/shard_map/all_to_all | solution.py:43
  18.9 33.2 %collective-permute-start = (bf16[480,768]{1,0:T(8,128)(2,1)S(1)}, bf16[480,768]{1,0:T(8,128)(2,1)}, u32[]{:S(2)}, u32[]{:S(2)}) collective-permute-start(bf16[480,768]{1,0:T(8,128)(2,1)S(1)} %copy-done), channel_id=1, source_target_pairs={{0,8},{8,16},{16,24},{24,32},{32,40},{40,48},{48,56},{56,64},{64,7... | collective-permute-start | bytes 2211848 | tf_op jit(solution)/shard_map/ppermute | solution.py:28
  21.1 31.0 %collective-permute-start.1 = (bf16[480,768]{1,0:T(8,128)(2,1)}, bf16[480,768]{1,0:T(8,128)(2,1)}, u32[]{:S(2)}, u32[]{:S(2)}) collective-permute-start(bf16[480,768]{1,0:T(8,128)(2,1)} %param.10), channel_id=1, source_target_pairs={{0,8},{8,16},{16,24},{24,32},{32,40},{40,48},{48,56},{56,64},{64,7... | collective-permute-start | bytes 2211848 | tf_op jit(solution)/shard_map/ppermute | solution.py:28
  23.3 28.8 %collective-permute-start.2 = (s32[480]{0:T(512)S(1)}, s32[480]{0:T(512)S(1)}, u32[]{:S(2)}, u32[]{:S(2)}) collective-permute-start(s32[480]{0:T(512)S(1)} %copy-done.4), channel_id=1, source_target_pairs={{0,8},{8,16},{16,24},{24,32},{32,40},{40,48},{48,56},{56,64},{64,7... | collective-permute-start | bytes 5768 | tf_op jit(solution)/shard_map/ppermute | solution.py:28
  26.5 36.1 %copy-start.1 = (bf16[480,768]{0,1:T(8,128)(2,1)}, bf16[480,768]{0,1:T(8,128)(2,1)S(1)}, u32[]{:S(2)}) copy-start(bf16[480,768]{0,1:T(8,128)(2,1)S(1)} %copy.116) | copy-start | bytes 2211844
  53.5 29.1 %collective-permute-start.3 = (bf16[480,768]{1,0:T(8,128)(2,1)}, bf16[480,768]{1,0:T(8,128)(2,1)}, u32[]{:S(2)}, u32[]{:S(2)}) collective-permute-start(bf16[480,768]{1,0:T(8,128)(2,1)} %collective-permute-done), channel_id=1, source_target_pairs={{0,8},{8,16},{16,24},{24,32},{32,40},{40,48},{48,56},{56,64},{64,7... | collective-permute-start | bytes 2211848 | tf_op jit(solution)/shard_map/ppermute | solution.py:28
  58.5 24.1 %collective-permute-start.5 = (s32[480]{0:T(512)S(1)}, s32[480]{0:T(512)S(1)}, u32[]{:S(2)}, u32[]{:S(2)}) collective-permute-start(s32[480]{0:T(512)S(1)} %collective-permute-done.2), channel_id=1, source_target_pairs={{0,8},{8,16},{16,24},{24,32},{32,40},{40,48},{48,56},{56,64},{64,7... | collective-permute-start | bytes 5768 | tf_op jit(solution)/shard_map/ppermute | solution.py:28
  59.8 29.1 %collective-permute-start.4 = (bf16[480,768]{1,0:T(8,128)(2,1)}, bf16[480,768]{1,0:T(8,128)(2,1)}, u32[]{:S(2)}, u32[]{:S(2)}) collective-permute-start(bf16[480,768]{1,0:T(8,128)(2,1)} %collective-permute-done.1), channel_id=1, source_target_pairs={{0,8},{8,16},{16,24},{24,32},{32,40},{40,48},{48,56},{56,64},{64,7... | collective-permute-start | bytes 2211848 | tf_op jit(solution)/shard_map/ppermute | solution.py:28
  77.3 14.2 %copy-start.2 = (bf16[480,768]{0,1:T(8,128)(2,1)S(1)}, bf16[480,768]{0,1:T(8,128)(2,1)}, u32[]{:S(2)}) copy-start(bf16[480,768]{0,1:T(8,128)(2,1)} %copy-done.1) | copy-start | bytes 2211844
  94.6 51.9 %all-to-all-start.1 = ((f32[96,1,6]{2,1,0:T(1,128)}), f32[96,1,6]{2,1,0:T(1,128)S(1)}, u32[]{:S(2)}, u32[]{:S(2)}) async-start(f32[96,1,6]{2,1,0:T(1,128)} %broadcast_in_dim.71), calls=%async_computation.1 | async-start | bytes 98304 | tf_op jit(solution)/shard_map/all_to_all | solution.py:43
  115.3 43.1 %copy-start.3 = (bf16[2,128,896]{2,1,0:T(8,128)(2,1)S(1)}, bf16[2,128,896]{2,1,0:T(8,128)(2,1)}, u32[]{:S(2)}) copy-start(bf16[2,128,896]{2,1,0:T(8,128)(2,1)} %param.13) | copy-start | bytes 1376260
  147.2 10.9 %all-to-all-start.2 = ((f32[8,1,6]{2,1,0:T(1,128)}), f32[8,1,6]{2,1,0:T(1,128)S(1)}, u32[]{:S(2)}, u32[]{:S(2)}) async-start(f32[8,1,6]{2,1,0:T(1,128)} %broadcast_in_dim.72), calls=%async_computation.2 | async-start | bytes 8192 | tf_op jit(solution)/shard_map/all_to_all | solution.py:43

commit v11 on v8

--- a/solution.py
+++ b/solution.py
@@ -146,13 +146,16 @@
     attention_out = jnp.transpose(mixed_groups, (1, 0, 2)).reshape(tokens_here, heads_here * HD)
     heads_all = heads_here * head_count
     head_slots = jnp.arange(heads_all, dtype=jnp.int32)
-    seq_max = jnp.max(gathered(head_max, "seq"), axis=0)
-    max_logit = gathered(seq_max, "head").reshape(heads_all)
-    root_gamma = jnp.sqrt(clip_tau / jnp.maximum(max_logit, clip_tau))
+    block_logit = gathered(head_max, "head").reshape(heads_all)
+    seq_count = lax.axis_size("seq")
+    wanted = (
+        jnp.arange(seq_count, dtype=jnp.int32)[:, None] * mats_here
+        + jnp.arange(mats_here, dtype=jnp.int32)[None, :]
+    ) % heads_all
+    max_logit = jnp.max(lax.all_to_all(block_logit[wanted], "seq", 0, 0, tiled=True), axis=0)
+    picked = jnp.sqrt(clip_tau / jnp.maximum(max_logit, clip_tau))
 
     matrix_index = seq_index * mats_here + jnp.arange(mats_here, dtype=jnp.int32)
-    one_hot = (matrix_index[:, None] % heads_all == head_slots[None, :]).astype(jnp.float32)
-    picked = jnp.sum(one_hot * root_gamma[None, :], axis=1)
     factor = jnp.where(matrix_index < 2 * heads_all, picked, 1.0)
     kept = (1.0 - learn_rate * decay_rate) * weights.astype(jnp.float32)
     new_weights = (factor[:, None, None] * (kept - learn_rate * update.astype(jnp.float32))).astype(

time: 158 us -> 159 us (level)
  local copies, waits for them, and re-layouts: 21.1 us -> 23.4 us
    all_to_all x3 -> x2, starting transfers between devices: 39 us -> 20.9 us  [gathered(): return lax.all_to_all(spread, axis, 0, 0, tiled=True)]
    all_to_all x0 -> x1, starting transfers between devices: none -> 17.6 us  [shards(): lax.all_to_all(block_logit[wanted], 'seq', 0, 0, tiled=True)]
    broadcast_in_dim x3 -> x2, local copies, waits for them, and re-layouts: 4.53 us -> 3.88 us  [gathered(): spread = jnp.broadcast_to(values[None], (size,) + values.shape)]
where the time goes in v11:
time: 159 us; the launch traced here: 158 us
  starting transfers between devices  52.3 us (33%)
  matrix products  33.7 us (21%)
  waiting for transfers between devices  30.3 us (19%)
  local copies, waits for them, and re-layouts  23.4 us (15%)
  other arithmetic  15.6 us (10%)
  loops' own time  2.04 us (1%)
    ppermute x6, waiting for transfers between devices, shifted(): return lax.ppermute(shard, axis, pairs)  29.2 us
    all_to_all x2, starting transfers between devices, gathered(): return lax.all_to_all(spread, axis, 0, 0, tiled=True)  20.9 us
    all_to_all x1, starting transfers between devices, shards(): lax.all_to_all(block_logit[wanted], 'seq', 0, 0, tiled=True)  17.6 us
    ppermute x6, starting transfers between devices, shifted(): return lax.ppermute(shard, axis, pairs)  13.7 us
    dot_general x3, matrix products, head_group(): jnp.einsum('qhd,khd->hqk', query_cols.reshape(tokens_here, group, HD), ke...  7.46 us
    dot_general x1, matrix products, shards(): jnp.einsum('jmrd,kmsd->mjrks', pieces, pieces, preferred_element_type=jnp...  7.05 us
    reduce_sum x3, other arithmetic, head_group(): row_total = jnp.sum(exp_scores, axis=2)  5.47 us
    dot_general x3, matrix products, block_max(): jnp.einsum('qhd,khd->hqk', query_vectors.reshape(tokens_here, heads_here,...  5 us
  transfers between devices with their start and end apart: 9, of which 3 were waited for; matrix products, arithmetic and copies ran while one was open for 39% of the time, Pallas kernels for 0%

profile of v11, /device:TPU:1, one launch (start us, length us, event | category | flops | bytes accessed | tf_op | source)
XLA Modules:
  0.0 158.4 jit_solution(2228409506964922228)
XLA Ops:
  0.6 3.3 %broadcast_in_dim.65 = bf16[8,2,16,7168]{3,2,1,0:T(8,128)(2,1)} broadcast(bf16[2,16,7168]{2,1,0:T(8,128)(2,1)} %param.12), dimensions={1,2,3} | broadcast | bytes 4128768 | tf_op jit(solution)/shard_map/broadcast_in_dim | solution.py:42
  3.9 15.0 %all-to-all-start = ((bf16[8,2,16,7168]{3,2,1,0:T(8,128)(2,1)}), bf16[8,2,16,7168]{3,2,1,0:T(8,128)(2,1)}, u32[]{:S(2)}, u32[]{:S(2)}) async-start(bf16[8,2,16,7168]{3,2,1,0:T(8,128)(2,1)} %broadcast_in_dim.65), calls=%async_computation | async-start | bytes 7340032 | tf_op jit(solution)/shard_map/all_to_all | solution.py:43
  20.3 2.2 %collective-permute-start.1 = (bf16[480,768]{1,0:T(8,128)(2,1)}, bf16[480,768]{1,0:T(8,128)(2,1)}, u32[]{:S(2)}, u32[]{:S(2)}) collective-permute-start(bf16[480,768]{1,0:T(8,128)(2,1)} %param.10), channel_id=1, source_target_pairs={{0,8},{8,16},{16,24},{24,32},{32,40},{40,48},{48,56},{56,64},{64,7... | collective-permute-start | bytes 2211848 | tf_op jit(solution)/shard_map/ppermute | solution.py:28
  25.3 1.4 copy.43
  28.3 23.8 %collective-permute-done.2 = s32[480]{0:T(512)S(1)} collective-permute-done((s32[480]{0:T(512)S(1)}, s32[480]{0:T(512)S(1)}, u32[]{:S(2)}, u32[]{:S(2)}) %collective-permute-start.2) | collective-permute-done | bytes 1952 | tf_op jit(solution)/shard_map/ppermute | solution.py:28
  53.3 4.2 %collective-permute-start.3 = (bf16[480,768]{1,0:T(8,128)(2,1)S(1)}, bf16[480,768]{1,0:T(8,128)(2,1)S(1)}, u32[]{:S(2)}, u32[]{:S(2)}) collective-permute-start(bf16[480,768]{1,0:T(8,128)(2,1)S(1)} %collective-permute-done), channel_id=1, source_target_pairs={{0,8},{8,16},{16,24},{24,32},{32,40},{40,48},{48,56},{56,64},{64,7... | collective-permute-start | bytes 2211848 | tf_op jit(solution)/shard_map/ppermute | solution.py:28
  57.5 1.9 %collective-permute-start.5 = (s32[480]{0:T(512)S(1)}, s32[480]{0:T(512)S(1)}, u32[]{:S(2)}, u32[]{:S(2)}) collective-permute-start(s32[480]{0:T(512)S(1)} %collective-permute-done.2), channel_id=1, source_target_pairs={{0,8},{8,16},{16,24},{24,32},{32,40},{40,48},{48,56},{56,64},{64,7... | collective-permute-start | bytes 5768 | tf_op jit(solution)/shard_map/ppermute | solution.py:28
  59.4 2.8 %collective-permute-start.4 = (bf16[480,768]{1,0:T(8,128)(2,1)}, bf16[480,768]{1,0:T(8,128)(2,1)}, u32[]{:S(2)}, u32[]{:S(2)}) collective-permute-start(bf16[480,768]{1,0:T(8,128)(2,1)} %collective-permute-done.1), channel_id=1, source_target_pairs={{0,8},{8,16},{16,24},{24,32},{32,40},{40,48},{48,56},{56,64},{64,7... | collective-permute-start | bytes 2211848 | tf_op jit(solution)/shard_map/ppermute | solution.py:28
  62.5 2.4 %fusion.27 = f32[6]{0:T(128)S(1)} fusion(pred[480,480]{1,0:T(8,128)(4,1)S(1)} %and_and_fusion.2, bf16[480,6,128]{0,2,1:T(8,128)(2,1)} %bitcast.121, bf16[480,6,128]{0,2,1:T(8,128)(2,1)S(1)} %bitcast.119), kind=kOutput, calls=%fused_computation.29 | convolution fusion | flops 358041600 | bytes 1704984 | tf_op jit(solution)/shard_map/qhd,khd->hqk/dot_general | solution.py:91
  65.0 7.0 %select_reduce_fusion.1 = (f32[2]{0:T(128)S(1)}, f32[2,8,16,8,16]{4,2,3,1,0:T(8,128)S(1)}) fusion(pred[8,16,8,16]{3,1,2,0:T(8,128)(4,1)} %broadcast_compare_fusion, bf16[8,2,16,7168]{3,2,1,0:T(8,128)(2,1)} %all-to-all-done), kind=kOutput, calls=%fused_computation.49 | convolution fusion | flops 469827584 | bytes 3817480 | tf_op jit(solution)/shard_map/jmrd,kmsd->mjrks/dot_general | solution.py:56
  73.3 1.4 fusion.37
  80.4 2.8 %fusion.32 = bf16[2,128,896]{2,1,0:T(8,128)(2,1)} fusion(f32[2,128,8,16]{1,3,2,0:T(8,128)S(1)} %bitcast.125, f32[2]{0:T(128)S(1)} %get-tuple-element.120, bf16[8,2,16,7168]{3,2,1,0:T(8,128)(2,1)} %all-to-all-done, s32[]{:T(128)S(6)} %select_n.63), kind=kOutput, calls=%fused_computation.38 | convolution fusion | flops 353239040 | bytes 1048588 | tf_op jit(solution)/shard_map/mijr,jmrd->mid/dot_general | solution.py:72
  83.2 5.4 %collective-permute-done.4 = bf16[480,768]{1,0:T(8,128)(2,1)} collective-permute-done((bf16[480,768]{1,0:T(8,128)(2,1)}, bf16[480,768]{1,0:T(8,128)(2,1)}, u32[]{:S(2)}, u32[]{:S(2)}) %collective-permute-start.4) | collective-permute-done | bytes 737312 | tf_op jit(solution)/shard_map/ppermute | solution.py:28
  91.0 5.9 %all-to-all-start.1 = ((f32[8,1,6]{2,1,0:T(1,128)}), f32[8,1,6]{2,1,0:T(1,128)S(1)}, u32[]{:S(2)}, u32[]{:S(2)}) async-start(f32[8,1,6]{2,1,0:T(1,128)} %broadcast_in_dim.69), calls=%async_computation.1 | async-start | bytes 8192 | tf_op jit(solution)/shard_map/all_to_all | solution.py:43
  96.9 3.2 %pad_maximum_fusion = (bf16[1440,768]{1,0:T(8,128)(2,1)S(1)}, bf16[1440,768]{1,0:T(8,128)(2,1)}) fusion(bf16[480,768]{1,0:T(8,128)(2,1)} %param.10, bf16[480,768]{1,0:T(8,128)(2,1)} %collective-permute-done.1, bf16[480,768]{1,0:T(8,128)(2,1)} %collective-permute-done.4, bf16[480,768]{1,0:T(8,128)(2,1)S(1)} %copy-done, bf16[480,768]{1,0:T(8,128)(2,1)} %copy-done.1, ...), kind=kLoop, calls=%fused_computation.34 | loop fusion | flops 13271040 | bytes 8847360 | tf_op jit(solution)/shard_map/concatenate | solution.py:109
  102.7 1.6 gather_fusion
  105.0 17.6 %all-to-all-start.2 = ((f32[96,1,2]{2,1,0:T(1,128)}), f32[96,1,2]{2,1,0:T(1,128)S(1)}, u32[]{:S(2)}, u32[]{:S(2)}) async-start(f32[96,1,2]{2,1,0:T(1,128)} %bitcast.13), calls=%async_computation.2 | async-start | bytes 98304 | tf_op jit(solution)/shard_map/all_to_all | solution.py:155
  122.7 31.1 %while.11 = (s32[]{:T(128)}, bf16[3,480,256]{2,1,0:T(8,128)(2,1)}, s32[3]{0:T(128)S(1)}, bf16[1440,768]{1,0:T(8,128)(2,1)S(1)}, bf16[480,768]{1,0:T(8,128)(2,1)}...) while((s32[]{:T(128)}, bf16[3,480,256]{2,1,0:T(8,128)(2,1)}, ...), condition=%wide.region_6.7_spmd.clone, body=%wide.region_3.6_spmd.clone.sunk | while | flops 726003840 | bytes 25780080 | solution.py:145
  124.0 1.4 dynamic-slice_bitcast_fusion.8
  126.1 2.5 %fusion.103 = (f32[2,480]{1,0:T(2,128)S(1)}, f32[2,480,1440]{2,1,0:T(8,128)S(1)}) fusion(pred[480,1440]{1,0:T(8,128)(4,1)S(1)} %and_and_fusion.5, bf16[180,2,8,128]{3,2,1,0:T(8,128)(2,1)S(1)} %get-tuple-element.197, bf16[480,768]{1,0:T(8,128)(2,1)} %get-tuple-element.235, s32[]{:T(128)S(6)} %select_n.106), kind=kOutput, calls=%fused_computation.4.clone.1 | convolution fusion | flops 358040640 | bytes 7207684 | tf_op jit(solution)/shard_map/while/body/eval_jaxpr/qhd,khd->hqk/dot_general | solution.py:127
  128.6 1.8 %fusion.104 = f32[2,480]{1,0:T(2,128)S(1)} fusion(f32[2,480,1440]{2,1,0:T(8,128)S(1)} %get-tuple-element.198, f32[2,480]{1,0:T(2,128)S(1)} %get-tuple-element.199, pred[480,1440]{1,0:T(8,128)(4,1)S(1)} %and_and_fusion.5), kind=kLoop, calls=%fused_computation.5.clone.1 | loop fusion | flops 5528640 | bytes 6228480 | tf_op jit(solution)/shard_map/while/body/eval_jaxpr/reduce_sum | solution.py:136
  130.4 1.5 fusion.105
  134.3 1.4 dynamic-slice_bitcast_fusion.8
  136.5 2.5 %fusion.103 = (f32[2,480]{1,0:T(2,128)S(1)}, f32[2,480,1440]{2,1,0:T(8,128)S(1)}) fusion(pred[480,1440]{1,0:T(8,128)(4,1)S(1)} %and_and_fusion.5, bf16[180,2,8,128]{3,2,1,0:T(8,128)(2,1)S(1)} %get-tuple-element.197, bf16[480,768]{1,0:T(8,128)(2,1)} %get-tuple-element.235, s32[]{:T(128)S(6)} %select_n.106), kind=kOutput, calls=%fused_computation.4.clone.1 | convolution fusion | flops 358040640 | bytes 7207684 | tf_op jit(solution)/shard_map/while/body/eval_jaxpr/qhd,khd->hqk/dot_general | solution.py:127
  138.9 1.8 %fusion.104 = f32[2,480]{1,0:T(2,128)S(1)} fusion(f32[2,480,1440]{2,1,0:T(8,128)S(1)} %get-tuple-element.198, f32[2,480]{1,0:T(2,128)S(1)} %get-tuple-element.199, pred[480,1440]{1,0:T(8,128)(4,1)S(1)} %and_and_fusion.5), kind=kLoop, calls=%fused_computation.5.clone.1 | loop fusion | flops 5528640 | bytes 6228480 | tf_op jit(solution)/shard_map/while/body/eval_jaxpr/reduce_sum | solution.py:136
  140.8 1.5 fusion.105
  144.6 1.4 dynamic-slice_bitcast_fusion.8
  146.8 2.5 %fusion.103 = (f32[2,480]{1,0:T(2,128)S(1)}, f32[2,480,1440]{2,1,0:T(8,128)S(1)}) fusion(pred[480,1440]{1,0:T(8,128)(4,1)S(1)} %and_and_fusion.5, bf16[180,2,8,128]{3,2,1,0:T(8,128)(2,1)S(1)} %get-tuple-element.197, bf16[480,768]{1,0:T(8,128)(2,1)} %get-tuple-element.235, s32[]{:T(128)S(6)} %select_n.106), kind=kOutput, calls=%fused_computation.4.clone.1 | convolution fusion | flops 358040640 | bytes 7207684 | tf_op jit(solution)/shard_map/while/body/eval_jaxpr/qhd,khd->hqk/dot_general | solution.py:127
  149.3 1.8 %fusion.104 = f32[2,480]{1,0:T(2,128)S(1)} fusion(f32[2,480,1440]{2,1,0:T(8,128)S(1)} %get-tuple-element.198, f32[2,480]{1,0:T(2,128)S(1)} %get-tuple-element.199, pred[480,1440]{1,0:T(8,128)(4,1)S(1)} %and_and_fusion.5), kind=kLoop, calls=%fused_computation.5.clone.1 | loop fusion | flops 5528640 | bytes 6228480 | tf_op jit(solution)/shard_map/while/body/eval_jaxpr/reduce_sum | solution.py:136
  151.1 1.5 fusion.105
  153.7 1.4 copy.57
  156.4 2.0 %multiply_convert_fusion = bf16[2,128,896]{2,1,0:T(8,128)(2,1)} fusion(bf16[2,128,896]{2,1,0:T(8,128)(2,1)} %fusion.32, bf16[2,128,896]{2,1,0:T(8,128)(2,1)S(1)} %copy-done.5, f32[2]{0:T(128)S(1)} %compare_select_fusion.1), kind=kLoop, calls=%fused_computation.54 | loop fusion | flops 1605632 | bytes 1376264 | tf_op jit(solution)/shard_map/convert_element_type | solution.py:161
  (92 shorter events, 28.3 us)
Async XLA Ops:
  3.9 15.0 %copy-start = (bf16[480,768]{1,0:T(8,128)(2,1)S(1)}, bf16[480,768]{1,0:T(8,128)(2,1)}, u32[]{:S(2)}) copy-start(bf16[480,768]{1,0:T(8,128)(2,1)} %param.9) | copy-start | bytes 2211844
  3.9 18.6 %copy-start.6 = (s32[480]{0:T(512)S(1)}, s32[480]{0:T(512)}, u32[]{:S(2)}) copy-start(s32[480]{0:T(512)} %param.11) | copy-start | bytes 5764
  3.9 61.0 %all-to-all-start = ((bf16[8,2,16,7168]{3,2,1,0:T(8,128)(2,1)}), bf16[8,2,16,7168]{3,2,1,0:T(8,128)(2,1)}, u32[]{:S(2)}, u32[]{:S(2)}) async-start(bf16[8,2,16,7168]{3,2,1,0:T(8,128)(2,1)} %broadcast_in_dim.65), calls=%async_computation | async-start | bytes 7340032 | tf_op jit(solution)/shard_map/all_to_all | solution.py:43
  18.9 33.1 %collective-permute-start = (bf16[480,768]{1,0:T(8,128)(2,1)S(1)}, bf16[480,768]{1,0:T(8,128)(2,1)S(1)}, u32[]{:S(2)}, u32[]{:S(2)}) collective-permute-start(bf16[480,768]{1,0:T(8,128)(2,1)S(1)} %copy-done), channel_id=1, source_target_pairs={{0,8},{8,16},{16,24},{24,32},{32,40},{40,48},{48,56},{56,64},{64,7... | collective-permute-start | bytes 2211848 | tf_op jit(solution)/shard_map/ppermute | solution.py:28
  20.3 31.8 %collective-permute-start.1 = (bf16[480,768]{1,0:T(8,128)(2,1)}, bf16[480,768]{1,0:T(8,128)(2,1)}, u32[]{:S(2)}, u32[]{:S(2)}) collective-permute-start(bf16[480,768]{1,0:T(8,128)(2,1)} %param.10), channel_id=1, source_target_pairs={{0,8},{8,16},{16,24},{24,32},{32,40},{40,48},{48,56},{56,64},{64,7... | collective-permute-start | bytes 2211848 | tf_op jit(solution)/shard_map/ppermute | solution.py:28
  22.5 29.6 %collective-permute-start.2 = (s32[480]{0:T(512)S(1)}, s32[480]{0:T(512)S(1)}, u32[]{:S(2)}, u32[]{:S(2)}) collective-permute-start(s32[480]{0:T(512)S(1)} %copy-done.6), channel_id=1, source_target_pairs={{0,8},{8,16},{16,24},{24,32},{32,40},{40,48},{48,56},{56,64},{64,7... | collective-permute-start | bytes 5768 | tf_op jit(solution)/shard_map/ppermute | solution.py:28
  26.7 35.9 %copy-start.3 = (bf16[480,768]{0,1:T(8,128)(2,1)}, bf16[480,768]{0,1:T(8,128)(2,1)S(1)}, u32[]{:S(2)}) copy-start(bf16[480,768]{0,1:T(8,128)(2,1)S(1)} %copy.43) | copy-start | bytes 2211844
  52.1 12.9 %copy-start.1 = (bf16[480,768]{1,0:T(8,128)(2,1)}, bf16[480,768]{1,0:T(8,128)(2,1)S(1)}, u32[]{:S(2)}) copy-start(bf16[480,768]{1,0:T(8,128)(2,1)S(1)} %collective-permute-done) | copy-start | bytes 2211844
  53.3 29.8 %collective-permute-start.3 = (bf16[480,768]{1,0:T(8,128)(2,1)S(1)}, bf16[480,768]{1,0:T(8,128)(2,1)S(1)}, u32[]{:S(2)}, u32[]{:S(2)}) collective-permute-start(bf16[480,768]{1,0:T(8,128)(2,1)S(1)} %collective-permute-done), channel_id=1, source_target_pairs={{0,8},{8,16},{16,24},{24,32},{32,40},{40,48},{48,56},{56,64},{64,7... | collective-permute-start | bytes 2211848 | tf_op jit(solution)/shard_map/ppermute | solution.py:28
  57.5 25.6 %collective-permute-start.5 = (s32[480]{0:T(512)S(1)}, s32[480]{0:T(512)S(1)}, u32[]{:S(2)}, u32[]{:S(2)}) collective-permute-start(s32[480]{0:T(512)S(1)} %collective-permute-done.2), channel_id=1, source_target_pairs={{0,8},{8,16},{16,24},{24,32},{32,40},{40,48},{48,56},{56,64},{64,7... | collective-permute-start | bytes 5768 | tf_op jit(solution)/shard_map/ppermute | solution.py:28
  59.4 29.1 %collective-permute-start.4 = (bf16[480,768]{1,0:T(8,128)(2,1)}, bf16[480,768]{1,0:T(8,128)(2,1)}, u32[]{:S(2)}, u32[]{:S(2)}) collective-permute-start(bf16[480,768]{1,0:T(8,128)(2,1)} %collective-permute-done.1), channel_id=1, source_target_pairs={{0,8},{8,16},{16,24},{24,32},{32,40},{40,48},{48,56},{56,64},{64,7... | collective-permute-start | bytes 2211848 | tf_op jit(solution)/shard_map/ppermute | solution.py:28
  77.9 11.2 %copy-start.4 = (bf16[480,768]{0,1:T(8,128)(2,1)S(1)}, bf16[480,768]{0,1:T(8,128)(2,1)}, u32[]{:S(2)}) copy-start(bf16[480,768]{0,1:T(8,128)(2,1)} %copy-done.3) | copy-start | bytes 2211844
  83.2 7.2 %copy-start.2 = (bf16[480,768]{1,0:T(8,128)(2,1)}, bf16[480,768]{1,0:T(8,128)(2,1)S(1)}, u32[]{:S(2)}) copy-start(bf16[480,768]{1,0:T(8,128)(2,1)S(1)} %collective-permute-done.3) | copy-start | bytes 2211844
  91.0 10.4 %all-to-all-start.1 = ((f32[8,1,6]{2,1,0:T(1,128)}), f32[8,1,6]{2,1,0:T(1,128)S(1)}, u32[]{:S(2)}, u32[]{:S(2)}) async-start(f32[8,1,6]{2,1,0:T(1,128)} %broadcast_in_dim.69), calls=%async_computation.1 | async-start | bytes 8192 | tf_op jit(solution)/shard_map/all_to_all | solution.py:43
  105.0 51.2 %all-to-all-start.2 = ((f32[96,1,2]{2,1,0:T(1,128)}), f32[96,1,2]{2,1,0:T(1,128)S(1)}, u32[]{:S(2)}, u32[]{:S(2)}) async-start(f32[96,1,2]{2,1,0:T(1,128)} %bitcast.13), calls=%async_computation.2 | async-start | bytes 98304 | tf_op jit(solution)/shard_map/all_to_all | solution.py:155
  122.6 33.7 %copy-start.5 = (bf16[2,128,896]{2,1,0:T(8,128)(2,1)S(1)}, bf16[2,128,896]{2,1,0:T(8,128)(2,1)}, u32[]{:S(2)}) copy-start(bf16[2,128,896]{2,1,0:T(8,128)(2,1)} %param.13) | copy-start | bytes 1376260
